TPU v7x, 1024 devices: a whole 8x8x8 slice. The times are simulated.
1024 devices in a mesh: curve: 64 (over y, x), coef: 16 (over z, core).
Axes of the slice: x: 8, y: 8, z: 8, core: 2. Of those that a mesh axis runs over, the one named last changes fastest.
Arguments:
- right_side: float32 [64, 1048576], P(None, ('curve', 'coef'))
- group_ids: int32 [1048576], P(('curve', 'coef')), may hold values from 0 to 8191, as said below
- pair_sources: int32 [8192, 16], P(('curve', 'coef')), may hold values from 0 to 8191, as said below
- pair_weights: float32 [8192, 16], P(('curve', 'coef')), may hold values from 0.3 to 1
- self_diag: float32 [1048576], P(('curve', 'coef')), may hold values from 1 to 4
- self_trans: float32 [64, 64], replicated, may hold values from -0.375 to 0.375
- far_trans: float32 [64, 64], replicated, may hold values from -0.015625 to 0.015625
Outputs:
- solution: float32 [64, 1048576], P(None, ('curve', 'coef'))
Inputs may be any that keep to these rules, and one draw needn't show every extreme that they name: `group_ids`: the particles of one device belong to its 8 groups: on device d the ids are non-decreasing and run from 8 * d to 8 * d + 7, first and last reached. `pair_sources`: each listed source group s of target group t has |s - t| <= 8; that distance is reached in every draw.
All inputs are finite; a program needn't handle non-finite values.
Results may differ from a plain program's by a relative error of at most 0.0001.
Values sent between devices are 32-bit elements; how exact they have to be, the bound alone decides.
No kernel may reach another device: no remote copies, remote signals or barrier semaphores. Data moves between devices by JAX's collectives and lax.ppermute only.
A program may use at most 32 MiB of HBM per device.

v0:
```python
import jax
import jax.numpy as jnp
from jax import lax
from jax.sharding import PartitionSpec as P

ITERS = 2


def shifted(array, axis, by):
    peers = lax.axis_size(axis)
    pairs = [(i, i + by) for i in range(peers) if 0 <= i + by < peers]
    return lax.ppermute(array, axis, pairs)


def apply_operator(
    field, slot_table, pair_sources, pair_weights, self_diag, self_trans, far_trans, base_group
):
    highest = lax.Precision.HIGHEST
    group_count = slot_table.shape[0]
    moments = jnp.dot(field, slot_table.T, precision=highest)
    lower = shifted(moments, ("curve", "coef"), 1)
    upper = shifted(moments, ("curve", "coef"), -1)
    extended = jnp.concatenate([lower, moments, upper], axis=1)
    columns = base_group - group_count + jnp.arange(3 * group_count, dtype=jnp.int32)
    matches = (pair_sources[:, :, None] == columns[None, None, :]).astype(jnp.float32)
    select_mat = jnp.sum(pair_weights[:, :, None] * matches, axis=1)
    gathered = jnp.dot(extended, select_mat.T, precision=highest)
    local = jnp.dot(far_trans, gathered, precision=highest)
    spread = jnp.dot(local, slot_table, precision=highest)
    return self_diag[None, :] * field + jnp.dot(self_trans, field, precision=highest) + spread


def least_squares(hessen, beta_norm):
    highest = lax.Precision.HIGHEST
    gram_mat = jnp.dot(hessen.T, hessen, precision=highest)
    factor = jnp.linalg.cholesky(gram_mat)
    target = beta_norm * hessen[0]
    forward = []
    for row in range(ITERS):
        value = target[row]
        for col in range(row):
            value = value - factor[row, col] * forward[col]
        forward.append(value / factor[row, row])
    backward = [None] * ITERS
    for row in range(ITERS - 1, -1, -1):
        value = forward[row]
        for col in range(row + 1, ITERS):
            value = value - factor[col, row] * backward[col]
        backward[row] = value / factor[row, row]
    return backward


def on_device(right_side, group_ids, pair_sources, pair_weights, self_diag, self_trans, far_trans):
    group_count = pair_sources.shape[0]
    base_group = lax.axis_index(("curve", "coef")) * group_count
    slots = group_ids - base_group
    slot_table = (slots[None, :] == jnp.arange(group_count, dtype=jnp.int32)[:, None]).astype(
        jnp.float32
    )
    hessen = jnp.zeros((ITERS + 1, ITERS), jnp.float32)
    squared_rhs = lax.psum(jnp.sum(right_side * right_side), ("curve", "coef"))
    beta_norm = jnp.sqrt(squared_rhs)
    basis = [right_side / beta_norm]
    first_column = 0
    for column in range(first_column, ITERS):
        image = apply_operator(
            basis[column],
            slot_table,
            pair_sources,
            pair_weights,
            self_diag,
            self_trans,
            far_trans,
            base_group,
        )
        partials = jnp.stack(
            [jnp.sum(basis[earlier] * image) for earlier in range(column + 1)]
            + [jnp.sum(image * image)]
        )
        totals = lax.psum(partials, ("curve", "coef"))
        projections = [totals[earlier] for earlier in range(column + 1)]
        lowest = jnp.sqrt(totals[column + 1] - sum((value * value for value in projections)))
        for earlier in range(column + 1):
            hessen = hessen.at[earlier, column].set(projections[earlier])
        hessen = hessen.at[column + 1, column].set(lowest)
        if column < ITERS - 1:
            remainder = image
            earlier = 0
            remainder = remainder - projections[earlier] * basis[earlier]
            basis.append(remainder / lowest)
    coeffs = least_squares(hessen, beta_norm)
    solution = coeffs[0] * basis[0]
    column = 1
    solution = solution + coeffs[column] * basis[column]
    return solution


def solution(mesh):
    placed = (
        P(None, ("curve", "coef")),
        P(("curve", "coef")),
        P(("curve", "coef"), None),
        P(("curve", "coef"), None),
        P(("curve", "coef")),
        P(),
        P(),
    )
    return jax.shard_map(
        on_device, mesh=mesh, in_specs=placed, out_specs=P(None, ("curve", "coef")), check_vma=False
    )
```

profile of v0, /device:TPU:1, one launch (start us, length us, event | category | flops | bytes accessed | tf_op | source)
XLA Modules:
  0.0 410.6 jit_solution(15760245619580423238)
XLA Ops:
  0.0 0.0 copy-start
  0.0 0.0 copy-start.1
  0.0 1.7 multiply_reduce_fusion.5
  1.7 128.6 %psum.21 = f32[]{:T(128)} all-reduce(f32[]{:T(128)} %multiply_reduce_fusion.5), channel_id=1, replica_groups=mesh['curve'=64,'coef'=16] {'curve','coef'}, use_global_device_ids=true, to_apply=%region_1.0 | all-reduce | flops 1 | bytes 8 | tf_op jit(solution)/shard_map/psum | solution.py:61
  130.2 0.0 copy-start.6
  131.0 0.0 copy-done.6
  131.0 0.0 copy-done.1
  131.0 0.0 copy-start.3
  131.0 0.2 fusion.3
  131.2 2.5 collective-permute-start
  133.7 1.9 collective-permute-start.1
  135.7 0.0 copy-done
  135.7 0.0 copy-done.3
  135.7 0.0 copy-start.4
  135.7 0.0 copy-start.5
  135.7 0.4 fusion.1
  136.1 0.3 copy-done.4
  136.4 0.0 copy-done.5
  136.4 0.0 copy-start.2
  136.4 0.1 select_reduce_fusion
  136.5 0.0 collective-permute-done
  136.5 2.1 collective-permute-done.1
  138.7 0.2 fusion.8
  138.9 0.0 copy-done.2
  138.9 0.2 fusion.29
  139.1 1.1 multiply_reduce_fusion.4
  140.2 1.4 pad_maximum_fusion
  141.6 0.7 fusion.27
  142.3 118.9 %psum.22 = f32[2]{0:T(128)S(1)} all-reduce(f32[2]{0:T(128)S(1)} %pad_maximum_fusion), channel_id=1, replica_groups=mesh['curve'=64,'coef'=16] {'curve','coef'}, use_global_device_ids=true, to_apply=%region_5.0 | all-reduce | flops 2 | bytes 16 | tf_op jit(solution)/shard_map/psum | solution.py:80
  261.2 0.6 fusion.28
  263.7 0.7 subtract_divide_fusion
  264.4 0.2 fusion.2
  264.6 2.0 collective-permute-start.2
  266.6 2.4 collective-permute-start.3
  269.0 0.4 fusion
  269.4 0.7 scatter.16
  270.1 0.0 collective-permute-done.2
  270.1 1.5 collective-permute-done.3
  271.5 0.2 fusion.14
  271.8 0.2 fusion.30
  272.0 1.1 multiply_reduce_fusion.2
  273.0 2.0 pad_maximum_fusion.1
  275.0 119.8 %psum.23 = f32[3]{0:T(128)S(1)} all-reduce(f32[3]{0:T(128)S(1)} %pad_maximum_fusion.1), channel_id=1, replica_groups=mesh['curve'=64,'coef'=16] {'curve','coef'}, use_global_device_ids=true, to_apply=%region_9.0 | all-reduce | flops 3 | bytes 24 | tf_op jit(solution)/shard_map/psum | solution.py:80
  394.9 0.6 fusion.26
  398.7 2.0 scatter.20
  400.7 0.7 scatter.21
  401.5 0.1 scatter.24
  401.6 0.2 fusion.31
  401.8 0.1 copy.9
  401.9 0.2 cholesky.18
  402.1 0.6 compare_reduce_fusion
  402.8 0.6 compare_select_fusion.1
  403.4 0.6 fusion.24
  404.0 0.6 fusion.25
  409.8 0.7 multiply_add_fusion
  (7 shorter events, 0.1 us)
Async XLA Ops:
  0.0 135.7 %copy-start = (f32[64,64]{1,0:T(8,128)S(1)}, f32[64,64]{1,0:T(8,128)}, u32[]{:S(2)}) copy-start(f32[64,64]{1,0:T(8,128)} %param.22) | copy-start | bytes 49156
  0.0 131.0 %copy-start.1 = (f32[64,1024]{1,0:T(8,128)S(1)}, f32[64,1024]{1,0:T(8,128)}, u32[]{:S(2)}) copy-start(f32[64,1024]{1,0:T(8,128)} %param.17) | copy-start | bytes 786436
  130.2 0.7 copy-start.6
  131.0 4.7 %copy-start.3 = (f32[1024]{0:T(1024)S(1)}, f32[1024]{0:T(1024)}, u32[]{:S(2)}) copy-start(f32[1024]{0:T(1024)} %param.21) | copy-start | bytes 12292
  131.2 5.3 %collective-permute-start = (f32[64,8]{0,1:T(8,128)S(1)}, f32[64,8]{0,1:T(8,128)S(1)}, u32[]{:S(2)}, u32[]{:S(2)}) collective-permute-start(f32[64,8]{0,1:T(8,128)S(1)} %fusion.3), channel_id=1, source_target_pairs={{0,1},{1,2},{2,3},{3,4},{4,5},{5,6},{6,7},{7,8},{8,9},{9,10},{10,1... | collective-permute-start | bytes 6152 | tf_op jit(solution)/shard_map/ppermute | solution.py:12
  133.7 4.9 %collective-permute-start.1 = (f32[64,8]{0,1:T(8,128)S(1)}, f32[64,8]{0,1:T(8,128)S(1)}, u32[]{:S(2)}, u32[]{:S(2)}) collective-permute-start(f32[64,8]{0,1:T(8,128)S(1)} %fusion.3), channel_id=1, source_target_pairs={{1,0},{2,1},{3,2},{4,3},{5,4},{6,5},{7,6},{8,7},{9,8},{10,9},{11,1... | collective-permute-start | bytes 6152 | tf_op jit(solution)/shard_map/ppermute | solution.py:12
  135.7 0.7 copy-start.4
  135.7 0.7 copy-start.5
  136.4 2.5 copy-start.2
  264.6 5.4 %collective-permute-start.2 = (f32[64,8]{0,1:T(8,128)S(1)}, f32[64,8]{0,1:T(8,128)S(1)}, u32[]{:S(2)}, u32[]{:S(2)}) collective-permute-start(f32[64,8]{0,1:T(8,128)S(1)} %fusion.2), channel_id=1, source_target_pairs={{0,1},{1,2},{2,3},{3,4},{4,5},{5,6},{6,7},{7,8},{8,9},{9,10},{10,1... | collective-permute-start | bytes 6152 | tf_op jit(solution)/shard_map/ppermute | solution.py:12
  266.6 4.9 %collective-permute-start.3 = (f32[64,8]{0,1:T(8,128)S(1)}, f32[64,8]{0,1:T(8,128)S(1)}, u32[]{:S(2)}, u32[]{:S(2)}) collective-permute-start(f32[64,8]{0,1:T(8,128)S(1)} %fusion.2), channel_id=1, source_target_pairs={{1,0},{2,1},{3,2},{4,3},{5,4},{6,5},{7,6},{8,7},{9,8},{10,9},{11,1... | collective-permute-start | bytes 6152 | tf_op jit(solution)/shard_map/ppermute | solution.py:12
where the time goes:
time: 411 us
  blocking collectives  367 us (89%)
  between operations  11.3 us (3%)
  starting transfers between devices  8.81 us (2%)
  other arithmetic  8.13 us (2%)
  local copies, waits for them, and re-layouts  7.14 us (2%)
  matrix products  4.34 us (1%)
    psum x2, blocking collectives, on_device(): totals = lax.psum(partials, ('curve', 'coef'))  239 us
    psum x1, blocking collectives, on_device(): squared_rhs = lax.psum(jnp.sum(right_side * right_side), ('curve', 'coef'))  129 us
    ppermute x4, starting transfers between devices, shifted(): return lax.ppermute(array, axis, pairs)  8.81 us
  transfers between devices with their start and end apart: 4, of which 2 were waited for; matrix products, arithmetic and copies ran while one was open for 0% of the time, Pallas kernels for 0%

commit v1 on v0

v1 whole, which is shorter than its diff:
```python
import jax
import jax.numpy as jnp
from jax import lax
from jax.sharding import PartitionSpec as P

ITERS = 2
DEVICES = ("curve", "coef")
GRAM_PAIRS = ((0, 0), (0, 1), (0, 2), (1, 1), (1, 2), (2, 2))


def shifted(array, axis, by):
    peers = lax.axis_size(axis)
    pairs = [(i, i + by) for i in range(peers) if 0 <= i + by < peers]
    return lax.ppermute(array, axis, pairs)


def apply_operator(field, slot_table, select_mat, self_diag, self_trans, far_trans):
    highest = lax.Precision.HIGHEST
    moments = jnp.dot(field, slot_table.T, precision=highest)
    lower = shifted(moments, DEVICES, 1)
    upper = shifted(moments, DEVICES, -1)
    extended = jnp.concatenate([lower, moments, upper], axis=1)
    gathered = jnp.dot(extended, select_mat.T, precision=highest)
    local = jnp.dot(far_trans, gathered, precision=highest)
    spread = jnp.dot(local, slot_table, precision=highest)
    return self_diag[None, :] * field + jnp.dot(self_trans, field, precision=highest) + spread


def least_squares(hessen, beta_norm):
    (h00, h01), (h10, h11), (h20, h21) = hessen
    g00 = h00 * h00 + h10 * h10 + h20 * h20
    g01 = h00 * h01 + h10 * h11 + h20 * h21
    g11 = h01 * h01 + h11 * h11 + h21 * h21
    l00 = jnp.sqrt(g00)
    l10 = g01 / l00
    l11 = jnp.sqrt(g11 - l10 * l10)
    f0 = beta_norm * h00 / l00
    f1 = (beta_norm * h01 - l10 * f0) / l11
    y1 = f1 / l11
    y0 = (f0 - l10 * y1) / l00
    return y0, y1


def on_device(right_side, group_ids, pair_sources, pair_weights, self_diag, self_trans, far_trans):
    group_count = pair_sources.shape[0]
    base_group = lax.axis_index(DEVICES) * group_count
    slots = group_ids - base_group
    slot_table = (slots[None, :] == jnp.arange(group_count, dtype=jnp.int32)[:, None]).astype(
        jnp.float32
    )
    columns = base_group - group_count + jnp.arange(3 * group_count, dtype=jnp.int32)
    matches = (pair_sources[:, :, None] == columns[None, None, :]).astype(jnp.float32)
    select_mat = jnp.sum(pair_weights[:, :, None] * matches, axis=1)
    operator = lambda field: apply_operator(
        field, slot_table, select_mat, self_diag, self_trans, far_trans
    )
    first = operator(right_side)
    second = operator(first)
    krylov = (right_side, first, second)
    partials = jnp.stack([jnp.sum(krylov[i] * krylov[j]) for i, j in GRAM_PAIRS])
    totals = lax.psum(partials, DEVICES)
    g00, g01, g02, g11, g12, g22 = [totals[k] for k in range(6)]
    beta_norm = jnp.sqrt(g00)
    h00 = g01 / g00
    h10 = jnp.sqrt(g11 / g00 - h00 * h00)
    scale = beta_norm * h10
    h01 = (g02 - h00 * g01) / (beta_norm * scale)
    h11 = (g12 - h00 * g11 - h00 * g02 + h00 * h00 * g01) / (scale * scale)
    ww1 = (g22 - 2.0 * h00 * g12 + h00 * h00 * g11) / (scale * scale)
    h21 = jnp.sqrt(ww1 - h01 * h01 - h11 * h11)
    zero = jnp.zeros((), jnp.float32)
    y0, y1 = least_squares(((h00, h01), (h10, h11), (zero, h21)), beta_norm)
    c1 = y1 / scale
    c0 = y0 / beta_norm - c1 * h00
    return c0 * right_side + c1 * first


def solution(mesh):
    placed = (
        P(None, DEVICES),
        P(DEVICES),
        P(DEVICES, None),
        P(DEVICES, None),
        P(DEVICES),
        P(),
        P(),
    )
    return jax.shard_map(
        on_device, mesh=mesh, in_specs=placed, out_specs=P(None, DEVICES), check_vma=False
    )
```

time: 411 us -> 174 us (0.42)
  blocking collectives: 367 us -> 127 us
  starting transfers between devices: 8.81 us -> 23.9 us
  other arithmetic: 8.13 us -> 0.85 us
    psum x3 -> x1, blocking collectives: 367 us -> 127 us  [on_device(): totals = lax.psum(partials, DEVICES)]
    ppermute x4, starting transfers between devices: 8.81 us -> 23.9 us  [shifted(): return lax.ppermute(array, axis, pairs)]
    another operation x5 -> x0, other arithmetic: 4.23 us -> none  [the longest x2 3.37 us: on_device(): jnp.stack([jnp.sum(basis[earlier] * image) for earlier in range(column +...]
where the time goes in v1:
time: 174 us; the launch traced here: 173 us
  blocking collectives  127 us (73%)
  starting transfers between devices  23.9 us (14%)
  between operations  9.55 us (5%)
  local copies, waits for them, and re-layouts  5.58 us (3%)
  matrix products  4.4 us (3%)
    psum x1, blocking collectives, on_device(): totals = lax.psum(partials, DEVICES)  127 us
    ppermute x4, starting transfers between devices, shifted(): return lax.ppermute(array, axis, pairs)  23.9 us
    another operation x1, local copies, waits for them, and re-layouts, on_device(): jnp.stack([jnp.sum(krylov[i] * krylov[j]) for i, j in GRAM_PAIRS])  3.85 us
  transfers between devices with their start and end apart: 4, of which 2 were waited for; matrix products, arithmetic and copies ran while one was open for 0% of the time, Pallas kernels for 0%

profile of v1, /device:TPU:1, one launch (start us, length us, event | category | flops | bytes accessed | tf_op | source)
XLA Modules:
  0.0 173.1 jit_solution(11643460404677599557)
XLA Ops:
  0.0 0.0 copy-start
  0.0 0.0 copy-start.6
  0.0 0.7 copy-done.6
  0.7 0.0 copy-start.4
  0.7 0.0 copy-start.5
  0.7 0.0 copy-start.2
  0.7 1.2 convolution_bitcast_fusion.1
  1.9 0.0 copy-start.1
  1.9 16.2 %collective-permute-start.1 = (f32[64,8]{0,1:T(8,128)S(1)}, f32[64,8]{0,1:T(8,128)S(1)}, u32[]{:S(2)}, u32[]{:S(2)}) collective-permute-start(f32[64,8]{0,1:T(8,128)S(1)} %convolution_bitcast_fusion.1), channel_id=1, source_target_pairs={{1,0},{2,1},{3,2},{4,3},{5,4},{6,5},{7,6},{8,7},{9,8},{10,9},{11,1... | collective-permute-start | bytes 6152 | tf_op jit(solution)/shard_map/ppermute | solution.py:14
  18.1 1.9 %collective-permute-start = (f32[64,8]{0,1:T(8,128)S(1)}, f32[64,8]{0,1:T(8,128)S(1)}, u32[]{:S(2)}, u32[]{:S(2)}) collective-permute-start(f32[64,8]{0,1:T(8,128)S(1)} %convolution_bitcast_fusion.1), channel_id=1, source_target_pairs={{0,1},{1,2},{2,3},{3,4},{4,5},{5,6},{6,7},{7,8},{8,9},{9,10},{10,1... | collective-permute-start | bytes 6152 | tf_op jit(solution)/shard_map/ppermute | solution.py:14
  20.1 0.0 copy-done.4
  20.1 0.0 copy-done.5
  20.1 0.1 select_reduce_fusion
  20.2 0.0 collective-permute-done.1
  20.2 1.0 collective-permute-done
  21.2 0.2 fusion.8
  21.4 0.0 copy-done.2
  21.5 0.2 fusion.23
  21.6 0.0 copy-start.3
  21.6 0.3 fusion.3
  22.0 0.0 copy-done
  22.0 0.0 copy-done.1
  22.0 0.4 copy-done.3
  22.4 0.4 fusion
  22.7 0.2 fusion.2
  22.9 2.1 %collective-permute-start.3 = (f32[64,8]{0,1:T(8,128)S(1)}, f32[64,8]{0,1:T(8,128)S(1)}, u32[]{:S(2)}, u32[]{:S(2)}) collective-permute-start(f32[64,8]{0,1:T(8,128)S(1)} %fusion.2), channel_id=1, source_target_pairs={{1,0},{2,1},{3,2},{4,3},{5,4},{6,5},{7,6},{8,7},{9,8},{10,9},{11,1... | collective-permute-start | bytes 6152 | tf_op jit(solution)/shard_map/ppermute | solution.py:14
  25.1 3.6 %collective-permute-start.2 = (f32[64,8]{0,1:T(8,128)S(1)}, f32[64,8]{0,1:T(8,128)S(1)}, u32[]{:S(2)}, u32[]{:S(2)}) collective-permute-start(f32[64,8]{0,1:T(8,128)S(1)} %fusion.2), channel_id=1, source_target_pairs={{0,1},{1,2},{2,3},{3,4},{4,5},{5,6},{6,7},{7,8},{8,9},{9,10},{10,1... | collective-permute-start | bytes 6152 | tf_op jit(solution)/shard_map/ppermute | solution.py:14
  28.7 0.4 fusion.1
  29.1 0.0 collective-permute-done.3
  29.1 0.3 collective-permute-done.2
  29.4 0.2 fusion.14
  29.7 0.2 fusion.24
  29.9 1.1 multiply_reduce_fusion
  31.0 3.8 %stack.27 = f32[6]{0:T(128)S(1)} concatenate(f32[1]{0:T(128)} %bitcast, f32[1]{0:T(128)} %bitcast.2, f32[1]{0:T(128)} %bitcast.4, f32[1]{0:T(128)} %bitcast.5, f32[1]{0:T(128)} %bitcast.6, f32[1]{0:T(128)} %bitcast.7), dimensions={0} | concatenate | bytes 48 | tf_op jit(solution)/shard_map/stack | solution.py:60
  34.8 127.5 %psum.7 = f32[6]{0:T(128)S(1)} all-reduce(f32[6]{0:T(128)S(1)} %stack.27), channel_id=1, replica_groups=mesh['curve'=64,'coef'=16] {'curve','coef'}, use_global_device_ids=true, to_apply=%region_7.0 | all-reduce | flops 6 | bytes 48 | tf_op jit(solution)/shard_map/psum | solution.py:61
  162.3 0.7 fusion.22
  172.3 0.7 multiply_add_fusion
  (2 shorter events, 0.0 us)
Async XLA Ops:
  0.0 22.0 %copy-start = (f32[64,64]{1,0:T(8,128)S(1)}, f32[64,64]{1,0:T(8,128)}, u32[]{:S(2)}) copy-start(f32[64,64]{1,0:T(8,128)} %param.12) | copy-start | bytes 49156
  0.0 0.7 copy-start.6
  0.7 19.4 %copy-start.4 = (f32[8,16]{1,0:T(8,128)S(1)}, f32[8,16]{1,0:T(8,128)}, u32[]{:S(2)}) copy-start(f32[8,16]{1,0:T(8,128)} %param.10) | copy-start | bytes 1540
  0.7 19.4 %copy-start.5 = (s32[8,16]{1,0:T(8,128)S(1)}, s32[8,16]{1,0:T(8,128)}, u32[]{:S(2)}) copy-start(s32[8,16]{1,0:T(8,128)} %param.9) | copy-start | bytes 1540
  0.7 20.7 %copy-start.2 = (f32[64,64]{1,0:T(8,128)S(1)}, f32[64,64]{1,0:T(8,128)}, u32[]{:S(2)}) copy-start(f32[64,64]{1,0:T(8,128)} %param.13) | copy-start | bytes 49156
  1.9 20.1 %copy-start.1 = (f32[64,1024]{1,0:T(8,128)S(1)}, f32[64,1024]{1,0:T(8,128)}, u32[]{:S(2)}) copy-start(f32[64,1024]{1,0:T(8,128)} %param.7) | copy-start | bytes 786436
  1.9 18.3 %collective-permute-start.1 = (f32[64,8]{0,1:T(8,128)S(1)}, f32[64,8]{0,1:T(8,128)S(1)}, u32[]{:S(2)}, u32[]{:S(2)}) collective-permute-start(f32[64,8]{0,1:T(8,128)S(1)} %convolution_bitcast_fusion.1), channel_id=1, source_target_pairs={{1,0},{2,1},{3,2},{4,3},{5,4},{6,5},{7,6},{8,7},{9,8},{10,9},{11,1... | collective-permute-start | bytes 6152 | tf_op jit(solution)/shard_map/ppermute | solution.py:14
  18.1 3.1 %collective-permute-start = (f32[64,8]{0,1:T(8,128)S(1)}, f32[64,8]{0,1:T(8,128)S(1)}, u32[]{:S(2)}, u32[]{:S(2)}) collective-permute-start(f32[64,8]{0,1:T(8,128)S(1)} %convolution_bitcast_fusion.1), channel_id=1, source_target_pairs={{0,1},{1,2},{2,3},{3,4},{4,5},{5,6},{6,7},{7,8},{8,9},{9,10},{10,1... | collective-permute-start | bytes 6152 | tf_op jit(solution)/shard_map/ppermute | solution.py:14
  21.6 0.7 copy-start.3
  22.9 6.1 %collective-permute-start.3 = (f32[64,8]{0,1:T(8,128)S(1)}, f32[64,8]{0,1:T(8,128)S(1)}, u32[]{:S(2)}, u32[]{:S(2)}) collective-permute-start(f32[64,8]{0,1:T(8,128)S(1)} %fusion.2), channel_id=1, source_target_pairs={{1,0},{2,1},{3,2},{4,3},{5,4},{6,5},{7,6},{8,7},{9,8},{10,9},{11,1... | collective-permute-start | bytes 6152 | tf_op jit(solution)/shard_map/ppermute | solution.py:14
  25.1 4.4 %collective-permute-start.2 = (f32[64,8]{0,1:T(8,128)S(1)}, f32[64,8]{0,1:T(8,128)S(1)}, u32[]{:S(2)}, u32[]{:S(2)}) collective-permute-start(f32[64,8]{0,1:T(8,128)S(1)} %fusion.2), channel_id=1, source_target_pairs={{0,1},{1,2},{2,3},{3,4},{4,5},{5,6},{6,7},{7,8},{8,9},{9,10},{10,1... | collective-permute-start | bytes 6152 | tf_op jit(solution)/shard_map/ppermute | solution.py:14

commit v2 on v1

--- a/solution.py
+++ b/solution.py
@@ -12,6 +12,15 @@
     peers = lax.axis_size(axis)
     pairs = [(i, i + by) for i in range(peers) if 0 <= i + by < peers]
     return lax.ppermute(array, axis, pairs)
+
+
+def all_sum(value):
+    peers = lax.axis_size(DEVICES)
+    rounds = peers.bit_length() - 1
+    for bit in range(rounds):
+        pairs = [(i, i ^ (1 << bit)) for i in range(peers)]
+        value = value + lax.ppermute(value, DEVICES, pairs)
+    return value
 
 
 def apply_operator(field, slot_table, select_mat, self_diag, self_trans, far_trans):
@@ -57,9 +66,11 @@
     first = operator(right_side)
     second = operator(first)
     krylov = (right_side, first, second)
-    partials = jnp.stack([jnp.sum(krylov[i] * krylov[j]) for i, j in GRAM_PAIRS])
-    totals = lax.psum(partials, DEVICES)
-    g00, g01, g02, g11, g12, g22 = [totals[k] for k in range(6)]
+    columns_sums = jnp.stack([jnp.sum(krylov[i] * krylov[j], axis=0) for i, j in GRAM_PAIRS])
+    partials = jnp.sum(columns_sums, axis=1)
+    totals = all_sum(partials)
+    lanes = lax.optimization_barrier(jnp.broadcast_to(totals[:, None], (len(GRAM_PAIRS), 128)))
+    g00, g01, g02, g11, g12, g22 = [lanes[k] for k in range(len(GRAM_PAIRS))]
     beta_norm = jnp.sqrt(g00)
     h00 = g01 / g00
     h10 = jnp.sqrt(g11 / g00 - h00 * h00)
@@ -68,11 +79,12 @@
     h11 = (g12 - h00 * g11 - h00 * g02 + h00 * h00 * g01) / (scale * scale)
     ww1 = (g22 - 2.0 * h00 * g12 + h00 * h00 * g11) / (scale * scale)
     h21 = jnp.sqrt(ww1 - h01 * h01 - h11 * h11)
-    zero = jnp.zeros((), jnp.float32)
+    zero = jnp.zeros_like(h00)
     y0, y1 = least_squares(((h00, h01), (h10, h11), (zero, h21)), beta_norm)
     c1 = y1 / scale
     c0 = y0 / beta_norm - c1 * h00
-    return c0 * right_side + c1 * first
+    c0, c1 = lax.optimization_barrier((c0, c1))
+    return c0[0] * right_side + c1[0] * first
 
 
 def solution(mesh):

time: 174 us -> 114 us (0.66)
  the two profiles are of different devices: /device:TPU:1 before, /device:TPU:64 now
where the time goes in v2:
time: 114 us
  waiting for transfers between devices  62.9 us (55%)
  starting transfers between devices  44.4 us (39%)
  matrix products  3.76 us (3%)
  local copies, waits for them, and re-layouts  1.18 us (1%)
  other arithmetic  1.15 us (1%)
    ppermute x10, waiting for transfers between devices, all_sum(): value = value + lax.ppermute(value, DEVICES, pairs)  47.1 us
    ppermute x4, starting transfers between devices, shifted(): return lax.ppermute(array, axis, pairs)  25.3 us
    ppermute x10, starting transfers between devices, all_sum(): value = value + lax.ppermute(value, DEVICES, pairs)  19.1 us
    ppermute x4, waiting for transfers between devices, shifted(): return lax.ppermute(array, axis, pairs)  15.8 us
  transfers between devices with their start and end apart: 14, of which 12 were waited for; matrix products, arithmetic and copies ran while one was open for 0% of the time, Pallas kernels for 0%

profile of v2, /device:TPU:64, one launch (start us, length us, event | category | flops | bytes accessed | tf_op | source)
XLA Modules:
  0.0 113.6 jit_solution(14721187756454036134)
XLA Ops:
  0.0 0.0 copy-start
  0.0 0.0 copy-start.6
  0.0 0.7 copy-done.6
  0.7 0.0 copy-start.4
  0.7 0.0 copy-start.5
  0.7 0.0 copy-start.2
  0.7 1.2 %convolution_bitcast_fusion.1 = f32[64,8]{0,1:T(8,128)S(1)} fusion(f32[64,1024]{1,0:T(8,128)} %param.7, s32[1024]{0:T(1024)S(1)} %broadcast_subtract_fusion), kind=kOutput, calls=%fused_computation.5 | convolution fusion | flops 6299648 | bytes 268288 | tf_op jit(solution)/shard_map/dot_general | solution.py:28
  1.9 0.0 copy-start.1
  1.9 19.0 %collective-permute-start.1 = (f32[64,8]{0,1:T(8,128)S(1)}, f32[64,8]{0,1:T(8,128)S(1)}, u32[]{:S(2)}, u32[]{:S(2)}) collective-permute-start(f32[64,8]{0,1:T(8,128)S(1)} %convolution_bitcast_fusion.1), channel_id=1, source_target_pairs={{1,0},{2,1},{3,2},{4,3},{5,4},{6,5},{7,6},{8,7},{9,8},{10,9},{11,1... | collective-permute-start | bytes 6152 | tf_op jit(solution)/shard_map/ppermute | solution.py:14
  20.9 1.9 %collective-permute-start = (f32[64,8]{0,1:T(8,128)S(1)}, f32[64,8]{0,1:T(8,128)S(1)}, u32[]{:S(2)}, u32[]{:S(2)}) collective-permute-start(f32[64,8]{0,1:T(8,128)S(1)} %convolution_bitcast_fusion.1), channel_id=1, source_target_pairs={{0,1},{1,2},{2,3},{3,4},{4,5},{5,6},{6,7},{7,8},{8,9},{9,10},{10,1... | collective-permute-start | bytes 6152 | tf_op jit(solution)/shard_map/ppermute | solution.py:14
  22.9 0.0 copy-done.4
  22.9 0.0 copy-done.5
  22.9 0.1 select_reduce_fusion
  23.0 0.0 collective-permute-done.1
  23.0 8.3 %collective-permute-done = f32[64,8]{0,1:T(8,128)S(1)} collective-permute-done((f32[64,8]{0,1:T(8,128)S(1)}, f32[64,8]{0,1:T(8,128)S(1)}, u32[]{:S(2)}, u32[]{:S(2)}) %collective-permute-start) | collective-permute-done | bytes 2080 | tf_op jit(solution)/shard_map/ppermute | solution.py:14
  31.3 0.2 fusion.8
  31.5 0.0 copy-done.2
  31.5 0.2 fusion.33
  31.7 0.0 copy-start.3
  31.7 0.3 fusion.3
  32.1 0.0 copy-done
  32.1 0.0 copy-done.1
  32.1 0.3 copy-done.3
  32.4 0.4 fusion
  32.8 0.2 fusion.2
  33.0 2.0 %collective-permute-start.3 = (f32[64,8]{0,1:T(8,128)S(1)}, f32[64,8]{0,1:T(8,128)S(1)}, u32[]{:S(2)}, u32[]{:S(2)}) collective-permute-start(f32[64,8]{0,1:T(8,128)S(1)} %fusion.2), channel_id=1, source_target_pairs={{1,0},{2,1},{3,2},{4,3},{5,4},{6,5},{7,6},{8,7},{9,8},{10,9},{11,1... | collective-permute-start | bytes 6152 | tf_op jit(solution)/shard_map/ppermute | solution.py:14
  35.0 2.4 %collective-permute-start.2 = (f32[64,8]{0,1:T(8,128)S(1)}, f32[64,8]{0,1:T(8,128)S(1)}, u32[]{:S(2)}, u32[]{:S(2)}) collective-permute-start(f32[64,8]{0,1:T(8,128)S(1)} %fusion.2), channel_id=1, source_target_pairs={{0,1},{1,2},{2,3},{3,4},{4,5},{5,6},{6,7},{7,8},{8,9},{9,10},{10,1... | collective-permute-start | bytes 6152 | tf_op jit(solution)/shard_map/ppermute | solution.py:14
  37.4 0.4 fusion.1
  37.8 0.0 collective-permute-done.3
  37.8 7.6 %collective-permute-done.2 = f32[64,8]{0,1:T(8,128)S(1)} collective-permute-done((f32[64,8]{0,1:T(8,128)S(1)}, f32[64,8]{0,1:T(8,128)S(1)}, u32[]{:S(2)}, u32[]{:S(2)}) %collective-permute-start.2) | collective-permute-done | bytes 2080 | tf_op jit(solution)/shard_map/ppermute | solution.py:14
  45.3 0.2 fusion.14
  45.6 0.2 fusion.34
  45.8 0.4 multiply_reduce_fusion
  46.2 0.1 stack.27
  46.3 0.1 reduce_sum.79
  46.4 1.9 %collective-permute-start.4 = (f32[6]{0:T(128)S(1)}, f32[6]{0:T(128)S(1)}, u32[]{:S(2)}, u32[]{:S(2)}) collective-permute-start(f32[6]{0:T(128)S(1)} %reduce_sum.79), channel_id=1, source_target_pairs={{0,1},{1,0},{2,3},{3,2},{4,5},{5,4},{6,7},{7,6},{8,9},{9,8},{10,11... | collective-permute-start | bytes 80 | tf_op jit(solution)/shard_map/ppermute | solution.py:22
  48.3 1.1 collective-permute-done.4
  49.4 1.9 %collective-permute-start.5 = (f32[6]{0:T(128)S(1)}, f32[6]{0:T(128)S(1)}, u32[]{:S(2)}, u32[]{:S(2)}) collective-permute-start(f32[6]{0:T(128)S(1)} %add.87), channel_id=1, source_target_pairs={{0,2},{1,3},{2,0},{3,1},{4,6},{5,7},{6,4},{7,5},{8,10},{9,11},{10,... | collective-permute-start | bytes 80 | tf_op jit(solution)/shard_map/ppermute | solution.py:22
  51.3 3.5 %collective-permute-done.5 = f32[6]{0:T(128)S(1)} collective-permute-done((f32[6]{0:T(128)S(1)}, f32[6]{0:T(128)S(1)}, u32[]{:S(2)}, u32[]{:S(2)}) %collective-permute-start.5) | collective-permute-done | bytes 56 | tf_op jit(solution)/shard_map/ppermute | solution.py:22
  54.8 1.9 %collective-permute-start.6 = (f32[6]{0:T(128)S(1)}, f32[6]{0:T(128)S(1)}, u32[]{:S(2)}, u32[]{:S(2)}) collective-permute-start(f32[6]{0:T(128)S(1)} %add.88), channel_id=1, source_target_pairs={{0,4},{1,5},{2,6},{3,7},{4,0},{5,1},{6,2},{7,3},{8,12},{9,13},{10,... | collective-permute-start | bytes 80 | tf_op jit(solution)/shard_map/ppermute | solution.py:22
  56.8 4.4 %collective-permute-done.6 = f32[6]{0:T(128)S(1)} collective-permute-done((f32[6]{0:T(128)S(1)}, f32[6]{0:T(128)S(1)}, u32[]{:S(2)}, u32[]{:S(2)}) %collective-permute-start.6) | collective-permute-done | bytes 56 | tf_op jit(solution)/shard_map/ppermute | solution.py:22
  61.2 1.9 %collective-permute-start.7 = (f32[6]{0:T(128)S(1)}, f32[6]{0:T(128)S(1)}, u32[]{:S(2)}, u32[]{:S(2)}) collective-permute-start(f32[6]{0:T(128)S(1)} %add.89), channel_id=1, source_target_pairs={{0,8},{1,9},{2,10},{3,11},{4,12},{5,13},{6,14},{7,15},{8,0},{9,1},... | collective-permute-start | bytes 80 | tf_op jit(solution)/shard_map/ppermute | solution.py:22
  63.1 7.4 %collective-permute-done.7 = f32[6]{0:T(128)S(1)} collective-permute-done((f32[6]{0:T(128)S(1)}, f32[6]{0:T(128)S(1)}, u32[]{:S(2)}, u32[]{:S(2)}) %collective-permute-start.7) | collective-permute-done | bytes 56 | tf_op jit(solution)/shard_map/ppermute | solution.py:22
  70.5 1.9 %collective-permute-start.8 = (f32[6]{0:T(128)S(1)}, f32[6]{0:T(128)S(1)}, u32[]{:S(2)}, u32[]{:S(2)}) collective-permute-start(f32[6]{0:T(128)S(1)} %add.90), channel_id=1, source_target_pairs={{0,16},{1,17},{2,18},{3,19},{4,20},{5,21},{6,22},{7,23},{8,24},{9,... | collective-permute-start | bytes 80 | tf_op jit(solution)/shard_map/ppermute | solution.py:22
  72.4 3.5 %collective-permute-done.8 = f32[6]{0:T(128)S(1)} collective-permute-done((f32[6]{0:T(128)S(1)}, f32[6]{0:T(128)S(1)}, u32[]{:S(2)}, u32[]{:S(2)}) %collective-permute-start.8) | collective-permute-done | bytes 56 | tf_op jit(solution)/shard_map/ppermute | solution.py:22
  75.9 1.9 %collective-permute-start.9 = (f32[6]{0:T(128)S(1)}, f32[6]{0:T(128)S(1)}, u32[]{:S(2)}, u32[]{:S(2)}) collective-permute-start(f32[6]{0:T(128)S(1)} %add.91), channel_id=1, source_target_pairs={{0,32},{1,33},{2,34},{3,35},{4,36},{5,37},{6,38},{7,39},{8,40},{9,... | collective-permute-start | bytes 80 | tf_op jit(solution)/shard_map/ppermute | solution.py:22
  77.8 4.4 %collective-permute-done.9 = f32[6]{0:T(128)S(1)} collective-permute-done((f32[6]{0:T(128)S(1)}, f32[6]{0:T(128)S(1)}, u32[]{:S(2)}, u32[]{:S(2)}) %collective-permute-start.9) | collective-permute-done | bytes 56 | tf_op jit(solution)/shard_map/ppermute | solution.py:22
  82.2 1.9 %collective-permute-start.10 = (f32[6]{0:T(128)S(1)}, f32[6]{0:T(128)S(1)}, u32[]{:S(2)}, u32[]{:S(2)}) collective-permute-start(f32[6]{0:T(128)S(1)} %add.92), channel_id=1, source_target_pairs={{0,64},{1,65},{2,66},{3,67},{4,68},{5,69},{6,70},{7,71},{8,72},{9,... | collective-permute-start | bytes 80 | tf_op jit(solution)/shard_map/ppermute | solution.py:22
  84.2 7.4 %collective-permute-done.10 = f32[6]{0:T(128)S(1)} collective-permute-done((f32[6]{0:T(128)S(1)}, f32[6]{0:T(128)S(1)}, u32[]{:S(2)}, u32[]{:S(2)}) %collective-permute-start.10) | collective-permute-done | bytes 56 | tf_op jit(solution)/shard_map/ppermute | solution.py:22
  91.6 1.9 %collective-permute-start.11 = (f32[6]{0:T(128)S(1)}, f32[6]{0:T(128)S(1)}, u32[]{:S(2)}, u32[]{:S(2)}) collective-permute-start(f32[6]{0:T(128)S(1)} %add.93), channel_id=1, source_target_pairs={{0,128},{1,129},{2,130},{3,131},{4,132},{5,133},{6,134},{7,135},{8... | collective-permute-start | bytes 80 | tf_op jit(solution)/shard_map/ppermute | solution.py:22
  93.5 3.5 %collective-permute-done.11 = f32[6]{0:T(128)S(1)} collective-permute-done((f32[6]{0:T(128)S(1)}, f32[6]{0:T(128)S(1)}, u32[]{:S(2)}, u32[]{:S(2)}) %collective-permute-start.11) | collective-permute-done | bytes 56 | tf_op jit(solution)/shard_map/ppermute | solution.py:22
  97.0 1.9 %collective-permute-start.12 = (f32[6]{0:T(128)S(1)}, f32[6]{0:T(128)S(1)}, u32[]{:S(2)}, u32[]{:S(2)}) collective-permute-start(f32[6]{0:T(128)S(1)} %add.94), channel_id=1, source_target_pairs={{0,256},{1,257},{2,258},{3,259},{4,260},{5,261},{6,262},{7,263},{8... | collective-permute-start | bytes 80 | tf_op jit(solution)/shard_map/ppermute | solution.py:22
  98.9 4.4 %collective-permute-done.12 = f32[6]{0:T(128)S(1)} collective-permute-done((f32[6]{0:T(128)S(1)}, f32[6]{0:T(128)S(1)}, u32[]{:S(2)}, u32[]{:S(2)}) %collective-permute-start.12) | collective-permute-done | bytes 56 | tf_op jit(solution)/shard_map/ppermute | solution.py:22
  103.3 1.9 %collective-permute-start.13 = (f32[6]{0:T(128)S(1)}, f32[6]{0:T(128)S(1)}, u32[]{:S(2)}, u32[]{:S(2)}) collective-permute-start(f32[6]{0:T(128)S(1)} %add.95), channel_id=1, source_target_pairs={{0,512},{1,513},{2,514},{3,515},{4,516},{5,517},{6,518},{7,519},{8... | collective-permute-start | bytes 80 | tf_op jit(solution)/shard_map/ppermute | solution.py:22
  105.2 7.4 %collective-permute-done.13 = f32[6]{0:T(128)S(1)} collective-permute-done((f32[6]{0:T(128)S(1)}, f32[6]{0:T(128)S(1)}, u32[]{:S(2)}, u32[]{:S(2)}) %collective-permute-start.13) | collective-permute-done | bytes 56 | tf_op jit(solution)/shard_map/ppermute | solution.py:22
  112.7 0.1 broadcast_in_dim.4
  112.9 0.8 multiply_add_fusion
  (16 shorter events, 0.1 us)
Async XLA Ops:
  0.0 32.1 %copy-start = (f32[64,64]{1,0:T(8,128)S(1)}, f32[64,64]{1,0:T(8,128)}, u32[]{:S(2)}) copy-start(f32[64,64]{1,0:T(8,128)} %param.12) | copy-start | bytes 49156
  0.0 0.7 copy-start.6
  0.7 22.2 %copy-start.4 = (f32[8,16]{1,0:T(8,128)S(1)}, f32[8,16]{1,0:T(8,128)}, u32[]{:S(2)}) copy-start(f32[8,16]{1,0:T(8,128)} %param.10) | copy-start | bytes 1540
  0.7 22.2 %copy-start.5 = (s32[8,16]{1,0:T(8,128)S(1)}, s32[8,16]{1,0:T(8,128)}, u32[]{:S(2)}) copy-start(s32[8,16]{1,0:T(8,128)} %param.9) | copy-start | bytes 1540
  0.7 30.8 %copy-start.2 = (f32[64,64]{1,0:T(8,128)S(1)}, f32[64,64]{1,0:T(8,128)}, u32[]{:S(2)}) copy-start(f32[64,64]{1,0:T(8,128)} %param.13) | copy-start | bytes 49156
  1.9 30.2 %copy-start.1 = (f32[64,1024]{1,0:T(8,128)S(1)}, f32[64,1024]{1,0:T(8,128)}, u32[]{:S(2)}) copy-start(f32[64,1024]{1,0:T(8,128)} %param.7) | copy-start | bytes 786436
  1.9 21.1 %collective-permute-start.1 = (f32[64,8]{0,1:T(8,128)S(1)}, f32[64,8]{0,1:T(8,128)S(1)}, u32[]{:S(2)}, u32[]{:S(2)}) collective-permute-start(f32[64,8]{0,1:T(8,128)S(1)} %convolution_bitcast_fusion.1), channel_id=1, source_target_pairs={{1,0},{2,1},{3,2},{4,3},{5,4},{6,5},{7,6},{8,7},{9,8},{10,9},{11,1... | collective-permute-start | bytes 6152 | tf_op jit(solution)/shard_map/ppermute | solution.py:14
  20.9 10.4 %collective-permute-start = (f32[64,8]{0,1:T(8,128)S(1)}, f32[64,8]{0,1:T(8,128)S(1)}, u32[]{:S(2)}, u32[]{:S(2)}) collective-permute-start(f32[64,8]{0,1:T(8,128)S(1)} %convolution_bitcast_fusion.1), channel_id=1, source_target_pairs={{0,1},{1,2},{2,3},{3,4},{4,5},{5,6},{6,7},{7,8},{8,9},{9,10},{10,1... | collective-permute-start | bytes 6152 | tf_op jit(solution)/shard_map/ppermute | solution.py:14
  31.7 0.7 copy-start.3
  33.0 4.8 %collective-permute-start.3 = (f32[64,8]{0,1:T(8,128)S(1)}, f32[64,8]{0,1:T(8,128)S(1)}, u32[]{:S(2)}, u32[]{:S(2)}) collective-permute-start(f32[64,8]{0,1:T(8,128)S(1)} %fusion.2), channel_id=1, source_target_pairs={{1,0},{2,1},{3,2},{4,3},{5,4},{6,5},{7,6},{8,7},{9,8},{10,9},{11,1... | collective-permute-start | bytes 6152 | tf_op jit(solution)/shard_map/ppermute | solution.py:14
  35.0 10.4 %collective-permute-start.2 = (f32[64,8]{0,1:T(8,128)S(1)}, f32[64,8]{0,1:T(8,128)S(1)}, u32[]{:S(2)}, u32[]{:S(2)}) collective-permute-start(f32[64,8]{0,1:T(8,128)S(1)} %fusion.2), channel_id=1, source_target_pairs={{0,1},{1,2},{2,3},{3,4},{4,5},{5,6},{6,7},{7,8},{8,9},{9,10},{10,1... | collective-permute-start | bytes 6152 | tf_op jit(solution)/shard_map/ppermute | solution.py:14
  46.4 3.0 %collective-permute-start.4 = (f32[6]{0:T(128)S(1)}, f32[6]{0:T(128)S(1)}, u32[]{:S(2)}, u32[]{:S(2)}) collective-permute-start(f32[6]{0:T(128)S(1)} %reduce_sum.79), channel_id=1, source_target_pairs={{0,1},{1,0},{2,3},{3,2},{4,5},{5,4},{6,7},{7,6},{8,9},{9,8},{10,11... | collective-permute-start | bytes 80 | tf_op jit(solution)/shard_map/ppermute | solution.py:22
  49.4 5.4 %collective-permute-start.5 = (f32[6]{0:T(128)S(1)}, f32[6]{0:T(128)S(1)}, u32[]{:S(2)}, u32[]{:S(2)}) collective-permute-start(f32[6]{0:T(128)S(1)} %add.87), channel_id=1, source_target_pairs={{0,2},{1,3},{2,0},{3,1},{4,6},{5,7},{6,4},{7,5},{8,10},{9,11},{10,... | collective-permute-start | bytes 80 | tf_op jit(solution)/shard_map/ppermute | solution.py:22
  54.8 6.3 %collective-permute-start.6 = (f32[6]{0:T(128)S(1)}, f32[6]{0:T(128)S(1)}, u32[]{:S(2)}, u32[]{:S(2)}) collective-permute-start(f32[6]{0:T(128)S(1)} %add.88), channel_id=1, source_target_pairs={{0,4},{1,5},{2,6},{3,7},{4,0},{5,1},{6,2},{7,3},{8,12},{9,13},{10,... | collective-permute-start | bytes 80 | tf_op jit(solution)/shard_map/ppermute | solution.py:22
  61.2 9.3 %collective-permute-start.7 = (f32[6]{0:T(128)S(1)}, f32[6]{0:T(128)S(1)}, u32[]{:S(2)}, u32[]{:S(2)}) collective-permute-start(f32[6]{0:T(128)S(1)} %add.89), channel_id=1, source_target_pairs={{0,8},{1,9},{2,10},{3,11},{4,12},{5,13},{6,14},{7,15},{8,0},{9,1},... | collective-permute-start | bytes 80 | tf_op jit(solution)/shard_map/ppermute | solution.py:22
  70.5 5.4 %collective-permute-start.8 = (f32[6]{0:T(128)S(1)}, f32[6]{0:T(128)S(1)}, u32[]{:S(2)}, u32[]{:S(2)}) collective-permute-start(f32[6]{0:T(128)S(1)} %add.90), channel_id=1, source_target_pairs={{0,16},{1,17},{2,18},{3,19},{4,20},{5,21},{6,22},{7,23},{8,24},{9,... | collective-permute-start | bytes 80 | tf_op jit(solution)/shard_map/ppermute | solution.py:22
  75.9 6.3 %collective-permute-start.9 = (f32[6]{0:T(128)S(1)}, f32[6]{0:T(128)S(1)}, u32[]{:S(2)}, u32[]{:S(2)}) collective-permute-start(f32[6]{0:T(128)S(1)} %add.91), channel_id=1, source_target_pairs={{0,32},{1,33},{2,34},{3,35},{4,36},{5,37},{6,38},{7,39},{8,40},{9,... | collective-permute-start | bytes 80 | tf_op jit(solution)/shard_map/ppermute | solution.py:22
  82.2 9.3 %collective-permute-start.10 = (f32[6]{0:T(128)S(1)}, f32[6]{0:T(128)S(1)}, u32[]{:S(2)}, u32[]{:S(2)}) collective-permute-start(f32[6]{0:T(128)S(1)} %add.92), channel_id=1, source_target_pairs={{0,64},{1,65},{2,66},{3,67},{4,68},{5,69},{6,70},{7,71},{8,72},{9,... | collective-permute-start | bytes 80 | tf_op jit(solution)/shard_map/ppermute | solution.py:22
  91.6 5.4 %collective-permute-start.11 = (f32[6]{0:T(128)S(1)}, f32[6]{0:T(128)S(1)}, u32[]{:S(2)}, u32[]{:S(2)}) collective-permute-start(f32[6]{0:T(128)S(1)} %add.93), channel_id=1, source_target_pairs={{0,128},{1,129},{2,130},{3,131},{4,132},{5,133},{6,134},{7,135},{8... | collective-permute-start | bytes 80 | tf_op jit(solution)/shard_map/ppermute | solution.py:22
  97.0 6.3 %collective-permute-start.12 = (f32[6]{0:T(128)S(1)}, f32[6]{0:T(128)S(1)}, u32[]{:S(2)}, u32[]{:S(2)}) collective-permute-start(f32[6]{0:T(128)S(1)} %add.94), channel_id=1, source_target_pairs={{0,256},{1,257},{2,258},{3,259},{4,260},{5,261},{6,262},{7,263},{8... | collective-permute-start | bytes 80 | tf_op jit(solution)/shard_map/ppermute | solution.py:22
  103.3 9.3 %collective-permute-start.13 = (f32[6]{0:T(128)S(1)}, f32[6]{0:T(128)S(1)}, u32[]{:S(2)}, u32[]{:S(2)}) collective-permute-start(f32[6]{0:T(128)S(1)} %add.95), channel_id=1, source_target_pairs={{0,512},{1,513},{2,514},{3,515},{4,516},{5,517},{6,518},{7,519},{8... | collective-permute-start | bytes 80 | tf_op jit(solution)/shard_map/ppermute | solution.py:22

commit v3 on v2

--- a/solution.py
+++ b/solution.py
@@ -15,11 +15,10 @@
 
 
 def all_sum(value):
-    peers = lax.axis_size(DEVICES)
-    rounds = peers.bit_length() - 1
-    for bit in range(rounds):
-        pairs = [(i, i ^ (1 << bit)) for i in range(peers)]
-        value = value + lax.ppermute(value, DEVICES, pairs)
+    for axis in ("coef", "curve"):
+        peers = lax.axis_size(axis)
+        spread = jnp.broadcast_to(value[None, :], (peers,) + value.shape)
+        value = jnp.sum(lax.all_to_all(spread, axis, 0, 0, tiled=True), axis=0)
     return value
 
 

time: 114 us -> 77.5 us (0.68)
  the two profiles are of different devices: /device:TPU:64 before, /device:TPU:1 now
where the time goes in v3:
time: 77.5 us; the launch traced here: 77.1 us
  blocking collectives  45.8 us (59%)
  starting transfers between devices  23.9 us (31%)
  matrix products  3.5 us (5%)
  waiting for transfers between devices  1.32 us (2%)
  other arithmetic  1.24 us (2%)
  local copies, waits for them, and re-layouts  1.21 us (2%)
    all_to_all x2, blocking collectives, all_sum(): value = jnp.sum(lax.all_to_all(spread, axis, 0, 0, tiled=True), axis=0)  45.8 us
    ppermute x4, starting transfers between devices, shifted(): return lax.ppermute(array, axis, pairs)  23.9 us
  transfers between devices with their start and end apart: 4, of which 2 were waited for; matrix products, arithmetic and copies ran while one was open for 1% of the time, Pallas kernels for 0%

profile of v3, /device:TPU:1, one launch (start us, length us, event | category | flops | bytes accessed | tf_op | source)
XLA Modules:
  0.0 77.1 jit_solution(8278941631729451846)
XLA Ops:
  0.0 0.0 copy-start
  0.0 0.0 copy-start.6
  0.0 0.7 copy-done.6
  0.7 0.0 copy-start.4
  0.7 0.0 copy-start.5
  0.7 0.0 copy-start.1
  0.7 1.2 %convolution_bitcast_fusion.1 = f32[64,8]{0,1:T(8,128)S(1)} fusion(f32[64,1024]{1,0:T(8,128)} %param.7, s32[1024]{0:T(1024)S(1)} %broadcast_subtract_fusion), kind=kOutput, calls=%fused_computation.5 | convolution fusion | flops 6299648 | bytes 268288 | tf_op jit(solution)/shard_map/dot_general | solution.py:27
  1.9 0.0 copy-start.2
  1.9 16.2 %collective-permute-start.1 = (f32[64,8]{0,1:T(8,128)S(1)}, f32[64,8]{0,1:T(8,128)S(1)}, u32[]{:S(2)}, u32[]{:S(2)}) collective-permute-start(f32[64,8]{0,1:T(8,128)S(1)} %convolution_bitcast_fusion.1), channel_id=1, source_target_pairs={{1,0},{2,1},{3,2},{4,3},{5,4},{6,5},{7,6},{8,7},{9,8},{10,9},{11,1... | collective-permute-start | bytes 6152 | tf_op jit(solution)/shard_map/ppermute | solution.py:14
  18.2 1.9 %collective-permute-start = (f32[64,8]{0,1:T(8,128)S(1)}, f32[64,8]{0,1:T(8,128)S(1)}, u32[]{:S(2)}, u32[]{:S(2)}) collective-permute-start(f32[64,8]{0,1:T(8,128)S(1)} %convolution_bitcast_fusion.1), channel_id=1, source_target_pairs={{0,1},{1,2},{2,3},{3,4},{4,5},{5,6},{6,7},{7,8},{8,9},{9,10},{10,1... | collective-permute-start | bytes 6152 | tf_op jit(solution)/shard_map/ppermute | solution.py:14
  20.1 0.0 copy-done.4
  20.1 0.0 copy-done.5
  20.1 0.1 select_reduce_fusion
  20.2 0.0 collective-permute-done.1
  20.3 1.0 %collective-permute-done = f32[64,8]{0,1:T(8,128)S(1)} collective-permute-done((f32[64,8]{0,1:T(8,128)S(1)}, f32[64,8]{0,1:T(8,128)S(1)}, u32[]{:S(2)}, u32[]{:S(2)}) %collective-permute-start) | collective-permute-done | bytes 2080 | tf_op jit(solution)/shard_map/ppermute | solution.py:14
  21.2 0.1 fusion.8
  21.4 0.0 copy-done.2
  21.4 0.1 fusion.33
  21.5 0.0 copy-start.3
  21.5 0.3 fusion.3
  21.9 0.0 copy-done
  21.9 0.0 copy-done.1
  21.9 0.3 copy-done.3
  22.2 0.4 fusion
  22.6 0.2 fusion.2
  22.8 2.1 %collective-permute-start.3 = (f32[64,8]{0,1:T(8,128)S(1)}, f32[64,8]{0,1:T(8,128)S(1)}, u32[]{:S(2)}, u32[]{:S(2)}) collective-permute-start(f32[64,8]{0,1:T(8,128)S(1)} %fusion.2), channel_id=1, source_target_pairs={{1,0},{2,1},{3,2},{4,3},{5,4},{6,5},{7,6},{8,7},{9,8},{10,9},{11,1... | collective-permute-start | bytes 6152 | tf_op jit(solution)/shard_map/ppermute | solution.py:14
  24.9 3.6 %collective-permute-start.2 = (f32[64,8]{0,1:T(8,128)S(1)}, f32[64,8]{0,1:T(8,128)S(1)}, u32[]{:S(2)}, u32[]{:S(2)}) collective-permute-start(f32[64,8]{0,1:T(8,128)S(1)} %fusion.2), channel_id=1, source_target_pairs={{0,1},{1,2},{2,3},{3,4},{4,5},{5,6},{6,7},{7,8},{8,9},{9,10},{10,1... | collective-permute-start | bytes 6152 | tf_op jit(solution)/shard_map/ppermute | solution.py:14
  28.6 0.4 fusion.1
  28.9 0.0 collective-permute-done.3
  29.0 0.3 collective-permute-done.2
  29.3 0.1 fusion.14
  29.4 0.1 fusion.34
  29.6 0.4 multiply_reduce_fusion
  30.0 0.1 stack.27
  30.1 0.1 reduce_sum.97
  30.2 16.3 %all_to_all.12 = f32[16,1,6]{2,1,0:T(1,128)S(1)} all-to-all(f32[16,1,6]{2,1,0:T(1,128)S(1)} %broadcast_in_dim.8), channel_id=1, replica_groups=mesh['curve'=64,'coef'=16] {'coef'}, dimensions={0} | all-to-all | bytes 768 | tf_op jit(solution)/shard_map/all_to_all | solution.py:21
  46.5 29.5 %all_to_all.13 = f32[64,1,6]{2,1,0:T(1,128)S(1)} all-to-all(f32[64,1,6]{2,1,0:T(1,128)S(1)} %broadcast_in_dim.9), channel_id=1, replica_groups=mesh['curve'=64,'coef'=16] {'curve'}, dimensions={0} | all-to-all | bytes 3072 | tf_op jit(solution)/shard_map/all_to_all | solution.py:21
  76.1 0.1 reduce_sum.99
  76.2 0.1 broadcast_in_dim.10
  76.4 0.8 %multiply_add_fusion = f32[64,1024]{1,0:T(8,128)} fusion(f32[64,1024]{1,0:T(8,128)S(1)} %fusion, f32[64,1024]{1,0:T(8,128)S(1)} %copy-done.1, f32[]{:T(128)S(1)} %bitcast.118, f32[]{:T(128)S(1)} %bitcast.117), kind=kLoop, calls=%fused_computation.6 | loop fusion | flops 196608 | bytes 786440 | tf_op jit(solution)/shard_map/add | solution.py:86
  (9 shorter events, 0.2 us)
Async XLA Ops:
  0.0 21.9 %copy-start = (f32[64,64]{1,0:T(8,128)S(1)}, f32[64,64]{1,0:T(8,128)}, u32[]{:S(2)}) copy-start(f32[64,64]{1,0:T(8,128)} %param.12) | copy-start | bytes 49156
  0.0 0.7 copy-start.6
  0.7 19.4 %copy-start.4 = (f32[8,16]{1,0:T(8,128)S(1)}, f32[8,16]{1,0:T(8,128)}, u32[]{:S(2)}) copy-start(f32[8,16]{1,0:T(8,128)} %param.10) | copy-start | bytes 1540
  0.7 19.4 %copy-start.5 = (s32[8,16]{1,0:T(8,128)S(1)}, s32[8,16]{1,0:T(8,128)}, u32[]{:S(2)}) copy-start(s32[8,16]{1,0:T(8,128)} %param.9) | copy-start | bytes 1540
  0.7 21.2 %copy-start.1 = (f32[64,1024]{1,0:T(8,128)S(1)}, f32[64,1024]{1,0:T(8,128)}, u32[]{:S(2)}) copy-start(f32[64,1024]{1,0:T(8,128)} %param.7) | copy-start | bytes 786436
  1.9 19.4 %copy-start.2 = (f32[64,64]{1,0:T(8,128)S(1)}, f32[64,64]{1,0:T(8,128)}, u32[]{:S(2)}) copy-start(f32[64,64]{1,0:T(8,128)} %param.13) | copy-start | bytes 49156
  1.9 18.3 %collective-permute-start.1 = (f32[64,8]{0,1:T(8,128)S(1)}, f32[64,8]{0,1:T(8,128)S(1)}, u32[]{:S(2)}, u32[]{:S(2)}) collective-permute-start(f32[64,8]{0,1:T(8,128)S(1)} %convolution_bitcast_fusion.1), channel_id=1, source_target_pairs={{1,0},{2,1},{3,2},{4,3},{5,4},{6,5},{7,6},{8,7},{9,8},{10,9},{11,1... | collective-permute-start | bytes 6152 | tf_op jit(solution)/shard_map/ppermute | solution.py:14
  18.2 3.1 %collective-permute-start = (f32[64,8]{0,1:T(8,128)S(1)}, f32[64,8]{0,1:T(8,128)S(1)}, u32[]{:S(2)}, u32[]{:S(2)}) collective-permute-start(f32[64,8]{0,1:T(8,128)S(1)} %convolution_bitcast_fusion.1), channel_id=1, source_target_pairs={{0,1},{1,2},{2,3},{3,4},{4,5},{5,6},{6,7},{7,8},{8,9},{9,10},{10,1... | collective-permute-start | bytes 6152 | tf_op jit(solution)/shard_map/ppermute | solution.py:14
  21.5 0.7 copy-start.3
  22.8 6.1 %collective-permute-start.3 = (f32[64,8]{0,1:T(8,128)S(1)}, f32[64,8]{0,1:T(8,128)S(1)}, u32[]{:S(2)}, u32[]{:S(2)}) collective-permute-start(f32[64,8]{0,1:T(8,128)S(1)} %fusion.2), channel_id=1, source_target_pairs={{1,0},{2,1},{3,2},{4,3},{5,4},{6,5},{7,6},{8,7},{9,8},{10,9},{11,1... | collective-permute-start | bytes 6152 | tf_op jit(solution)/shard_map/ppermute | solution.py:14
  24.9 4.4 %collective-permute-start.2 = (f32[64,8]{0,1:T(8,128)S(1)}, f32[64,8]{0,1:T(8,128)S(1)}, u32[]{:S(2)}, u32[]{:S(2)}) collective-permute-start(f32[64,8]{0,1:T(8,128)S(1)} %fusion.2), channel_id=1, source_target_pairs={{0,1},{1,2},{2,3},{3,4},{4,5},{5,6},{6,7},{7,8},{8,9},{9,10},{10,1... | collective-permute-start | bytes 6152 | tf_op jit(solution)/shard_map/ppermute | solution.py:14

commit v4 on v3

--- a/solution.py
+++ b/solution.py
@@ -22,16 +22,9 @@
     return value
 
 
-def apply_operator(field, slot_table, select_mat, self_diag, self_trans, far_trans):
+def local_part(field, self_diag, self_trans):
     highest = lax.Precision.HIGHEST
-    moments = jnp.dot(field, slot_table.T, precision=highest)
-    lower = shifted(moments, DEVICES, 1)
-    upper = shifted(moments, DEVICES, -1)
-    extended = jnp.concatenate([lower, moments, upper], axis=1)
-    gathered = jnp.dot(extended, select_mat.T, precision=highest)
-    local = jnp.dot(far_trans, gathered, precision=highest)
-    spread = jnp.dot(local, slot_table, precision=highest)
-    return self_diag[None, :] * field + jnp.dot(self_trans, field, precision=highest) + spread
+    return self_diag[None, :] * field + jnp.dot(self_trans, field, precision=highest)
 
 
 def least_squares(hessen, beta_norm):
@@ -59,11 +52,50 @@
     columns = base_group - group_count + jnp.arange(3 * group_count, dtype=jnp.int32)
     matches = (pair_sources[:, :, None] == columns[None, None, :]).astype(jnp.float32)
     select_mat = jnp.sum(pair_weights[:, :, None] * matches, axis=1)
-    operator = lambda field: apply_operator(
-        field, slot_table, select_mat, self_diag, self_trans, far_trans
+    counts = jnp.sum(slot_table, axis=1)
+    highest = lax.Precision.HIGHEST
+    dot = lambda a, b: jnp.dot(a, b, precision=highest)
+    moments = dot(right_side, slot_table.T)
+    own_part = dot(right_side * self_diag[None, :], slot_table.T) + dot(self_trans, moments)
+    g = group_count
+    filler = jnp.zeros((g, g), jnp.float32)
+    payload = jnp.concatenate(
+        [
+            jnp.concatenate([moments, own_part, jnp.zeros_like(moments)], axis=1),
+            select_mat,
+            jnp.concatenate([counts[:, None], jnp.zeros((g, 3 * g - 1), jnp.float32)], axis=1),
+        ],
+        axis=0,
     )
-    first = operator(right_side)
-    second = operator(first)
+    rows = moments.shape[0]
+    below = shifted(payload, DEVICES, 1)
+    above = shifted(payload, DEVICES, -1)
+    two_below = shifted(moments, DEVICES, 2)
+    two_above = shifted(moments, DEVICES, -2)
+    unpack = lambda block: (
+        block[:rows, :g],
+        block[:rows, g : 2 * g],
+        block[rows : rows + g],
+        block[rows + g :, 0],
+    )
+    moments_below, part_below, select_below, counts_below = unpack(below)
+    moments_above, part_above, select_above, counts_above = unpack(above)
+    wide = jnp.concatenate([two_below, moments_below, moments, moments_above, two_above], axis=1)
+    wide_select = jnp.concatenate(
+        [
+            jnp.concatenate([select_below, filler, filler], axis=1),
+            jnp.concatenate([filler, select_mat, filler], axis=1),
+            jnp.concatenate([filler, filler, select_above], axis=1),
+        ],
+        axis=0,
+    )
+    local_near = dot(far_trans, dot(wide, wide_select.T))
+    near_counts = jnp.concatenate([counts_below, counts, counts_above])
+    near_part = jnp.concatenate([part_below, own_part, part_above], axis=1)
+    near_moments = near_part + near_counts[None, :] * local_near
+    first = local_part(right_side, self_diag, self_trans) + dot(local_near[:, g : 2 * g], slot_table)
+    local_next = dot(far_trans, dot(near_moments, select_mat.T))
+    second = local_part(first, self_diag, self_trans) + dot(local_next, slot_table)
     krylov = (right_side, first, second)
     columns_sums = jnp.stack([jnp.sum(krylov[i] * krylov[j], axis=0) for i, j in GRAM_PAIRS])
     partials = jnp.sum(columns_sums, axis=1)

time: 77.5 us -> 78.2 us (level)
  other arithmetic: 1.24 us -> 2.27 us
  blocking collectives: 45.8 us -> 44.9 us
    all_to_all x2, blocking collectives: 45.8 us -> 44.9 us  [all_sum(): value = jnp.sum(lax.all_to_all(spread, axis, 0, 0, tiled=True), axis=0)]
    dot_general x10 -> x11, matrix products: 3.5 us -> 3.78 us  [the longest x9 3.01 us: on_device(): dot = lambda a, b: jnp.dot(a, b, precision=highest)]
  transfers between devices with their start and end apart: 4 -> 4, of which waited for: 2 -> 1; matrix products, arithmetic and copies ran while one was open for 1% -> 1% of each run, Pallas kernels for 0% -> 0%
where the time goes in v4:
time: 78.2 us; the launch traced here: 77.8 us
  blocking collectives  44.9 us (57%)
  starting transfers between devices  24 us (31%)
  matrix products  3.78 us (5%)
  other arithmetic  2.27 us (3%)
  local copies, waits for them, and re-layouts  1.5 us (2%)
  waiting for transfers between devices  1.13 us (1%)
    all_to_all x2, blocking collectives, all_sum(): value = jnp.sum(lax.all_to_all(spread, axis, 0, 0, tiled=True), axis=0)  44.9 us
    ppermute x4, starting transfers between devices, shifted(): return lax.ppermute(array, axis, pairs)  24 us
    dot_general x9, matrix products, on_device(): dot = lambda a, b: jnp.dot(a, b, precision=highest)  3.01 us
  transfers between devices with their start and end apart: 4, of which 1 were waited for; matrix products, arithmetic and copies ran while one was open for 1% of the time, Pallas kernels for 0%

profile of v4, /device:TPU:1, one launch (start us, length us, event | category | flops | bytes accessed | tf_op | source)
XLA Modules:
  0.0 77.8 jit_solution(14848587036835895198)
XLA Ops:
  0.0 0.0 copy-start
  0.0 0.0 copy-start.1
  0.0 0.7 broadcast_subtract_fusion
  0.7 1.1 %fusion.7 = f32[8,64]{1,0:T(8,128)S(1)} fusion(f32[64,1024]{1,0:T(8,128)} %param.7, s32[1024]{0:T(1024)S(1)} %broadcast_subtract_fusion), kind=kOutput, calls=%fused_computation.22 | convolution fusion | flops 6299648 | bytes 268288 | tf_op jit(solution)/shard_map/dot_general | solution.py:57
  1.9 0.0 copy-start.3
  1.9 1.5 %collective-permute-start.3 = (f32[64,8]{0,1:T(8,128)S(1)}, f32[64,8]{0,1:T(8,128)S(1)}, u32[]{:S(2)}, u32[]{:S(2)}) collective-permute-start(f32[64,8]{0,1:T(8,128)S(1)} %bitcast.122), channel_id=1, source_target_pairs={{2,0},{3,1},{4,2},{5,3},{6,4},{7,5},{8,6},{9,7},{10,8},{11,9},{12,... | collective-permute-start | bytes 6152 | tf_op jit(solution)/shard_map/ppermute | solution.py:14
  3.4 6.4 %collective-permute-start = (f32[64,8]{0,1:T(8,128)S(1)}, f32[64,8]{0,1:T(8,128)S(1)}, u32[]{:S(2)}, u32[]{:S(2)}) collective-permute-start(f32[64,8]{0,1:T(8,128)S(1)} %bitcast.123), channel_id=1, source_target_pairs={{0,2},{1,3},{2,4},{3,5},{4,6},{5,7},{6,8},{7,9},{8,10},{9,11},{10,... | collective-permute-start | bytes 6152 | tf_op jit(solution)/shard_map/ppermute | solution.py:14
  9.7 0.1 convert_reduce_fusion
  9.9 0.0 copy-done.1
  9.9 0.0 copy-done.3
  9.9 0.0 copy-start.4
  9.9 0.0 copy-start.5
  9.9 0.2 fusion.3
  10.1 0.5 copy-done.4
  10.6 0.0 copy-done.5
  10.6 0.1 select_reduce_fusion
  10.7 0.1 copy.16
  10.8 0.0 copy-done
  10.8 0.1 fusion.2
  10.9 0.1 select_maximum_fusion.4
  11.0 14.2 %collective-permute-start.2 = (f32[80,24]{0,1:T(8,128)S(1)}, f32[80,24]{0,1:T(8,128)S(1)}, u32[]{:S(2)}, u32[]{:S(2)}) collective-permute-start(f32[80,24]{0,1:T(8,128)S(1)} %select_maximum_fusion.4), channel_id=1, source_target_pairs={{1,0},{2,1},{3,2},{4,3},{5,4},{6,5},{7,6},{8,7},{9,8},{10,9},{11,1... | collective-permute-start | bytes 23048 | tf_op jit(solution)/shard_map/ppermute | solution.py:14
  25.3 1.9 %collective-permute-start.1 = (f32[80,24]{0,1:T(8,128)S(1)}, f32[80,24]{0,1:T(8,128)S(1)}, u32[]{:S(2)}, u32[]{:S(2)}) collective-permute-start(f32[80,24]{0,1:T(8,128)S(1)} %select_maximum_fusion.4), channel_id=1, source_target_pairs={{0,1},{1,2},{2,3},{3,4},{4,5},{5,6},{6,7},{7,8},{8,9},{9,10},{10,1... | collective-permute-start | bytes 23048 | tf_op jit(solution)/shard_map/ppermute | solution.py:14
  27.2 0.0 collective-permute-done
  27.2 1.1 %collective-permute-done.1 = f32[80,24]{0,1:T(8,128)S(1)} collective-permute-done((f32[80,24]{0,1:T(8,128)S(1)}, f32[80,24]{0,1:T(8,128)S(1)}, u32[]{:S(2)}, u32[]{:S(2)}) %collective-permute-start.1) | collective-permute-done | bytes 7712 | tf_op jit(solution)/shard_map/ppermute | solution.py:14
  28.4 0.0 collective-permute-done.2
  28.4 0.1 slice.71
  28.4 0.1 slice.70
  28.5 0.0 collective-permute-done.3
  28.5 0.0 copy-start.2
  28.5 0.3 fusion.8
  28.8 0.5 copy-done.2
  29.3 0.2 convolution_bitcast_fusion.1
  29.4 0.3 fusion.6
  29.8 0.1 slice_bitcast_fusion
  29.8 0.1 slice_bitcast_fusion.1
  29.9 0.1 pad_maximum_fusion
  30.0 0.2 fusion.20
  30.2 0.2 fusion.49
  30.3 0.4 fusion
  30.8 0.4 fusion.1
  31.1 0.4 multiply_reduce_fusion
  31.6 0.1 stack.27
  31.6 0.1 reduce_sum.107
  31.8 15.4 %all_to_all.12 = f32[16,1,6]{2,1,0:T(1,128)S(1)} all-to-all(f32[16,1,6]{2,1,0:T(1,128)S(1)} %broadcast_in_dim.17), channel_id=1, replica_groups=mesh['curve'=64,'coef'=16] {'coef'}, dimensions={0} | all-to-all | bytes 768 | tf_op jit(solution)/shard_map/all_to_all | solution.py:21
  47.2 29.5 %all_to_all.13 = f32[64,1,6]{2,1,0:T(1,128)S(1)} all-to-all(f32[64,1,6]{2,1,0:T(1,128)S(1)} %broadcast_in_dim.18), channel_id=1, replica_groups=mesh['curve'=64,'coef'=16] {'curve'}, dimensions={0} | all-to-all | bytes 3072 | tf_op jit(solution)/shard_map/all_to_all | solution.py:21
  76.7 0.1 reduce_sum.109
  76.8 0.1 broadcast_in_dim.19
  77.0 0.8 multiply_add_fusion
  (15 shorter events, 0.2 us)
Async XLA Ops:
  0.0 10.8 %copy-start = (f32[64,64]{1,0:T(8,128)S(1)}, f32[64,64]{1,0:T(8,128)}, u32[]{:S(2)}) copy-start(f32[64,64]{1,0:T(8,128)} %param.12) | copy-start | bytes 49156
  0.0 9.9 %copy-start.1 = (f32[64,1024]{1,0:T(8,128)S(1)}, f32[64,1024]{1,0:T(8,128)}, u32[]{:S(2)}) copy-start(f32[64,1024]{1,0:T(8,128)} %param.7) | copy-start | bytes 786436
  1.9 8.0 %copy-start.3 = (f32[1024]{0:T(1024)S(1)}, f32[1024]{0:T(1024)}, u32[]{:S(2)}) copy-start(f32[1024]{0:T(1024)} %param.11) | copy-start | bytes 12292
  1.9 26.6 %collective-permute-start.3 = (f32[64,8]{0,1:T(8,128)S(1)}, f32[64,8]{0,1:T(8,128)S(1)}, u32[]{:S(2)}, u32[]{:S(2)}) collective-permute-start(f32[64,8]{0,1:T(8,128)S(1)} %bitcast.122), channel_id=1, source_target_pairs={{2,0},{3,1},{4,2},{5,3},{6,4},{7,5},{8,6},{9,7},{10,8},{11,9},{12,... | collective-permute-start | bytes 6152 | tf_op jit(solution)/shard_map/ppermute | solution.py:14
  3.4 23.9 %collective-permute-start = (f32[64,8]{0,1:T(8,128)S(1)}, f32[64,8]{0,1:T(8,128)S(1)}, u32[]{:S(2)}, u32[]{:S(2)}) collective-permute-start(f32[64,8]{0,1:T(8,128)S(1)} %bitcast.123), channel_id=1, source_target_pairs={{0,2},{1,3},{2,4},{3,5},{4,6},{5,7},{6,8},{7,9},{8,10},{9,11},{10,... | collective-permute-start | bytes 6152 | tf_op jit(solution)/shard_map/ppermute | solution.py:14
  9.9 0.7 copy-start.4
  9.9 0.7 copy-start.5
  11.0 17.3 %collective-permute-start.2 = (f32[80,24]{0,1:T(8,128)S(1)}, f32[80,24]{0,1:T(8,128)S(1)}, u32[]{:S(2)}, u32[]{:S(2)}) collective-permute-start(f32[80,24]{0,1:T(8,128)S(1)} %select_maximum_fusion.4), channel_id=1, source_target_pairs={{1,0},{2,1},{3,2},{4,3},{5,4},{6,5},{7,6},{8,7},{9,8},{10,9},{11,1... | collective-permute-start | bytes 23048 | tf_op jit(solution)/shard_map/ppermute | solution.py:14
  25.3 3.1 %collective-permute-start.1 = (f32[80,24]{0,1:T(8,128)S(1)}, f32[80,24]{0,1:T(8,128)S(1)}, u32[]{:S(2)}, u32[]{:S(2)}) collective-permute-start(f32[80,24]{0,1:T(8,128)S(1)} %select_maximum_fusion.4), channel_id=1, source_target_pairs={{0,1},{1,2},{2,3},{3,4},{4,5},{5,6},{6,7},{7,8},{8,9},{9,10},{10,1... | collective-permute-start | bytes 23048 | tf_op jit(solution)/shard_map/ppermute | solution.py:14
  28.5 0.8 copy-start.2

commit v5 on v4

--- a/solution.py
+++ b/solution.py
@@ -68,6 +68,7 @@
         axis=0,
     )
     rows = moments.shape[0]
+    payload, moments = lax.optimization_barrier((payload, moments))
     below = shifted(payload, DEVICES, 1)
     above = shifted(payload, DEVICES, -1)
     two_below = shifted(moments, DEVICES, 2)

time: 78.2 us -> 73.3 us (0.937)
  blocking collectives: 44.9 us -> 41.5 us
  starting transfers between devices: 24 us -> 22.8 us
    all_to_all x2, blocking collectives: 44.9 us -> 41.5 us  [all_sum(): value = jnp.sum(lax.all_to_all(spread, axis, 0, 0, tiled=True), axis=0)]
    ppermute x4, starting transfers between devices: 24 us -> 22.8 us  [shifted(): return lax.ppermute(array, axis, pairs)]
  transfers between devices with their start and end apart: 4 -> 4, of which waited for: 1 -> 1; matrix products, arithmetic and copies ran while one was open for 1% -> 0% of each run, Pallas kernels for 0% -> 0%
where the time goes in v5:
time: 73.3 us; the launch traced here: 73 us
  blocking collectives  41.5 us (57%)
  starting transfers between devices  22.8 us (31%)
  matrix products  3.8 us (5%)
  other arithmetic  2.27 us (3%)
  local copies, waits for them, and re-layouts  1.55 us (2%)
  waiting for transfers between devices  0.8 us (1%)
    all_to_all x2, blocking collectives, all_sum(): value = jnp.sum(lax.all_to_all(spread, axis, 0, 0, tiled=True), axis=0)  41.5 us
    ppermute x4, starting transfers between devices, shifted(): return lax.ppermute(array, axis, pairs)  22.8 us
    dot_general x9, matrix products, on_device(): dot = lambda a, b: jnp.dot(a, b, precision=highest)  3.02 us
  transfers between devices with their start and end apart: 4, of which 1 were waited for; matrix products, arithmetic and copies ran while one was open for 0% of the time, Pallas kernels for 0%

profile of v5, /device:TPU:1, one launch (start us, length us, event | category | flops | bytes accessed | tf_op | source)
XLA Modules:
  0.0 73.0 jit_solution(18278829227971734352)
XLA Ops:
  0.0 0.0 copy-start
  0.0 0.0 copy-start.1
  0.0 0.7 %broadcast_subtract_fusion = s32[1024]{0:T(1024)S(1)} fusion(s32[1024]{0:T(1024)} %param.8, s32[]{:T(128)S(6)} %mul.152), kind=kLoop, calls=%fused_computation.60 | loop fusion | flops 1024 | bytes 8196 | tf_op jit(solution)/shard_map/sub | solution.py:48
  0.7 0.1 convert_reduce_fusion
  0.9 0.0 copy-start.3
  0.9 1.2 %fusion.7 = f32[8,64]{1,0:T(8,128)S(1)} fusion(f32[64,1024]{1,0:T(8,128)} %param.7, s32[1024]{0:T(1024)S(1)} %broadcast_subtract_fusion), kind=kOutput, calls=%fused_computation.22 | convolution fusion | flops 6299648 | bytes 268288 | tf_op jit(solution)/shard_map/dot_general | solution.py:57
  2.0 0.0 copy-done.1
  2.0 0.1 copy-done.3
  2.1 0.0 copy-start.4
  2.1 0.0 copy-start.5
  2.1 0.2 fusion.3
  2.3 0.5 copy-done.4
  2.8 0.0 copy-done.5
  2.8 0.1 select_reduce_fusion
  2.9 0.1 copy.16
  3.0 0.0 copy-done
  3.0 0.1 fusion.2
  3.1 0.1 select_maximum_fusion.4
  3.2 5.7 %collective-permute-start = (f32[64,8]{0,1:T(8,128)S(1)}, f32[64,8]{0,1:T(8,128)S(1)}, u32[]{:S(2)}, u32[]{:S(2)}) collective-permute-start(f32[64,8]{0,1:T(8,128)S(1)} %bitcast.122), channel_id=1, source_target_pairs={{0,2},{1,3},{2,4},{3,5},{4,6},{5,7},{6,8},{7,9},{8,10},{9,11},{10,... | collective-permute-start | bytes 6152 | tf_op jit(solution)/shard_map/ppermute | solution.py:14
  9.0 1.3 %collective-permute-start.3 = (f32[64,8]{0,1:T(8,128)S(1)}, f32[64,8]{0,1:T(8,128)S(1)}, u32[]{:S(2)}, u32[]{:S(2)}) collective-permute-start(f32[64,8]{0,1:T(8,128)S(1)} %bitcast.123), channel_id=1, source_target_pairs={{2,0},{3,1},{4,2},{5,3},{6,4},{7,5},{8,6},{9,7},{10,8},{11,9},{12,... | collective-permute-start | bytes 6152 | tf_op jit(solution)/shard_map/ppermute | solution.py:14
  10.3 11.6 %collective-permute-start.2 = (f32[80,24]{0,1:T(8,128)S(1)}, f32[80,24]{0,1:T(8,128)S(1)}, u32[]{:S(2)}, u32[]{:S(2)}) collective-permute-start(f32[80,24]{0,1:T(8,128)S(1)} %select_maximum_fusion.4), channel_id=1, source_target_pairs={{1,0},{2,1},{3,2},{4,3},{5,4},{6,5},{7,6},{8,7},{9,8},{10,9},{11,1... | collective-permute-start | bytes 23048 | tf_op jit(solution)/shard_map/ppermute | solution.py:14
  21.9 4.2 %collective-permute-start.1 = (f32[80,24]{0,1:T(8,128)S(1)}, f32[80,24]{0,1:T(8,128)S(1)}, u32[]{:S(2)}, u32[]{:S(2)}) collective-permute-start(f32[80,24]{0,1:T(8,128)S(1)} %select_maximum_fusion.4), channel_id=1, source_target_pairs={{0,1},{1,2},{2,3},{3,4},{4,5},{5,6},{6,7},{7,8},{8,9},{9,10},{10,1... | collective-permute-start | bytes 23048 | tf_op jit(solution)/shard_map/ppermute | solution.py:14
  26.1 0.0 collective-permute-done
  26.1 0.8 %collective-permute-done.1 = f32[80,24]{0,1:T(8,128)S(1)} collective-permute-done((f32[80,24]{0,1:T(8,128)S(1)}, f32[80,24]{0,1:T(8,128)S(1)}, u32[]{:S(2)}, u32[]{:S(2)}) %collective-permute-start.1) | collective-permute-done | bytes 7712 | tf_op jit(solution)/shard_map/ppermute | solution.py:14
  26.9 0.0 collective-permute-done.2
  26.9 0.1 slice.71
  27.0 0.1 slice.70
  27.0 0.0 collective-permute-done.3
  27.1 0.0 copy-start.2
  27.1 0.3 fusion.8
  27.4 0.5 copy-done.2
  27.8 0.2 convolution_bitcast_fusion.1
  28.0 0.3 fusion.6
  28.3 0.1 slice_bitcast_fusion
  28.4 0.1 slice_bitcast_fusion.1
  28.4 0.1 pad_maximum_fusion
  28.5 0.2 fusion.20
  28.7 0.2 fusion.49
  28.9 0.4 fusion
  29.3 0.4 fusion.1
  29.7 0.4 multiply_reduce_fusion
  30.1 0.1 stack.27
  30.2 0.1 reduce_sum.107
  30.3 14.6 %all_to_all.12 = f32[16,1,6]{2,1,0:T(1,128)S(1)} all-to-all(f32[16,1,6]{2,1,0:T(1,128)S(1)} %broadcast_in_dim.17), channel_id=1, replica_groups=mesh['curve'=64,'coef'=16] {'coef'}, dimensions={0} | all-to-all | bytes 768 | tf_op jit(solution)/shard_map/all_to_all | solution.py:21
  45.0 26.9 %all_to_all.13 = f32[64,1,6]{2,1,0:T(1,128)S(1)} all-to-all(f32[64,1,6]{2,1,0:T(1,128)S(1)} %broadcast_in_dim.18), channel_id=1, replica_groups=mesh['curve'=64,'coef'=16] {'curve'}, dimensions={0} | all-to-all | bytes 3072 | tf_op jit(solution)/shard_map/all_to_all | solution.py:21
  71.9 0.1 reduce_sum.109
  72.0 0.1 broadcast_in_dim.19
  72.2 0.8 %multiply_add_fusion = f32[64,1024]{1,0:T(8,128)} fusion(f32[64,1024]{1,0:T(8,128)S(1)} %fusion, f32[64,1024]{1,0:T(8,128)S(1)} %copy-done.1, f32[]{:T(128)S(1)} %bitcast.133, f32[]{:T(128)S(1)} %bitcast.132), kind=kLoop, calls=%fused_computation.8 | loop fusion | flops 196608 | bytes 786440 | tf_op jit(solution)/shard_map/add | solution.py:119
  (15 shorter events, 0.2 us)
Async XLA Ops:
  0.0 3.0 %copy-start = (f32[64,64]{1,0:T(8,128)S(1)}, f32[64,64]{1,0:T(8,128)}, u32[]{:S(2)}) copy-start(f32[64,64]{1,0:T(8,128)} %param.12) | copy-start | bytes 49156
  0.0 2.0 %copy-start.1 = (f32[64,1024]{1,0:T(8,128)S(1)}, f32[64,1024]{1,0:T(8,128)}, u32[]{:S(2)}) copy-start(f32[64,1024]{1,0:T(8,128)} %param.7) | copy-start | bytes 786436
  0.9 1.2 %copy-start.3 = (f32[1024]{0:T(1024)S(1)}, f32[1024]{0:T(1024)}, u32[]{:S(2)}) copy-start(f32[1024]{0:T(1024)} %param.11) | copy-start | bytes 12292
  2.1 0.7 copy-start.4
  2.1 0.7 copy-start.5
  3.2 22.8 %collective-permute-start = (f32[64,8]{0,1:T(8,128)S(1)}, f32[64,8]{0,1:T(8,128)S(1)}, u32[]{:S(2)}, u32[]{:S(2)}) collective-permute-start(f32[64,8]{0,1:T(8,128)S(1)} %bitcast.122), channel_id=1, source_target_pairs={{0,2},{1,3},{2,4},{3,5},{4,6},{5,7},{6,8},{7,9},{8,10},{9,11},{10,... | collective-permute-start | bytes 6152 | tf_op jit(solution)/shard_map/ppermute | solution.py:14
  9.0 18.1 %collective-permute-start.3 = (f32[64,8]{0,1:T(8,128)S(1)}, f32[64,8]{0,1:T(8,128)S(1)}, u32[]{:S(2)}, u32[]{:S(2)}) collective-permute-start(f32[64,8]{0,1:T(8,128)S(1)} %bitcast.123), channel_id=1, source_target_pairs={{2,0},{3,1},{4,2},{5,3},{6,4},{7,5},{8,6},{9,7},{10,8},{11,9},{12,... | collective-permute-start | bytes 6152 | tf_op jit(solution)/shard_map/ppermute | solution.py:14
  10.3 16.6 %collective-permute-start.2 = (f32[80,24]{0,1:T(8,128)S(1)}, f32[80,24]{0,1:T(8,128)S(1)}, u32[]{:S(2)}, u32[]{:S(2)}) collective-permute-start(f32[80,24]{0,1:T(8,128)S(1)} %select_maximum_fusion.4), channel_id=1, source_target_pairs={{1,0},{2,1},{3,2},{4,3},{5,4},{6,5},{7,6},{8,7},{9,8},{10,9},{11,1... | collective-permute-start | bytes 23048 | tf_op jit(solution)/shard_map/ppermute | solution.py:14
  21.9 5.0 %collective-permute-start.1 = (f32[80,24]{0,1:T(8,128)S(1)}, f32[80,24]{0,1:T(8,128)S(1)}, u32[]{:S(2)}, u32[]{:S(2)}) collective-permute-start(f32[80,24]{0,1:T(8,128)S(1)} %select_maximum_fusion.4), channel_id=1, source_target_pairs={{0,1},{1,2},{2,3},{3,4},{4,5},{5,6},{6,7},{7,8},{8,9},{9,10},{10,1... | collective-permute-start | bytes 23048 | tf_op jit(solution)/shard_map/ppermute | solution.py:14
  27.1 0.8 %copy-start.2 = (f32[64,64]{1,0:T(8,128)S(1)}, f32[64,64]{1,0:T(8,128)}, u32[]{:S(2)}) copy-start(f32[64,64]{1,0:T(8,128)} %param.13) | copy-start | bytes 49156

commit v6 on v5

--- a/solution.py
+++ b/solution.py
@@ -57,6 +57,7 @@
     dot = lambda a, b: jnp.dot(a, b, precision=highest)
     moments = dot(right_side, slot_table.T)
     own_part = dot(right_side * self_diag[None, :], slot_table.T) + dot(self_trans, moments)
+    moments = dot(far_trans, moments)
     g = group_count
     filler = jnp.zeros((g, g), jnp.float32)
     payload = jnp.concatenate(
@@ -90,7 +91,7 @@
         ],
         axis=0,
     )
-    local_near = dot(far_trans, dot(wide, wide_select.T))
+    local_near = dot(wide, wide_select.T)
     near_counts = jnp.concatenate([counts_below, counts, counts_above])
     near_part = jnp.concatenate([part_below, own_part, part_above], axis=1)
     near_moments = near_part + near_counts[None, :] * local_near

time: 73.3 us -> 72.8 us (level)
  no operation moved by 1% of the time
where the time goes in v6:
time: 72.8 us; the launch traced here: 72.5 us
  blocking collectives  41.5 us (57%)
  starting transfers between devices  22.8 us (31%)
  matrix products  3.82 us (5%)
  other arithmetic  2.27 us (3%)
  local copies, waits for them, and re-layouts  1.08 us (1%)
  waiting for transfers between devices  0.8 us (1%)
    all_to_all x2, blocking collectives, all_sum(): value = jnp.sum(lax.all_to_all(spread, axis, 0, 0, tiled=True), axis=0)  41.5 us
    ppermute x4, starting transfers between devices, shifted(): return lax.ppermute(array, axis, pairs)  22.8 us
    dot_general x9, matrix products, on_device(): dot = lambda a, b: jnp.dot(a, b, precision=highest)  3.04 us
  transfers between devices with their start and end apart: 4, of which 1 were waited for; matrix products, arithmetic and copies ran while one was open for 0% of the time, Pallas kernels for 0%

profile of v6, /device:TPU:1, one launch (start us, length us, event | category | flops | bytes accessed | tf_op | source)
XLA Modules:
  0.0 72.5 jit_solution(8784310390149359195)
XLA Ops:
  0.0 0.0 copy-start
  0.0 0.0 copy-start.1
  0.0 0.7 %broadcast_subtract_fusion = s32[1024]{0:T(1024)S(1)} fusion(s32[1024]{0:T(1024)} %param.8, s32[]{:T(128)S(6)} %mul.152), kind=kLoop, calls=%fused_computation.60 | loop fusion | flops 1024 | bytes 8196 | tf_op jit(solution)/shard_map/sub | solution.py:48
  0.7 0.1 convert_reduce_fusion
  0.9 0.0 copy-start.3
  0.9 1.2 %fusion.7 = f32[8,64]{1,0:T(8,128)S(1)} fusion(f32[64,1024]{1,0:T(8,128)} %param.7, s32[1024]{0:T(1024)S(1)} %broadcast_subtract_fusion), kind=kOutput, calls=%fused_computation.22 | convolution fusion | flops 6299648 | bytes 268288 | tf_op jit(solution)/shard_map/dot_general | solution.py:57
  2.0 0.0 copy-done.1
  2.0 0.1 copy-done.3
  2.1 0.0 copy-start.4
  2.1 0.0 copy-start.5
  2.1 0.0 copy-start.2
  2.1 0.2 fusion.3
  2.3 0.5 copy-done.4
  2.8 0.0 copy-done.5
  2.8 0.1 select_reduce_fusion
  2.9 0.1 copy.16
  3.0 0.0 copy-done.2
  3.0 0.1 convolution_bitcast_fusion.2
  3.1 0.0 copy-done
  3.1 0.2 fusion.2
  3.3 0.1 select_maximum_fusion.4
  3.4 5.7 %collective-permute-start = (f32[64,8]{0,1:T(8,128)S(1)}, f32[64,8]{0,1:T(8,128)S(1)}, u32[]{:S(2)}, u32[]{:S(2)}) collective-permute-start(f32[64,8]{0,1:T(8,128)S(1)} %convolution_bitcast_fusion.2), channel_id=1, source_target_pairs={{0,2},{1,3},{2,4},{3,5},{4,6},{5,7},{6,8},{7,9},{8,10},{9,11},{10,... | collective-permute-start | bytes 6152 | tf_op jit(solution)/shard_map/ppermute | solution.py:14
  9.2 1.3 %collective-permute-start.3 = (f32[64,8]{0,1:T(8,128)S(1)}, f32[64,8]{0,1:T(8,128)S(1)}, u32[]{:S(2)}, u32[]{:S(2)}) collective-permute-start(f32[64,8]{0,1:T(8,128)S(1)} %convolution_bitcast_fusion.2), channel_id=1, source_target_pairs={{2,0},{3,1},{4,2},{5,3},{6,4},{7,5},{8,6},{9,7},{10,8},{11,9},{12,... | collective-permute-start | bytes 6152 | tf_op jit(solution)/shard_map/ppermute | solution.py:14
  10.5 11.6 %collective-permute-start.2 = (f32[80,24]{0,1:T(8,128)S(1)}, f32[80,24]{0,1:T(8,128)S(1)}, u32[]{:S(2)}, u32[]{:S(2)}) collective-permute-start(f32[80,24]{0,1:T(8,128)S(1)} %select_maximum_fusion.4), channel_id=1, source_target_pairs={{1,0},{2,1},{3,2},{4,3},{5,4},{6,5},{7,6},{8,7},{9,8},{10,9},{11,1... | collective-permute-start | bytes 23048 | tf_op jit(solution)/shard_map/ppermute | solution.py:14
  22.1 4.2 %collective-permute-start.1 = (f32[80,24]{0,1:T(8,128)S(1)}, f32[80,24]{0,1:T(8,128)S(1)}, u32[]{:S(2)}, u32[]{:S(2)}) collective-permute-start(f32[80,24]{0,1:T(8,128)S(1)} %select_maximum_fusion.4), channel_id=1, source_target_pairs={{0,1},{1,2},{2,3},{3,4},{4,5},{5,6},{6,7},{7,8},{8,9},{9,10},{10,1... | collective-permute-start | bytes 23048 | tf_op jit(solution)/shard_map/ppermute | solution.py:14
  26.3 0.0 collective-permute-done
  26.3 0.8 %collective-permute-done.1 = f32[80,24]{0,1:T(8,128)S(1)} collective-permute-done((f32[80,24]{0,1:T(8,128)S(1)}, f32[80,24]{0,1:T(8,128)S(1)}, u32[]{:S(2)}, u32[]{:S(2)}) %collective-permute-start.1) | collective-permute-done | bytes 7712 | tf_op jit(solution)/shard_map/ppermute | solution.py:14
  27.1 0.0 collective-permute-done.2
  27.1 0.1 slice.71
  27.2 0.1 slice.70
  27.2 0.0 collective-permute-done.3
  27.2 0.3 fusion.8
  27.5 0.3 fusion.6
  27.8 0.1 slice_bitcast_fusion
  27.9 0.1 slice_bitcast_fusion.1
  28.0 0.1 pad_maximum_fusion
  28.1 0.2 fusion.20
  28.3 0.1 fusion.49
  28.4 0.4 fusion
  28.8 0.4 fusion.1
  29.2 0.4 multiply_reduce_fusion
  29.6 0.1 stack.27
  29.7 0.1 reduce_sum.107
  29.8 14.6 %all_to_all.12 = f32[16,1,6]{2,1,0:T(1,128)S(1)} all-to-all(f32[16,1,6]{2,1,0:T(1,128)S(1)} %broadcast_in_dim.17), channel_id=1, replica_groups=mesh['curve'=64,'coef'=16] {'coef'}, dimensions={0} | all-to-all | bytes 768 | tf_op jit(solution)/shard_map/all_to_all | solution.py:21
  44.5 26.9 %all_to_all.13 = f32[64,1,6]{2,1,0:T(1,128)S(1)} all-to-all(f32[64,1,6]{2,1,0:T(1,128)S(1)} %broadcast_in_dim.18), channel_id=1, replica_groups=mesh['curve'=64,'coef'=16] {'curve'}, dimensions={0} | all-to-all | bytes 3072 | tf_op jit(solution)/shard_map/all_to_all | solution.py:21
  71.4 0.1 reduce_sum.109
  71.5 0.1 broadcast_in_dim.19
  71.7 0.8 %multiply_add_fusion = f32[64,1024]{1,0:T(8,128)} fusion(f32[64,1024]{1,0:T(8,128)S(1)} %fusion, f32[64,1024]{1,0:T(8,128)S(1)} %copy-done.1, f32[]{:T(128)S(1)} %bitcast.128, f32[]{:T(128)S(1)} %bitcast.127), kind=kLoop, calls=%fused_computation.8 | loop fusion | flops 196608 | bytes 786440 | tf_op jit(solution)/shard_map/add | solution.py:120
  (15 shorter events, 0.2 us)
Async XLA Ops:
  0.0 3.1 %copy-start = (f32[64,64]{1,0:T(8,128)S(1)}, f32[64,64]{1,0:T(8,128)}, u32[]{:S(2)}) copy-start(f32[64,64]{1,0:T(8,128)} %param.12) | copy-start | bytes 49156
  0.0 2.0 %copy-start.1 = (f32[64,1024]{1,0:T(8,128)S(1)}, f32[64,1024]{1,0:T(8,128)}, u32[]{:S(2)}) copy-start(f32[64,1024]{1,0:T(8,128)} %param.7) | copy-start | bytes 786436
  0.9 1.2 %copy-start.3 = (f32[1024]{0:T(1024)S(1)}, f32[1024]{0:T(1024)}, u32[]{:S(2)}) copy-start(f32[1024]{0:T(1024)} %param.11) | copy-start | bytes 12292
  2.1 0.7 copy-start.4
  2.1 0.7 copy-start.5
  2.1 0.9 %copy-start.2 = (f32[64,64]{1,0:T(8,128)S(1)}, f32[64,64]{1,0:T(8,128)}, u32[]{:S(2)}) copy-start(f32[64,64]{1,0:T(8,128)} %param.13) | copy-start | bytes 49156
  3.4 22.8 %collective-permute-start = (f32[64,8]{0,1:T(8,128)S(1)}, f32[64,8]{0,1:T(8,128)S(1)}, u32[]{:S(2)}, u32[]{:S(2)}) collective-permute-start(f32[64,8]{0,1:T(8,128)S(1)} %convolution_bitcast_fusion.2), channel_id=1, source_target_pairs={{0,2},{1,3},{2,4},{3,5},{4,6},{5,7},{6,8},{7,9},{8,10},{9,11},{10,... | collective-permute-start | bytes 6152 | tf_op jit(solution)/shard_map/ppermute | solution.py:14
  9.2 18.1 %collective-permute-start.3 = (f32[64,8]{0,1:T(8,128)S(1)}, f32[64,8]{0,1:T(8,128)S(1)}, u32[]{:S(2)}, u32[]{:S(2)}) collective-permute-start(f32[64,8]{0,1:T(8,128)S(1)} %convolution_bitcast_fusion.2), channel_id=1, source_target_pairs={{2,0},{3,1},{4,2},{5,3},{6,4},{7,5},{8,6},{9,7},{10,8},{11,9},{12,... | collective-permute-start | bytes 6152 | tf_op jit(solution)/shard_map/ppermute | solution.py:14
  10.5 16.6 %collective-permute-start.2 = (f32[80,24]{0,1:T(8,128)S(1)}, f32[80,24]{0,1:T(8,128)S(1)}, u32[]{:S(2)}, u32[]{:S(2)}) collective-permute-start(f32[80,24]{0,1:T(8,128)S(1)} %select_maximum_fusion.4), channel_id=1, source_target_pairs={{1,0},{2,1},{3,2},{4,3},{5,4},{6,5},{7,6},{8,7},{9,8},{10,9},{11,1... | collective-permute-start | bytes 23048 | tf_op jit(solution)/shard_map/ppermute | solution.py:14
  22.1 5.0 %collective-permute-start.1 = (f32[80,24]{0,1:T(8,128)S(1)}, f32[80,24]{0,1:T(8,128)S(1)}, u32[]{:S(2)}, u32[]{:S(2)}) collective-permute-start(f32[80,24]{0,1:T(8,128)S(1)} %select_maximum_fusion.4), channel_id=1, source_target_pairs={{0,1},{1,2},{2,3},{3,4},{4,5},{5,6},{6,7},{7,8},{8,9},{9,10},{10,1... | collective-permute-start | bytes 23048 | tf_op jit(solution)/shard_map/ppermute | solution.py:14

commit v7 on v6

--- a/solution.py
+++ b/solution.py
@@ -55,8 +55,9 @@
     counts = jnp.sum(slot_table, axis=1)
     highest = lax.Precision.HIGHEST
     dot = lambda a, b: jnp.dot(a, b, precision=highest)
-    moments = dot(right_side, slot_table.T)
-    own_part = dot(right_side * self_diag[None, :], slot_table.T) + dot(self_trans, moments)
+    onehot_right = lambda a, b: jnp.dot(a, b, precision=(highest, lax.Precision.DEFAULT))
+    moments = onehot_right(right_side, slot_table.T)
+    own_part = onehot_right(right_side * self_diag[None, :], slot_table.T) + dot(self_trans, moments)
     moments = dot(far_trans, moments)
     g = group_count
     filler = jnp.zeros((g, g), jnp.float32)
@@ -95,9 +96,9 @@
     near_counts = jnp.concatenate([counts_below, counts, counts_above])
     near_part = jnp.concatenate([part_below, own_part, part_above], axis=1)
     near_moments = near_part + near_counts[None, :] * local_near
-    first = local_part(right_side, self_diag, self_trans) + dot(local_near[:, g : 2 * g], slot_table)
+    first = local_part(right_side, self_diag, self_trans) + onehot_right(local_near[:, g : 2 * g], slot_table)
     local_next = dot(far_trans, dot(near_moments, select_mat.T))
-    second = local_part(first, self_diag, self_trans) + dot(local_next, slot_table)
+    second = local_part(first, self_diag, self_trans) + onehot_right(local_next, slot_table)
     krylov = (right_side, first, second)
     columns_sums = jnp.stack([jnp.sum(krylov[i] * krylov[j], axis=0) for i, j in GRAM_PAIRS])
     partials = jnp.sum(columns_sums, axis=1)

time: 72.8 us -> 72.8 us (level)
    dot_general x0 -> x4, matrix products: none -> 2.09 us  [on_device(): jnp.dot(a, b, precision=(highest, lax.Precision.DEFAULT))]
    dot_general x9 -> x5, matrix products: 3.04 us -> 0.95 us  [on_device(): dot = lambda a, b: jnp.dot(a, b, precision=highest)]
where the time goes in v7:
time: 72.8 us; the launch traced here: 72.5 us
  blocking collectives  41.5 us (57%)
  starting transfers between devices  22.8 us (31%)
  matrix products  3.82 us (5%)
  other arithmetic  2.27 us (3%)
  local copies, waits for them, and re-layouts  1.08 us (1%)
  waiting for transfers between devices  0.8 us (1%)
    all_to_all x2, blocking collectives, all_sum(): value = jnp.sum(lax.all_to_all(spread, axis, 0, 0, tiled=True), axis=0)  41.5 us
    ppermute x4, starting transfers between devices, shifted(): return lax.ppermute(array, axis, pairs)  22.8 us
    dot_general x4, matrix products, on_device(): jnp.dot(a, b, precision=(highest, lax.Precision.DEFAULT))  2.09 us
  transfers between devices with their start and end apart: 4, of which 1 were waited for; matrix products, arithmetic and copies ran while one was open for 0% of the time, Pallas kernels for 0%

profile of v7, /device:TPU:1, one launch (start us, length us, event | category | flops | bytes accessed | tf_op | source)
XLA Modules:
  0.0 72.5 jit_solution(8784310390149359195)
XLA Ops:
  0.0 0.0 copy-start
  0.0 0.0 copy-start.1
  0.0 0.7 %broadcast_subtract_fusion = s32[1024]{0:T(1024)S(1)} fusion(s32[1024]{0:T(1024)} %param.8, s32[]{:T(128)S(6)} %mul.152), kind=kLoop, calls=%fused_computation.60 | loop fusion | flops 1024 | bytes 8196 | tf_op jit(solution)/shard_map/sub | solution.py:48
  0.7 0.1 convert_reduce_fusion
  0.9 0.0 copy-start.3
  0.9 1.2 %fusion.7 = f32[8,64]{1,0:T(8,128)S(1)} fusion(f32[64,1024]{1,0:T(8,128)} %param.7, s32[1024]{0:T(1024)S(1)} %broadcast_subtract_fusion), kind=kOutput, calls=%fused_computation.22 | convolution fusion | flops 6299648 | bytes 268288 | tf_op jit(solution)/shard_map/dot_general | solution.py:58
  2.0 0.0 copy-done.1
  2.0 0.1 copy-done.3
  2.1 0.0 copy-start.4
  2.1 0.0 copy-start.5
  2.1 0.0 copy-start.2
  2.1 0.2 fusion.3
  2.3 0.5 copy-done.4
  2.8 0.0 copy-done.5
  2.8 0.1 select_reduce_fusion
  2.9 0.1 copy.16
  3.0 0.0 copy-done.2
  3.0 0.1 convolution_bitcast_fusion.2
  3.1 0.0 copy-done
  3.1 0.2 fusion.2
  3.3 0.1 select_maximum_fusion.4
  3.4 5.7 %collective-permute-start = (f32[64,8]{0,1:T(8,128)S(1)}, f32[64,8]{0,1:T(8,128)S(1)}, u32[]{:S(2)}, u32[]{:S(2)}) collective-permute-start(f32[64,8]{0,1:T(8,128)S(1)} %convolution_bitcast_fusion.2), channel_id=1, source_target_pairs={{0,2},{1,3},{2,4},{3,5},{4,6},{5,7},{6,8},{7,9},{8,10},{9,11},{10,... | collective-permute-start | bytes 6152 | tf_op jit(solution)/shard_map/ppermute | solution.py:14
  9.2 1.3 %collective-permute-start.3 = (f32[64,8]{0,1:T(8,128)S(1)}, f32[64,8]{0,1:T(8,128)S(1)}, u32[]{:S(2)}, u32[]{:S(2)}) collective-permute-start(f32[64,8]{0,1:T(8,128)S(1)} %convolution_bitcast_fusion.2), channel_id=1, source_target_pairs={{2,0},{3,1},{4,2},{5,3},{6,4},{7,5},{8,6},{9,7},{10,8},{11,9},{12,... | collective-permute-start | bytes 6152 | tf_op jit(solution)/shard_map/ppermute | solution.py:14
  10.5 11.6 %collective-permute-start.2 = (f32[80,24]{0,1:T(8,128)S(1)}, f32[80,24]{0,1:T(8,128)S(1)}, u32[]{:S(2)}, u32[]{:S(2)}) collective-permute-start(f32[80,24]{0,1:T(8,128)S(1)} %select_maximum_fusion.4), channel_id=1, source_target_pairs={{1,0},{2,1},{3,2},{4,3},{5,4},{6,5},{7,6},{8,7},{9,8},{10,9},{11,1... | collective-permute-start | bytes 23048 | tf_op jit(solution)/shard_map/ppermute | solution.py:14
  22.1 4.2 %collective-permute-start.1 = (f32[80,24]{0,1:T(8,128)S(1)}, f32[80,24]{0,1:T(8,128)S(1)}, u32[]{:S(2)}, u32[]{:S(2)}) collective-permute-start(f32[80,24]{0,1:T(8,128)S(1)} %select_maximum_fusion.4), channel_id=1, source_target_pairs={{0,1},{1,2},{2,3},{3,4},{4,5},{5,6},{6,7},{7,8},{8,9},{9,10},{10,1... | collective-permute-start | bytes 23048 | tf_op jit(solution)/shard_map/ppermute | solution.py:14
  26.3 0.0 collective-permute-done
  26.3 0.8 %collective-permute-done.1 = f32[80,24]{0,1:T(8,128)S(1)} collective-permute-done((f32[80,24]{0,1:T(8,128)S(1)}, f32[80,24]{0,1:T(8,128)S(1)}, u32[]{:S(2)}, u32[]{:S(2)}) %collective-permute-start.1) | collective-permute-done | bytes 7712 | tf_op jit(solution)/shard_map/ppermute | solution.py:14
  27.1 0.0 collective-permute-done.2
  27.1 0.1 slice.71
  27.2 0.1 slice.70
  27.2 0.0 collective-permute-done.3
  27.2 0.3 fusion.8
  27.5 0.3 fusion.6
  27.8 0.1 slice_bitcast_fusion
  27.9 0.1 slice_bitcast_fusion.1
  28.0 0.1 pad_maximum_fusion
  28.1 0.2 fusion.20
  28.3 0.1 fusion.49
  28.4 0.4 fusion
  28.8 0.4 fusion.1
  29.2 0.4 multiply_reduce_fusion
  29.6 0.1 stack.27
  29.7 0.1 reduce_sum.107
  29.8 14.6 %all_to_all.12 = f32[16,1,6]{2,1,0:T(1,128)S(1)} all-to-all(f32[16,1,6]{2,1,0:T(1,128)S(1)} %broadcast_in_dim.17), channel_id=1, replica_groups=mesh['curve'=64,'coef'=16] {'coef'}, dimensions={0} | all-to-all | bytes 768 | tf_op jit(solution)/shard_map/all_to_all | solution.py:21
  44.5 26.9 %all_to_all.13 = f32[64,1,6]{2,1,0:T(1,128)S(1)} all-to-all(f32[64,1,6]{2,1,0:T(1,128)S(1)} %broadcast_in_dim.18), channel_id=1, replica_groups=mesh['curve'=64,'coef'=16] {'curve'}, dimensions={0} | all-to-all | bytes 3072 | tf_op jit(solution)/shard_map/all_to_all | solution.py:21
  71.4 0.1 reduce_sum.109
  71.5 0.1 broadcast_in_dim.19
  71.7 0.8 %multiply_add_fusion = f32[64,1024]{1,0:T(8,128)} fusion(f32[64,1024]{1,0:T(8,128)S(1)} %fusion, f32[64,1024]{1,0:T(8,128)S(1)} %copy-done.1, f32[]{:T(128)S(1)} %bitcast.128, f32[]{:T(128)S(1)} %bitcast.127), kind=kLoop, calls=%fused_computation.8 | loop fusion | flops 196608 | bytes 786440 | tf_op jit(solution)/shard_map/add | solution.py:121
  (15 shorter events, 0.2 us)
Async XLA Ops:
  0.0 3.1 %copy-start = (f32[64,64]{1,0:T(8,128)S(1)}, f32[64,64]{1,0:T(8,128)}, u32[]{:S(2)}) copy-start(f32[64,64]{1,0:T(8,128)} %param.12) | copy-start | bytes 49156
  0.0 2.0 %copy-start.1 = (f32[64,1024]{1,0:T(8,128)S(1)}, f32[64,1024]{1,0:T(8,128)}, u32[]{:S(2)}) copy-start(f32[64,1024]{1,0:T(8,128)} %param.7) | copy-start | bytes 786436
  0.9 1.2 %copy-start.3 = (f32[1024]{0:T(1024)S(1)}, f32[1024]{0:T(1024)}, u32[]{:S(2)}) copy-start(f32[1024]{0:T(1024)} %param.11) | copy-start | bytes 12292
  2.1 0.7 copy-start.4
  2.1 0.7 copy-start.5
  2.1 0.9 %copy-start.2 = (f32[64,64]{1,0:T(8,128)S(1)}, f32[64,64]{1,0:T(8,128)}, u32[]{:S(2)}) copy-start(f32[64,64]{1,0:T(8,128)} %param.13) | copy-start | bytes 49156
  3.4 22.8 %collective-permute-start = (f32[64,8]{0,1:T(8,128)S(1)}, f32[64,8]{0,1:T(8,128)S(1)}, u32[]{:S(2)}, u32[]{:S(2)}) collective-permute-start(f32[64,8]{0,1:T(8,128)S(1)} %convolution_bitcast_fusion.2), channel_id=1, source_target_pairs={{0,2},{1,3},{2,4},{3,5},{4,6},{5,7},{6,8},{7,9},{8,10},{9,11},{10,... | collective-permute-start | bytes 6152 | tf_op jit(solution)/shard_map/ppermute | solution.py:14
  9.2 18.1 %collective-permute-start.3 = (f32[64,8]{0,1:T(8,128)S(1)}, f32[64,8]{0,1:T(8,128)S(1)}, u32[]{:S(2)}, u32[]{:S(2)}) collective-permute-start(f32[64,8]{0,1:T(8,128)S(1)} %convolution_bitcast_fusion.2), channel_id=1, source_target_pairs={{2,0},{3,1},{4,2},{5,3},{6,4},{7,5},{8,6},{9,7},{10,8},{11,9},{12,... | collective-permute-start | bytes 6152 | tf_op jit(solution)/shard_map/ppermute | solution.py:14
  10.5 16.6 %collective-permute-start.2 = (f32[80,24]{0,1:T(8,128)S(1)}, f32[80,24]{0,1:T(8,128)S(1)}, u32[]{:S(2)}, u32[]{:S(2)}) collective-permute-start(f32[80,24]{0,1:T(8,128)S(1)} %select_maximum_fusion.4), channel_id=1, source_target_pairs={{1,0},{2,1},{3,2},{4,3},{5,4},{6,5},{7,6},{8,7},{9,8},{10,9},{11,1... | collective-permute-start | bytes 23048 | tf_op jit(solution)/shard_map/ppermute | solution.py:14
  22.1 5.0 %collective-permute-start.1 = (f32[80,24]{0,1:T(8,128)S(1)}, f32[80,24]{0,1:T(8,128)S(1)}, u32[]{:S(2)}, u32[]{:S(2)}) collective-permute-start(f32[80,24]{0,1:T(8,128)S(1)} %select_maximum_fusion.4), channel_id=1, source_target_pairs={{0,1},{1,2},{2,3},{3,4},{4,5},{5,6},{6,7},{7,8},{8,9},{9,10},{10,1... | collective-permute-start | bytes 23048 | tf_op jit(solution)/shard_map/ppermute | solution.py:14

commit v8 on v7

--- a/solution.py
+++ b/solution.py
@@ -57,7 +57,9 @@
     dot = lambda a, b: jnp.dot(a, b, precision=highest)
     onehot_right = lambda a, b: jnp.dot(a, b, precision=(highest, lax.Precision.DEFAULT))
     moments = onehot_right(right_side, slot_table.T)
-    own_part = onehot_right(right_side * self_diag[None, :], slot_table.T) + dot(self_trans, moments)
+    diag_moments = onehot_right(right_side * self_diag[None, :], slot_table.T)
+    own_part = diag_moments + dot(self_trans, moments)
+    untranslated = moments
     moments = dot(far_trans, moments)
     g = group_count
     filler = jnp.zeros((g, g), jnp.float32)
@@ -96,12 +98,50 @@
     near_counts = jnp.concatenate([counts_below, counts, counts_above])
     near_part = jnp.concatenate([part_below, own_part, part_above], axis=1)
     near_moments = near_part + near_counts[None, :] * local_near
-    first = local_part(right_side, self_diag, self_trans) + onehot_right(local_near[:, g : 2 * g], slot_table)
-    local_next = dot(far_trans, dot(near_moments, select_mat.T))
-    second = local_part(first, self_diag, self_trans) + onehot_right(local_next, slot_table)
-    krylov = (right_side, first, second)
-    columns_sums = jnp.stack([jnp.sum(krylov[i] * krylov[j], axis=0) for i, j in GRAM_PAIRS])
-    partials = jnp.sum(columns_sums, axis=1)
+    once = local_part(right_side, self_diag, self_trans)
+    twice = local_part(once, self_diag, self_trans)
+    column_sums = jnp.stack(
+        [
+            jnp.sum(a * b, axis=0)
+            for a, b in (
+                (right_side, right_side),
+                (right_side, once),
+                (right_side, twice),
+                (once, once),
+                (once, twice),
+                (twice, twice),
+            )
+        ]
+    )
+    diag_once = onehot_right(once * self_diag[None, :], slot_table.T)
+    twice_sums = onehot_right(twice, slot_table.T)
+    diag_twice = onehot_right(twice * self_diag[None, :], slot_table.T)
+    diag_sums = onehot_right(self_diag[None, :], slot_table.T)[0]
+    diag_squares = onehot_right((self_diag * self_diag)[None, :], slot_table.T)[0]
+    first_far = local_near[:, g : 2 * g]
+    second_far = dot(far_trans, dot(near_moments, select_mat.T))
+    shared = dot(self_trans, first_far) + second_far
+    far_sq = first_far * first_far
+    far_shared = first_far * shared
+    group_terms = jnp.stack(
+        [
+            jnp.zeros_like(first_far),
+            untranslated * first_far,
+            diag_moments * first_far + untranslated * shared,
+            2.0 * own_part * first_far + counts[None, :] * far_sq,
+            (diag_once + twice_sums) * first_far
+            + own_part * shared
+            + diag_sums[None, :] * far_sq
+            + counts[None, :] * far_shared,
+            2.0 * diag_twice * first_far
+            + 2.0 * twice_sums * shared
+            + diag_squares[None, :] * far_sq
+            + 2.0 * diag_sums[None, :] * far_shared
+            + counts[None, :] * shared * shared,
+        ]
+    )
+    partials = jnp.sum(column_sums, axis=1) + jnp.sum(group_terms, axis=(1, 2))
+    first = once + onehot_right(first_far, slot_table)
     totals = all_sum(partials)
     lanes = lax.optimization_barrier(jnp.broadcast_to(totals[:, None], (len(GRAM_PAIRS), 128)))
     g00, g01, g02, g11, g12, g22 = [lanes[k] for k in range(len(GRAM_PAIRS))]

time: 72.8 us -> 74.7 us (1.026)
  starting transfers between devices: 22.8 us -> 19.9 us
  blocking collectives: 41.5 us -> 44.3 us
  matrix products: 3.82 us -> 5.39 us
    ppermute x4, starting transfers between devices: 22.8 us -> 19.9 us  [shifted(): return lax.ppermute(array, axis, pairs)]
    all_to_all x2, blocking collectives: 41.5 us -> 44.3 us  [all_sum(): value = jnp.sum(lax.all_to_all(spread, axis, 0, 0, tiled=True), axis=0)]
    dot_general x4 -> x8, matrix products: 2.09 us -> 3.46 us  [on_device(): jnp.dot(a, b, precision=(highest, lax.Precision.DEFAULT))]
    add x1, other arithmetic: 0.78 us -> 0.01 us  [on_device(): partials = jnp.sum(column_sums, axis=1) + jnp.sum(group_terms, axis=(1, 2))]
  transfers between devices with their start and end apart: 4 -> 4, of which waited for: 1 -> 1; matrix products, arithmetic and copies ran while one was open for 0% -> 2% of each run, Pallas kernels for 0% -> 0%
where the time goes in v8:
time: 74.7 us; the launch traced here: 74.3 us
  blocking collectives  44.3 us (59%)
  starting transfers between devices  19.9 us (27%)
  matrix products  5.39 us (7%)
  other arithmetic  1.74 us (2%)
  waiting for transfers between devices  1.39 us (2%)
  local copies, waits for them, and re-layouts  1.24 us (2%)
    all_to_all x2, blocking collectives, all_sum(): value = jnp.sum(lax.all_to_all(spread, axis, 0, 0, tiled=True), axis=0)  44.3 us
    ppermute x4, starting transfers between devices, shifted(): return lax.ppermute(array, axis, pairs)  19.9 us
    dot_general x8, matrix products, on_device(): jnp.dot(a, b, precision=(highest, lax.Precision.DEFAULT))  3.46 us
  transfers between devices with their start and end apart: 4, of which 1 were waited for; matrix products, arithmetic and copies ran while one was open for 2% of the time, Pallas kernels for 0%

profile of v8, /device:TPU:1, one launch (start us, length us, event | category | flops | bytes accessed | tf_op | source)
XLA Modules:
  0.0 74.3 jit_solution(4273710030468626427)
XLA Ops:
  0.0 0.0 copy-start
  0.0 0.0 copy-start.1
  0.0 0.7 broadcast_subtract_fusion
  0.7 0.1 convert_reduce_fusion
  0.9 0.0 copy-start.2
  0.9 1.2 %fusion.40 = f32[8,64]{1,0:T(8,128)S(1)} fusion(f32[64,1024]{1,0:T(8,128)} %param.7, s32[1024]{0:T(1024)S(1)} %broadcast_subtract_fusion), kind=kOutput, calls=%fused_computation.45 | convolution fusion | flops 6299648 | bytes 268288 | tf_op jit(solution)/shard_map/dot_general | solution.py:58
  2.0 0.0 copy-done.1
  2.0 0.1 copy-done.2
  2.1 0.0 copy-start.4
  2.1 0.0 copy-start.5
  2.1 0.2 fusion.34
  2.3 0.0 copy-start.3
  2.4 0.4 copy-done.4
  2.8 0.0 copy-done.5
  2.8 0.1 select_reduce_fusion
  2.9 0.1 copy.16
  3.0 0.1 copy-done.3
  3.1 0.1 convolution_bitcast_fusion.2
  3.3 0.0 copy-done
  3.3 0.2 fusion.10
  3.4 0.1 select_maximum_fusion.4
  3.6 6.3 %collective-permute-start.1 = (f32[80,24]{0,1:T(8,128)S(1)}, f32[80,24]{0,1:T(8,128)S(1)}, u32[]{:S(2)}, u32[]{:S(2)}) collective-permute-start(f32[80,24]{0,1:T(8,128)S(1)} %select_maximum_fusion.4), channel_id=1, source_target_pairs={{0,1},{1,2},{2,3},{3,4},{4,5},{5,6},{6,7},{7,8},{8,9},{9,10},{10,1... | collective-permute-start | bytes 23048 | tf_op jit(solution)/shard_map/ppermute | solution.py:14
  9.9 11.1 %collective-permute-start.2 = (f32[80,24]{0,1:T(8,128)S(1)}, f32[80,24]{0,1:T(8,128)S(1)}, u32[]{:S(2)}, u32[]{:S(2)}) collective-permute-start(f32[80,24]{0,1:T(8,128)S(1)} %select_maximum_fusion.4), channel_id=1, source_target_pairs={{1,0},{2,1},{3,2},{4,3},{5,4},{6,5},{7,6},{8,7},{9,8},{10,9},{11,1... | collective-permute-start | bytes 23048 | tf_op jit(solution)/shard_map/ppermute | solution.py:14
  20.9 1.3 %collective-permute-start = (f32[64,8]{0,1:T(8,128)S(1)}, f32[64,8]{0,1:T(8,128)S(1)}, u32[]{:S(2)}, u32[]{:S(2)}) collective-permute-start(f32[64,8]{0,1:T(8,128)S(1)} %convolution_bitcast_fusion.2), channel_id=1, source_target_pairs={{0,2},{1,3},{2,4},{3,5},{4,6},{5,7},{6,8},{7,9},{8,10},{9,11},{10,... | collective-permute-start | bytes 6152 | tf_op jit(solution)/shard_map/ppermute | solution.py:14
  22.2 1.3 %collective-permute-start.3 = (f32[64,8]{0,1:T(8,128)S(1)}, f32[64,8]{0,1:T(8,128)S(1)}, u32[]{:S(2)}, u32[]{:S(2)}) collective-permute-start(f32[64,8]{0,1:T(8,128)S(1)} %convolution_bitcast_fusion.2), channel_id=1, source_target_pairs={{2,0},{3,1},{4,2},{5,3},{6,4},{7,5},{8,6},{9,7},{10,8},{11,9},{12,... | collective-permute-start | bytes 6152 | tf_op jit(solution)/shard_map/ppermute | solution.py:14
  23.5 0.4 convolution_add_fusion
  23.9 0.5 multiply_reduce_fusion
  24.4 0.2 fusion.39
  24.6 0.2 broadcast_multiply_fusion
  24.7 0.2 convolution_bitcast_fusion.3
  24.9 0.1 stack.45
  25.0 0.1 reduce_sum.114
  25.1 0.0 collective-permute-done
  25.1 0.0 collective-permute-done.1
  25.2 0.0 collective-permute-done.2
  25.2 0.1 slice.70
  25.3 0.1 slice.71
  25.3 1.4 %collective-permute-done.3 = f32[64,8]{0,1:T(8,128)S(1)} collective-permute-done((f32[64,8]{0,1:T(8,128)S(1)}, f32[64,8]{0,1:T(8,128)S(1)}, u32[]{:S(2)}, u32[]{:S(2)}) %collective-permute-start.3) | collective-permute-done | bytes 2080 | tf_op jit(solution)/shard_map/ppermute | solution.py:14
  26.7 0.3 fusion.41
  27.0 0.1 fusion.69
  27.2 0.1 slice_bitcast_fusion
  27.3 0.1 slice_bitcast_fusion.1
  27.3 0.1 pad_maximum_fusion
  27.4 0.2 fusion.57
  27.6 0.2 constant_dynamic-update-slice_fusion.6
  27.8 0.1 constant_dynamic-update-slice_fusion.5
  27.8 0.2 fusion.31
  28.1 0.3 fusion.21
  28.4 0.2 reduce_sum.117
  28.6 18.8 %all_to_all.12 = f32[16,1,6]{2,1,0:T(1,128)S(1)} all-to-all(f32[16,1,6]{2,1,0:T(1,128)S(1)} %broadcast_in_dim.17), channel_id=1, replica_groups=mesh['curve'=64,'coef'=16] {'coef'}, dimensions={0} | all-to-all | bytes 768 | tf_op jit(solution)/shard_map/all_to_all | solution.py:21
  47.4 25.5 %all_to_all.13 = f32[64,1,6]{2,1,0:T(1,128)S(1)} all-to-all(f32[64,1,6]{2,1,0:T(1,128)S(1)} %broadcast_in_dim.18), channel_id=1, replica_groups=mesh['curve'=64,'coef'=16] {'curve'}, dimensions={0} | all-to-all | bytes 3072 | tf_op jit(solution)/shard_map/all_to_all | solution.py:21
  73.0 0.1 reduce_sum.119
  73.0 0.1 broadcast_in_dim.19
  73.2 1.1 %fusion.1 = f32[64,1024]{1,0:T(8,128)} fusion(f32[64,1024]{1,0:T(8,128)S(1)} %convolution_add_fusion, f32[64,1024]{1,0:T(8,128)S(1)} %copy-done.1, f32[]{:T(128)S(1)} %bitcast.164, f32[]{:T(128)S(1)} %bitcast.163, s32[1024]{0:T(1024)S(1)} %broadcast_subtract_fusion, f32[64,24]{0,1:T(8,128)S(1)} %fusion.41), kind=kOutput, calls=%fused_computation.3 | convolution fusion | flops 6561792 | bytes 795648 | tf_op jit(solution)/shard_map/dot_general | solution.py:58
  (19 shorter events, 0.2 us)
Async XLA Ops:
  0.0 3.3 %copy-start = (f32[64,64]{1,0:T(8,128)S(1)}, f32[64,64]{1,0:T(8,128)}, u32[]{:S(2)}) copy-start(f32[64,64]{1,0:T(8,128)} %param.12) | copy-start | bytes 49156
  0.0 2.0 %copy-start.1 = (f32[64,1024]{1,0:T(8,128)S(1)}, f32[64,1024]{1,0:T(8,128)}, u32[]{:S(2)}) copy-start(f32[64,1024]{1,0:T(8,128)} %param.7) | copy-start | bytes 786436
  0.9 1.2 %copy-start.2 = (f32[1024]{0:T(1024)S(1)}, f32[1024]{0:T(1024)}, u32[]{:S(2)}) copy-start(f32[1024]{0:T(1024)} %param.11) | copy-start | bytes 12292
  2.1 0.7 copy-start.4
  2.1 0.7 copy-start.5
  2.3 0.8 %copy-start.3 = (f32[64,64]{1,0:T(8,128)S(1)}, f32[64,64]{1,0:T(8,128)}, u32[]{:S(2)}) copy-start(f32[64,64]{1,0:T(8,128)} %param.13) | copy-start | bytes 49156
  3.6 21.6 %collective-permute-start.1 = (f32[80,24]{0,1:T(8,128)S(1)}, f32[80,24]{0,1:T(8,128)S(1)}, u32[]{:S(2)}, u32[]{:S(2)}) collective-permute-start(f32[80,24]{0,1:T(8,128)S(1)} %select_maximum_fusion.4), channel_id=1, source_target_pairs={{0,1},{1,2},{2,3},{3,4},{4,5},{5,6},{6,7},{7,8},{8,9},{9,10},{10,1... | collective-permute-start | bytes 23048 | tf_op jit(solution)/shard_map/ppermute | solution.py:14
  9.9 15.3 %collective-permute-start.2 = (f32[80,24]{0,1:T(8,128)S(1)}, f32[80,24]{0,1:T(8,128)S(1)}, u32[]{:S(2)}, u32[]{:S(2)}) collective-permute-start(f32[80,24]{0,1:T(8,128)S(1)} %select_maximum_fusion.4), channel_id=1, source_target_pairs={{1,0},{2,1},{3,2},{4,3},{5,4},{6,5},{7,6},{8,7},{9,8},{10,9},{11,1... | collective-permute-start | bytes 23048 | tf_op jit(solution)/shard_map/ppermute | solution.py:14
  20.9 4.2 %collective-permute-start = (f32[64,8]{0,1:T(8,128)S(1)}, f32[64,8]{0,1:T(8,128)S(1)}, u32[]{:S(2)}, u32[]{:S(2)}) collective-permute-start(f32[64,8]{0,1:T(8,128)S(1)} %convolution_bitcast_fusion.2), channel_id=1, source_target_pairs={{0,2},{1,3},{2,4},{3,5},{4,6},{5,7},{6,8},{7,9},{8,10},{9,11},{10,... | collective-permute-start | bytes 6152 | tf_op jit(solution)/shard_map/ppermute | solution.py:14
  22.2 4.5 %collective-permute-start.3 = (f32[64,8]{0,1:T(8,128)S(1)}, f32[64,8]{0,1:T(8,128)S(1)}, u32[]{:S(2)}, u32[]{:S(2)}) collective-permute-start(f32[64,8]{0,1:T(8,128)S(1)} %convolution_bitcast_fusion.2), channel_id=1, source_target_pairs={{2,0},{3,1},{4,2},{5,3},{6,4},{7,5},{8,6},{9,7},{10,8},{11,9},{12,... | collective-permute-start | bytes 6152 | tf_op jit(solution)/shard_map/ppermute | solution.py:14

commit v9 on v6

--- a/solution.py
+++ b/solution.py
@@ -53,6 +53,7 @@
     matches = (pair_sources[:, :, None] == columns[None, None, :]).astype(jnp.float32)
     select_mat = jnp.sum(pair_weights[:, :, None] * matches, axis=1)
     counts = jnp.sum(slot_table, axis=1)
+    select_mat, counts, right_side = lax.optimization_barrier((select_mat, counts, right_side))
     highest = lax.Precision.HIGHEST
     dot = lambda a, b: jnp.dot(a, b, precision=highest)
     moments = dot(right_side, slot_table.T)

time: 72.8 us -> 77.9 us (1.070)
  blocking collectives: 41.5 us -> 44.9 us
  starting transfers between devices: 22.8 us -> 23.8 us
  other arithmetic: 2.27 us -> 3.05 us
    all_to_all x2, blocking collectives: 41.5 us -> 44.9 us  [all_sum(): value = jnp.sum(lax.all_to_all(spread, axis, 0, 0, tiled=True), axis=0)]
    ppermute x4, starting transfers between devices: 22.8 us -> 23.8 us  [shifted(): return lax.ppermute(array, axis, pairs)]
  transfers between devices with their start and end apart: 4 -> 4, of which waited for: 1 -> 1; matrix products, arithmetic and copies ran while one was open for 0% -> 1% of each run, Pallas kernels for 0% -> 0%
where the time goes in v9:
time: 77.9 us; the launch traced here: 77.5 us
  blocking collectives  44.9 us (58%)
  starting transfers between devices  23.8 us (31%)
  matrix products  3.8 us (5%)
  other arithmetic  3.05 us (4%)
  local copies, waits for them, and re-layouts  1.15 us (1%)
    all_to_all x2, blocking collectives, all_sum(): value = jnp.sum(lax.all_to_all(spread, axis, 0, 0, tiled=True), axis=0)  44.9 us
    ppermute x4, starting transfers between devices, shifted(): return lax.ppermute(array, axis, pairs)  23.8 us
    dot_general x9, matrix products, on_device(): dot = lambda a, b: jnp.dot(a, b, precision=highest)  3.06 us
  transfers between devices with their start and end apart: 4, of which 1 were waited for; matrix products, arithmetic and copies ran while one was open for 1% of the time, Pallas kernels for 0%

profile of v9, /device:TPU:1, one launch (start us, length us, event | category | flops | bytes accessed | tf_op | source)
XLA Modules:
  0.0 77.5 jit_solution(18043078136159205880)
XLA Ops:
  0.0 0.0 copy-start
  0.0 0.0 copy-start.1
  0.0 0.7 broadcast_subtract_fusion
  0.7 0.1 convert_reduce_fusion
  0.9 0.8 %select_reduce_fusion = f32[8,24]{1,0:T(8,128)S(1)} fusion(f32[8,16]{1,0:T(8,128)} %param.10, s32[24]{0:T(128)S(1)} %iota_add_fusion, s32[8,16]{1,0:T(8,128)} %param.9), kind=kLoop, calls=%fused_computation.19 | loop fusion | flops 9024 | bytes 1888 | tf_op jit(solution)/shard_map/reduce_sum | solution.py:54
  1.7 0.0 copy-start.3
  1.7 1.1 %fusion.6 = f32[64,8]{0,1:T(8,128)S(1)} fusion(f32[64,1024]{1,0:T(8,128)} %param.7, s32[1024]{0:T(1024)S(1)} %broadcast_subtract_fusion), kind=kOutput, calls=%fused_computation.22 | convolution fusion | flops 6299648 | bytes 268288 | tf_op jit(solution)/shard_map/dot_general | solution.py:58
  2.9 0.0 copy-done.1
  2.9 0.1 copy-done.3
  2.9 0.0 copy-start.2
  2.9 0.2 fusion.3
  3.1 0.1 copy.16
  3.2 0.5 copy-done.2
  3.7 0.1 convolution_bitcast_fusion.3
  3.8 0.0 copy-done
  3.8 0.2 fusion.2
  4.0 0.1 select_maximum_fusion.4
  4.1 1.3 %collective-permute-start.3 = (f32[64,8]{0,1:T(8,128)S(1)}, f32[64,8]{0,1:T(8,128)S(1)}, u32[]{:S(2)}, u32[]{:S(2)}) collective-permute-start(f32[64,8]{0,1:T(8,128)S(1)} %convolution_bitcast_fusion.3), channel_id=1, source_target_pairs={{2,0},{3,1},{4,2},{5,3},{6,4},{7,5},{8,6},{9,7},{10,8},{11,9},{12,... | collective-permute-start | bytes 6152 | tf_op jit(solution)/shard_map/ppermute | solution.py:14
  5.4 6.4 %collective-permute-start = (f32[64,8]{0,1:T(8,128)S(1)}, f32[64,8]{0,1:T(8,128)S(1)}, u32[]{:S(2)}, u32[]{:S(2)}) collective-permute-start(f32[64,8]{0,1:T(8,128)S(1)} %convolution_bitcast_fusion.3), channel_id=1, source_target_pairs={{0,2},{1,3},{2,4},{3,5},{4,6},{5,7},{6,8},{7,9},{8,10},{9,11},{10,... | collective-permute-start | bytes 6152 | tf_op jit(solution)/shard_map/ppermute | solution.py:14
  11.8 14.2 %collective-permute-start.2 = (f32[80,24]{0,1:T(8,128)S(1)}, f32[80,24]{0,1:T(8,128)S(1)}, u32[]{:S(2)}, u32[]{:S(2)}) collective-permute-start(f32[80,24]{0,1:T(8,128)S(1)} %select_maximum_fusion.4), channel_id=1, source_target_pairs={{1,0},{2,1},{3,2},{4,3},{5,4},{6,5},{7,6},{8,7},{9,8},{10,9},{11,1... | collective-permute-start | bytes 23048 | tf_op jit(solution)/shard_map/ppermute | solution.py:14
  26.0 1.9 %collective-permute-start.1 = (f32[80,24]{0,1:T(8,128)S(1)}, f32[80,24]{0,1:T(8,128)S(1)}, u32[]{:S(2)}, u32[]{:S(2)}) collective-permute-start(f32[80,24]{0,1:T(8,128)S(1)} %select_maximum_fusion.4), channel_id=1, source_target_pairs={{0,1},{1,2},{2,3},{3,4},{4,5},{5,6},{6,7},{7,8},{8,9},{9,10},{10,1... | collective-permute-start | bytes 23048 | tf_op jit(solution)/shard_map/ppermute | solution.py:14
  27.9 0.4 fusion.1
  28.3 0.1 pad_maximum_fusion
  28.4 0.1 copy.17
  28.5 0.0 collective-permute-done
  28.5 0.6 collective-permute-done.1
  29.1 0.1 slice_bitcast_fusion.1
  29.2 0.0 collective-permute-done.2
  29.2 0.1 slice_bitcast_fusion
  29.2 0.1 pad_maximum_fusion.1
  29.3 0.1 slice.71
  29.4 0.1 slice.70
  29.5 0.0 collective-permute-done.3
  29.5 0.3 fusion.7
  29.8 0.2 fusion.15
  30.0 0.2 fusion.44
  30.1 0.3 convolution_add_fusion.1
  30.5 0.4 fusion
  30.9 0.4 multiply_reduce_fusion
  31.3 0.1 stack.27
  31.3 0.1 reduce_sum.107
  31.5 15.4 %all_to_all.12 = f32[16,1,6]{2,1,0:T(1,128)S(1)} all-to-all(f32[16,1,6]{2,1,0:T(1,128)S(1)} %broadcast_in_dim.17), channel_id=1, replica_groups=mesh['curve'=64,'coef'=16] {'coef'}, dimensions={0} | all-to-all | bytes 768 | tf_op jit(solution)/shard_map/all_to_all | solution.py:21
  46.9 29.5 %all_to_all.13 = f32[64,1,6]{2,1,0:T(1,128)S(1)} all-to-all(f32[64,1,6]{2,1,0:T(1,128)S(1)} %broadcast_in_dim.18), channel_id=1, replica_groups=mesh['curve'=64,'coef'=16] {'curve'}, dimensions={0} | all-to-all | bytes 3072 | tf_op jit(solution)/shard_map/all_to_all | solution.py:21
  76.4 0.1 reduce_sum.109
  76.5 0.1 broadcast_in_dim.19
  76.7 0.8 %multiply_add_fusion = f32[64,1024]{1,0:T(8,128)} fusion(f32[64,1024]{1,0:T(8,128)S(1)} %convolution_add_fusion.1, f32[64,1024]{1,0:T(8,128)S(1)} %copy-done.1, f32[]{:T(128)S(1)} %bitcast.132, f32[]{:T(128)S(1)} %bitcast.131), kind=kLoop, calls=%fused_computation.9 | loop fusion | flops 196608 | bytes 786440 | tf_op jit(solution)/shard_map/add | solution.py:121
  (15 shorter events, 0.2 us)
Async XLA Ops:
  0.0 3.8 %copy-start = (f32[64,64]{1,0:T(8,128)S(1)}, f32[64,64]{1,0:T(8,128)}, u32[]{:S(2)}) copy-start(f32[64,64]{1,0:T(8,128)} %param.12) | copy-start | bytes 49156
  0.0 2.9 %copy-start.1 = (f32[64,1024]{1,0:T(8,128)S(1)}, f32[64,1024]{1,0:T(8,128)}, u32[]{:S(2)}) copy-start(f32[64,1024]{1,0:T(8,128)} %param.7) | copy-start | bytes 786436
  1.7 1.2 %copy-start.3 = (f32[1024]{0:T(1024)S(1)}, f32[1024]{0:T(1024)}, u32[]{:S(2)}) copy-start(f32[1024]{0:T(1024)} %param.11) | copy-start | bytes 12292
  2.9 0.8 copy-start.2
  4.1 25.4 %collective-permute-start.3 = (f32[64,8]{0,1:T(8,128)S(1)}, f32[64,8]{0,1:T(8,128)S(1)}, u32[]{:S(2)}, u32[]{:S(2)}) collective-permute-start(f32[64,8]{0,1:T(8,128)S(1)} %convolution_bitcast_fusion.3), channel_id=1, source_target_pairs={{2,0},{3,1},{4,2},{5,3},{6,4},{7,5},{8,6},{9,7},{10,8},{11,9},{12,... | collective-permute-start | bytes 6152 | tf_op jit(solution)/shard_map/ppermute | solution.py:14
  5.4 23.1 %collective-permute-start = (f32[64,8]{0,1:T(8,128)S(1)}, f32[64,8]{0,1:T(8,128)S(1)}, u32[]{:S(2)}, u32[]{:S(2)}) collective-permute-start(f32[64,8]{0,1:T(8,128)S(1)} %convolution_bitcast_fusion.3), channel_id=1, source_target_pairs={{0,2},{1,3},{2,4},{3,5},{4,6},{5,7},{6,8},{7,9},{8,10},{9,11},{10,... | collective-permute-start | bytes 6152 | tf_op jit(solution)/shard_map/ppermute | solution.py:14
  11.8 17.4 %collective-permute-start.2 = (f32[80,24]{0,1:T(8,128)S(1)}, f32[80,24]{0,1:T(8,128)S(1)}, u32[]{:S(2)}, u32[]{:S(2)}) collective-permute-start(f32[80,24]{0,1:T(8,128)S(1)} %select_maximum_fusion.4), channel_id=1, source_target_pairs={{1,0},{2,1},{3,2},{4,3},{5,4},{6,5},{7,6},{8,7},{9,8},{10,9},{11,1... | collective-permute-start | bytes 23048 | tf_op jit(solution)/shard_map/ppermute | solution.py:14
  26.0 3.1 %collective-permute-start.1 = (f32[80,24]{0,1:T(8,128)S(1)}, f32[80,24]{0,1:T(8,128)S(1)}, u32[]{:S(2)}, u32[]{:S(2)}) collective-permute-start(f32[80,24]{0,1:T(8,128)S(1)} %select_maximum_fusion.4), channel_id=1, source_target_pairs={{0,1},{1,2},{2,3},{3,4},{4,5},{5,6},{6,7},{7,8},{8,9},{9,10},{10,1... | collective-permute-start | bytes 23048 | tf_op jit(solution)/shard_map/ppermute | solution.py:14

commit v10 on v6

--- a/solution.py
+++ b/solution.py
@@ -15,7 +15,7 @@
 
 
 def all_sum(value):
-    for axis in ("coef", "curve"):
+    for axis in ("curve", "coef"):
         peers = lax.axis_size(axis)
         spread = jnp.broadcast_to(value[None, :], (peers,) + value.shape)
         value = jnp.sum(lax.all_to_all(spread, axis, 0, 0, tiled=True), axis=0)

time: 72.8 us -> 74.3 us (1.021)
  blocking collectives: 41.5 us -> 43 us
    all_to_all x2, blocking collectives: 41.5 us -> 43 us  [all_sum(): value = jnp.sum(lax.all_to_all(spread, axis, 0, 0, tiled=True), axis=0)]
where the time goes in v10:
time: 74.3 us; the launch traced here: 73.9 us
  blocking collectives  43 us (58%)
  starting transfers between devices  22.8 us (31%)
  matrix products  3.82 us (5%)
  other arithmetic  2.27 us (3%)
  local copies, waits for them, and re-layouts  1.08 us (1%)
  waiting for transfers between devices  0.8 us (1%)
    all_to_all x2, blocking collectives, all_sum(): value = jnp.sum(lax.all_to_all(spread, axis, 0, 0, tiled=True), axis=0)  43 us
    ppermute x4, starting transfers between devices, shifted(): return lax.ppermute(array, axis, pairs)  22.8 us
    dot_general x9, matrix products, on_device(): dot = lambda a, b: jnp.dot(a, b, precision=highest)  3.04 us
  transfers between devices with their start and end apart: 4, of which 1 were waited for; matrix products, arithmetic and copies ran while one was open for 0% of the time, Pallas kernels for 0%

profile of v10, /device:TPU:1, one launch (start us, length us, event | category | flops | bytes accessed | tf_op | source)
XLA Modules:
  0.0 73.9 jit_solution(9515366432847867489)
XLA Ops:
  0.0 0.0 copy-start
  0.0 0.0 copy-start.1
  0.0 0.7 broadcast_subtract_fusion
  0.7 0.1 convert_reduce_fusion
  0.9 0.0 copy-start.3
  0.9 1.2 %fusion.7 = f32[8,64]{1,0:T(8,128)S(1)} fusion(f32[64,1024]{1,0:T(8,128)} %param.7, s32[1024]{0:T(1024)S(1)} %broadcast_subtract_fusion), kind=kOutput, calls=%fused_computation.22 | convolution fusion | flops 6299648 | bytes 268288 | tf_op jit(solution)/shard_map/dot_general | solution.py:57
  2.0 0.0 copy-done.1
  2.0 0.1 copy-done.3
  2.1 0.0 copy-start.4
  2.1 0.0 copy-start.5
  2.1 0.0 copy-start.2
  2.1 0.2 fusion.3
  2.3 0.5 copy-done.4
  2.8 0.0 copy-done.5
  2.8 0.1 select_reduce_fusion
  2.9 0.1 copy.16
  3.0 0.0 copy-done.2
  3.0 0.1 convolution_bitcast_fusion.2
  3.1 0.0 copy-done
  3.1 0.2 fusion.2
  3.3 0.1 select_maximum_fusion.4
  3.4 5.7 %collective-permute-start = (f32[64,8]{0,1:T(8,128)S(1)}, f32[64,8]{0,1:T(8,128)S(1)}, u32[]{:S(2)}, u32[]{:S(2)}) collective-permute-start(f32[64,8]{0,1:T(8,128)S(1)} %convolution_bitcast_fusion.2), channel_id=1, source_target_pairs={{0,2},{1,3},{2,4},{3,5},{4,6},{5,7},{6,8},{7,9},{8,10},{9,11},{10,... | collective-permute-start | bytes 6152 | tf_op jit(solution)/shard_map/ppermute | solution.py:14
  9.2 1.3 %collective-permute-start.3 = (f32[64,8]{0,1:T(8,128)S(1)}, f32[64,8]{0,1:T(8,128)S(1)}, u32[]{:S(2)}, u32[]{:S(2)}) collective-permute-start(f32[64,8]{0,1:T(8,128)S(1)} %convolution_bitcast_fusion.2), channel_id=1, source_target_pairs={{2,0},{3,1},{4,2},{5,3},{6,4},{7,5},{8,6},{9,7},{10,8},{11,9},{12,... | collective-permute-start | bytes 6152 | tf_op jit(solution)/shard_map/ppermute | solution.py:14
  10.5 11.6 %collective-permute-start.2 = (f32[80,24]{0,1:T(8,128)S(1)}, f32[80,24]{0,1:T(8,128)S(1)}, u32[]{:S(2)}, u32[]{:S(2)}) collective-permute-start(f32[80,24]{0,1:T(8,128)S(1)} %select_maximum_fusion.4), channel_id=1, source_target_pairs={{1,0},{2,1},{3,2},{4,3},{5,4},{6,5},{7,6},{8,7},{9,8},{10,9},{11,1... | collective-permute-start | bytes 23048 | tf_op jit(solution)/shard_map/ppermute | solution.py:14
  22.1 4.2 %collective-permute-start.1 = (f32[80,24]{0,1:T(8,128)S(1)}, f32[80,24]{0,1:T(8,128)S(1)}, u32[]{:S(2)}, u32[]{:S(2)}) collective-permute-start(f32[80,24]{0,1:T(8,128)S(1)} %select_maximum_fusion.4), channel_id=1, source_target_pairs={{0,1},{1,2},{2,3},{3,4},{4,5},{5,6},{6,7},{7,8},{8,9},{9,10},{10,1... | collective-permute-start | bytes 23048 | tf_op jit(solution)/shard_map/ppermute | solution.py:14
  26.3 0.0 collective-permute-done
  26.3 0.8 %collective-permute-done.1 = f32[80,24]{0,1:T(8,128)S(1)} collective-permute-done((f32[80,24]{0,1:T(8,128)S(1)}, f32[80,24]{0,1:T(8,128)S(1)}, u32[]{:S(2)}, u32[]{:S(2)}) %collective-permute-start.1) | collective-permute-done | bytes 7712 | tf_op jit(solution)/shard_map/ppermute | solution.py:14
  27.1 0.0 collective-permute-done.2
  27.1 0.1 slice.71
  27.2 0.1 slice.70
  27.2 0.0 collective-permute-done.3
  27.2 0.3 fusion.8
  27.5 0.3 fusion.6
  27.8 0.1 slice_bitcast_fusion
  27.9 0.1 slice_bitcast_fusion.1
  28.0 0.1 pad_maximum_fusion
  28.1 0.2 fusion.20
  28.3 0.1 fusion.49
  28.4 0.4 fusion
  28.8 0.4 fusion.1
  29.2 0.4 multiply_reduce_fusion
  29.6 0.1 stack.27
  29.7 0.1 reduce_sum.107
  29.9 26.4 %all_to_all.12 = f32[64,1,6]{2,1,0:T(1,128)S(1)} all-to-all(f32[64,1,6]{2,1,0:T(1,128)S(1)} %broadcast_in_dim.17), channel_id=1, replica_groups=mesh['curve'=64,'coef'=16] {'curve'}, dimensions={0} | all-to-all | bytes 3072 | tf_op jit(solution)/shard_map/all_to_all | solution.py:21
  56.2 0.1 reduce_sum.108
  56.3 16.6 %all_to_all.13 = f32[16,1,6]{2,1,0:T(1,128)S(1)} all-to-all(f32[16,1,6]{2,1,0:T(1,128)S(1)} %broadcast_in_dim.18), channel_id=1, replica_groups=mesh['curve'=64,'coef'=16] {'coef'}, dimensions={0} | all-to-all | bytes 768 | tf_op jit(solution)/shard_map/all_to_all | solution.py:21
  72.9 0.1 broadcast_in_dim.19
  73.1 0.8 %multiply_add_fusion = f32[64,1024]{1,0:T(8,128)} fusion(f32[64,1024]{1,0:T(8,128)S(1)} %fusion, f32[64,1024]{1,0:T(8,128)S(1)} %copy-done.1, f32[]{:T(128)S(1)} %bitcast.128, f32[]{:T(128)S(1)} %bitcast.127), kind=kLoop, calls=%fused_computation.8 | loop fusion | flops 196608 | bytes 786440 | tf_op jit(solution)/shard_map/add | solution.py:120
  (15 shorter events, 0.2 us)
Async XLA Ops:
  0.0 3.1 %copy-start = (f32[64,64]{1,0:T(8,128)S(1)}, f32[64,64]{1,0:T(8,128)}, u32[]{:S(2)}) copy-start(f32[64,64]{1,0:T(8,128)} %param.12) | copy-start | bytes 49156
  0.0 2.0 %copy-start.1 = (f32[64,1024]{1,0:T(8,128)S(1)}, f32[64,1024]{1,0:T(8,128)}, u32[]{:S(2)}) copy-start(f32[64,1024]{1,0:T(8,128)} %param.7) | copy-start | bytes 786436
  0.9 1.2 %copy-start.3 = (f32[1024]{0:T(1024)S(1)}, f32[1024]{0:T(1024)}, u32[]{:S(2)}) copy-start(f32[1024]{0:T(1024)} %param.11) | copy-start | bytes 12292
  2.1 0.7 copy-start.4
  2.1 0.7 copy-start.5
  2.1 0.9 %copy-start.2 = (f32[64,64]{1,0:T(8,128)S(1)}, f32[64,64]{1,0:T(8,128)}, u32[]{:S(2)}) copy-start(f32[64,64]{1,0:T(8,128)} %param.13) | copy-start | bytes 49156
  3.4 22.8 %collective-permute-start = (f32[64,8]{0,1:T(8,128)S(1)}, f32[64,8]{0,1:T(8,128)S(1)}, u32[]{:S(2)}, u32[]{:S(2)}) collective-permute-start(f32[64,8]{0,1:T(8,128)S(1)} %convolution_bitcast_fusion.2), channel_id=1, source_target_pairs={{0,2},{1,3},{2,4},{3,5},{4,6},{5,7},{6,8},{7,9},{8,10},{9,11},{10,... | collective-permute-start | bytes 6152 | tf_op jit(solution)/shard_map/ppermute | solution.py:14
  9.2 18.1 %collective-permute-start.3 = (f32[64,8]{0,1:T(8,128)S(1)}, f32[64,8]{0,1:T(8,128)S(1)}, u32[]{:S(2)}, u32[]{:S(2)}) collective-permute-start(f32[64,8]{0,1:T(8,128)S(1)} %convolution_bitcast_fusion.2), channel_id=1, source_target_pairs={{2,0},{3,1},{4,2},{5,3},{6,4},{7,5},{8,6},{9,7},{10,8},{11,9},{12,... | collective-permute-start | bytes 6152 | tf_op jit(solution)/shard_map/ppermute | solution.py:14
  10.5 16.6 %collective-permute-start.2 = (f32[80,24]{0,1:T(8,128)S(1)}, f32[80,24]{0,1:T(8,128)S(1)}, u32[]{:S(2)}, u32[]{:S(2)}) collective-permute-start(f32[80,24]{0,1:T(8,128)S(1)} %select_maximum_fusion.4), channel_id=1, source_target_pairs={{1,0},{2,1},{3,2},{4,3},{5,4},{6,5},{7,6},{8,7},{9,8},{10,9},{11,1... | collective-permute-start | bytes 23048 | tf_op jit(solution)/shard_map/ppermute | solution.py:14
  22.1 5.0 %collective-permute-start.1 = (f32[80,24]{0,1:T(8,128)S(1)}, f32[80,24]{0,1:T(8,128)S(1)}, u32[]{:S(2)}, u32[]{:S(2)}) collective-permute-start(f32[80,24]{0,1:T(8,128)S(1)} %select_maximum_fusion.4), channel_id=1, source_target_pairs={{0,1},{1,2},{2,3},{3,4},{4,5},{5,6},{6,7},{7,8},{8,9},{9,10},{10,1... | collective-permute-start | bytes 23048 | tf_op jit(solution)/shard_map/ppermute | solution.py:14

commit v11 on v6

--- a/solution.py
+++ b/solution.py
@@ -55,8 +55,17 @@
     counts = jnp.sum(slot_table, axis=1)
     highest = lax.Precision.HIGHEST
     dot = lambda a, b: jnp.dot(a, b, precision=highest)
-    moments = dot(right_side, slot_table.T)
-    own_part = dot(right_side * self_diag[None, :], slot_table.T) + dot(self_trans, moments)
+    fields = jnp.concatenate([right_side, right_side * self_diag[None, :]], axis=0)
+    high = fields.astype(jnp.bfloat16)
+    rest = fields - high.astype(jnp.float32)
+    middle = rest.astype(jnp.bfloat16)
+    low = (rest - middle.astype(jnp.float32)).astype(jnp.bfloat16)
+    parts = jnp.concatenate([high, middle, low], axis=0)
+    sums = jnp.dot(parts, slot_table.T.astype(jnp.bfloat16), preferred_element_type=jnp.float32)
+    sums = sums.reshape((3,) + fields.shape[:1] + sums.shape[1:]).sum(axis=0)
+    rows = right_side.shape[0]
+    moments = sums[:rows]
+    own_part = sums[rows:] + dot(self_trans, moments)
     moments = dot(far_trans, moments)
     g = group_count
     filler = jnp.zeros((g, g), jnp.float32)
@@ -68,7 +77,6 @@
         ],
         axis=0,
     )
-    rows = moments.shape[0]
     payload, moments = lax.optimization_barrier((payload, moments))
     below = shifted(payload, DEVICES, 1)
     above = shifted(payload, DEVICES, -1)

time: 72.8 us -> 71.4 us (0.981)
  starting transfers between devices: 22.8 us -> 19.9 us
  waiting for transfers between devices: 0.8 us -> 2.96 us
  matrix products: 3.82 us -> 2.99 us
    ppermute x4, starting transfers between devices: 22.8 us -> 19.9 us  [shifted(): return lax.ppermute(array, axis, pairs)]
    ppermute x4, waiting for transfers between devices: 0.8 us -> 2.96 us  [shifted(): return lax.ppermute(array, axis, pairs)]
    dot_general x9 -> x7, matrix products: 3.04 us -> 1.67 us  [on_device(): dot = lambda a, b: jnp.dot(a, b, precision=highest)]
    mul x0 -> x1, other arithmetic: none -> 1.04 us  [local_part(): self_diag[None, :] * field + jnp.dot(self_trans, field, precision=highest)]
    sub x1, other arithmetic: 0.74 us -> 0.01 us  [on_device(): slots = group_ids - base_group]
where the time goes in v11:
time: 71.4 us; the launch traced here: 71.1 us
  blocking collectives  40.8 us (57%)
  starting transfers between devices  19.9 us (28%)
  matrix products  2.99 us (4%)
  waiting for transfers between devices  2.96 us (4%)
  other arithmetic  2.68 us (4%)
  local copies, waits for them, and re-layouts  1.42 us (2%)
    all_to_all x2, blocking collectives, all_sum(): value = jnp.sum(lax.all_to_all(spread, axis, 0, 0, tiled=True), axis=0)  40.8 us
    ppermute x4, starting transfers between devices, shifted(): return lax.ppermute(array, axis, pairs)  19.9 us
    ppermute x4, waiting for transfers between devices, shifted(): return lax.ppermute(array, axis, pairs)  2.96 us
    dot_general x7, matrix products, on_device(): dot = lambda a, b: jnp.dot(a, b, precision=highest)  1.67 us
  transfers between devices with their start and end apart: 4, of which 1 were waited for; matrix products, arithmetic and copies ran while one was open for 0% of the time, Pallas kernels for 0%

profile of v11, /device:TPU:1, one launch (start us, length us, event | category | flops | bytes accessed | tf_op | source)
XLA Modules:
  0.0 71.1 jit_solution(588247494651758170)
XLA Ops:
  0.0 0.0 copy-start
  0.0 0.0 copy-start.1
  0.0 1.0 %broadcast_multiply_fusion = f32[64,1024]{1,0:T(8,128)S(1)} fusion(f32[64,1024]{1,0:T(8,128)} %param.7, f32[1024]{0:T(1024)} %param.11), kind=kLoop, calls=%fused_computation.30 | loop fusion | flops 65536 | bytes 528384 | tf_op jit(solution)/shard_map/mul | solution.py:27
  1.1 0.0 copy-done.1
  1.1 0.1 fusion.10
  1.2 0.0 copy-start.6
  1.2 0.6 copy-done.6
  1.8 0.1 convert_reduce_fusion
  2.0 0.0 copy-start.2
  2.0 0.0 copy-start.4
  2.0 0.0 copy-start.5
  2.0 0.6 fusion.2
  2.6 0.2 copy-done.2
  2.7 0.1 convolution_bitcast_fusion.3
  2.9 0.0 copy-done
  2.9 0.2 fusion.3
  3.0 0.0 copy-done.4
  3.1 0.0 copy-done.5
  3.1 0.1 select_reduce_fusion
  3.2 0.1 copy.16
  3.3 0.1 select_maximum_fusion.4
  3.4 5.7 %collective-permute-start = (f32[64,8]{0,1:T(8,128)S(1)}, f32[64,8]{0,1:T(8,128)S(1)}, u32[]{:S(2)}, u32[]{:S(2)}) collective-permute-start(f32[64,8]{0,1:T(8,128)S(1)} %convolution_bitcast_fusion.3), channel_id=1, source_target_pairs={{0,2},{1,3},{2,4},{3,5},{4,6},{5,7},{6,8},{7,9},{8,10},{9,11},{10,... | collective-permute-start | bytes 6152 | tf_op jit(solution)/shard_map/ppermute | solution.py:14
  9.1 5.8 %collective-permute-start.1 = (f32[80,24]{0,1:T(8,128)S(1)}, f32[80,24]{0,1:T(8,128)S(1)}, u32[]{:S(2)}, u32[]{:S(2)}) collective-permute-start(f32[80,24]{0,1:T(8,128)S(1)} %select_maximum_fusion.4), channel_id=1, source_target_pairs={{0,1},{1,2},{2,3},{3,4},{4,5},{5,6},{6,7},{7,8},{8,9},{9,10},{10,1... | collective-permute-start | bytes 23048 | tf_op jit(solution)/shard_map/ppermute | solution.py:14
  14.9 7.2 %collective-permute-start.2 = (f32[80,24]{0,1:T(8,128)S(1)}, f32[80,24]{0,1:T(8,128)S(1)}, u32[]{:S(2)}, u32[]{:S(2)}) collective-permute-start(f32[80,24]{0,1:T(8,128)S(1)} %select_maximum_fusion.4), channel_id=1, source_target_pairs={{1,0},{2,1},{3,2},{4,3},{5,4},{6,5},{7,6},{8,7},{9,8},{10,9},{11,1... | collective-permute-start | bytes 23048 | tf_op jit(solution)/shard_map/ppermute | solution.py:14
  22.0 1.3 %collective-permute-start.3 = (f32[64,8]{0,1:T(8,128)S(1)}, f32[64,8]{0,1:T(8,128)S(1)}, u32[]{:S(2)}, u32[]{:S(2)}) collective-permute-start(f32[64,8]{0,1:T(8,128)S(1)} %convolution_bitcast_fusion.3), channel_id=1, source_target_pairs={{2,0},{3,1},{4,2},{5,3},{6,4},{7,5},{8,6},{9,7},{10,8},{11,9},{12,... | collective-permute-start | bytes 6152 | tf_op jit(solution)/shard_map/ppermute | solution.py:14
  23.3 0.0 collective-permute-done
  23.4 0.0 collective-permute-done.1
  23.4 0.0 collective-permute-done.2
  23.4 0.0 copy-start.3
  23.4 0.1 slice.78
  23.5 0.1 slice.79
  23.6 3.0 %collective-permute-done.3 = f32[64,8]{0,1:T(8,128)S(1)} collective-permute-done((f32[64,8]{0,1:T(8,128)S(1)}, f32[64,8]{0,1:T(8,128)S(1)}, u32[]{:S(2)}, u32[]{:S(2)}) %collective-permute-start.3) | collective-permute-done | bytes 2080 | tf_op jit(solution)/shard_map/ppermute | solution.py:14
  26.5 0.3 fusion.13
  26.8 0.3 fusion.12
  27.1 0.1 slice_bitcast_fusion
  27.2 0.1 slice_bitcast_fusion.1
  27.3 0.1 pad_maximum_fusion.1
  27.4 0.2 fusion.23
  27.6 0.1 fusion.55
  27.7 0.0 copy-done.3
  27.7 0.4 fusion
  28.1 0.4 fusion.1
  28.5 0.4 multiply_reduce_fusion
  28.9 0.1 stack.27
  29.0 0.1 reduce_sum.117
  29.1 17.0 %all_to_all.12 = f32[16,1,6]{2,1,0:T(1,128)S(1)} all-to-all(f32[16,1,6]{2,1,0:T(1,128)S(1)} %broadcast_in_dim.17), channel_id=1, replica_groups=mesh['curve'=64,'coef'=16] {'coef'}, dimensions={0} | all-to-all | bytes 768 | tf_op jit(solution)/shard_map/all_to_all | solution.py:21
  46.1 23.9 %all_to_all.13 = f32[64,1,6]{2,1,0:T(1,128)S(1)} all-to-all(f32[64,1,6]{2,1,0:T(1,128)S(1)} %broadcast_in_dim.18), channel_id=1, replica_groups=mesh['curve'=64,'coef'=16] {'curve'}, dimensions={0} | all-to-all | bytes 3072 | tf_op jit(solution)/shard_map/all_to_all | solution.py:21
  70.0 0.1 reduce_sum.119
  70.1 0.1 broadcast_in_dim.19
  70.3 0.8 %multiply_add_fusion = f32[64,1024]{1,0:T(8,128)} fusion(f32[64,1024]{1,0:T(8,128)S(1)} %fusion, f32[64,1024]{1,0:T(8,128)S(1)} %copy-done.1, f32[]{:T(128)S(1)} %bitcast.129, f32[]{:T(128)S(1)} %bitcast.128), kind=kLoop, calls=%fused_computation.22 | loop fusion | flops 196608 | bytes 786440 | tf_op jit(solution)/shard_map/add | solution.py:128
  (17 shorter events, 0.2 us)
Async XLA Ops:
  0.0 2.9 %copy-start = (f32[64,64]{1,0:T(8,128)S(1)}, f32[64,64]{1,0:T(8,128)}, u32[]{:S(2)}) copy-start(f32[64,64]{1,0:T(8,128)} %param.12) | copy-start | bytes 49156
  0.0 1.1 %copy-start.1 = (f32[64,1024]{1,0:T(8,128)S(1)}, f32[64,1024]{1,0:T(8,128)}, u32[]{:S(2)}) copy-start(f32[64,1024]{1,0:T(8,128)} %param.7) | copy-start | bytes 786436
  1.2 0.7 copy-start.6
  2.0 0.8 %copy-start.2 = (f32[64,64]{1,0:T(8,128)S(1)}, f32[64,64]{1,0:T(8,128)}, u32[]{:S(2)}) copy-start(f32[64,64]{1,0:T(8,128)} %param.13) | copy-start | bytes 49156
  2.0 1.1 %copy-start.4 = (f32[8,16]{1,0:T(8,128)S(1)}, f32[8,16]{1,0:T(8,128)}, u32[]{:S(2)}) copy-start(f32[8,16]{1,0:T(8,128)} %param.10) | copy-start | bytes 1540
  2.0 1.1 %copy-start.5 = (s32[8,16]{1,0:T(8,128)S(1)}, s32[8,16]{1,0:T(8,128)}, u32[]{:S(2)}) copy-start(s32[8,16]{1,0:T(8,128)} %param.9) | copy-start | bytes 1540
  3.4 20.0 %collective-permute-start = (f32[64,8]{0,1:T(8,128)S(1)}, f32[64,8]{0,1:T(8,128)S(1)}, u32[]{:S(2)}, u32[]{:S(2)}) collective-permute-start(f32[64,8]{0,1:T(8,128)S(1)} %convolution_bitcast_fusion.3), channel_id=1, source_target_pairs={{0,2},{1,3},{2,4},{3,5},{4,6},{5,7},{6,8},{7,9},{8,10},{9,11},{10,... | collective-permute-start | bytes 6152 | tf_op jit(solution)/shard_map/ppermute | solution.py:14
  9.1 14.2 %collective-permute-start.1 = (f32[80,24]{0,1:T(8,128)S(1)}, f32[80,24]{0,1:T(8,128)S(1)}, u32[]{:S(2)}, u32[]{:S(2)}) collective-permute-start(f32[80,24]{0,1:T(8,128)S(1)} %select_maximum_fusion.4), channel_id=1, source_target_pairs={{0,1},{1,2},{2,3},{3,4},{4,5},{5,6},{6,7},{7,8},{8,9},{9,10},{10,1... | collective-permute-start | bytes 23048 | tf_op jit(solution)/shard_map/ppermute | solution.py:14
  14.9 8.5 %collective-permute-start.2 = (f32[80,24]{0,1:T(8,128)S(1)}, f32[80,24]{0,1:T(8,128)S(1)}, u32[]{:S(2)}, u32[]{:S(2)}) collective-permute-start(f32[80,24]{0,1:T(8,128)S(1)} %select_maximum_fusion.4), channel_id=1, source_target_pairs={{1,0},{2,1},{3,2},{4,3},{5,4},{6,5},{7,6},{8,7},{9,8},{10,9},{11,1... | collective-permute-start | bytes 23048 | tf_op jit(solution)/shard_map/ppermute | solution.py:14
  22.0 4.5 %collective-permute-start.3 = (f32[64,8]{0,1:T(8,128)S(1)}, f32[64,8]{0,1:T(8,128)S(1)}, u32[]{:S(2)}, u32[]{:S(2)}) collective-permute-start(f32[64,8]{0,1:T(8,128)S(1)} %convolution_bitcast_fusion.3), channel_id=1, source_target_pairs={{2,0},{3,1},{4,2},{5,3},{6,4},{7,5},{8,6},{9,7},{10,8},{11,9},{12,... | collective-permute-start | bytes 6152 | tf_op jit(solution)/shard_map/ppermute | solution.py:14
  23.4 4.3 %copy-start.3 = (f32[1024]{0:T(1024)S(1)}, f32[1024]{0:T(1024)}, u32[]{:S(2)}) copy-start(f32[1024]{0:T(1024)} %param.11) | copy-start | bytes 12292

commit v12 on v11

--- a/solution.py
+++ b/solution.py
@@ -56,11 +56,12 @@
     highest = lax.Precision.HIGHEST
     dot = lambda a, b: jnp.dot(a, b, precision=highest)
     fields = jnp.concatenate([right_side, right_side * self_diag[None, :]], axis=0)
-    high = fields.astype(jnp.bfloat16)
-    rest = fields - high.astype(jnp.float32)
-    middle = rest.astype(jnp.bfloat16)
-    low = (rest - middle.astype(jnp.float32)).astype(jnp.bfloat16)
-    parts = jnp.concatenate([high, middle, low], axis=0)
+    to_bf16 = lambda x: lax.reduce_precision(x, exponent_bits=8, mantissa_bits=7)
+    high = to_bf16(fields)
+    rest = fields - high
+    middle = to_bf16(rest)
+    low = rest - middle
+    parts = jnp.concatenate([high, middle, low], axis=0).astype(jnp.bfloat16)
     sums = jnp.dot(parts, slot_table.T.astype(jnp.bfloat16), preferred_element_type=jnp.float32)
     sums = sums.reshape((3,) + fields.shape[:1] + sums.shape[1:]).sum(axis=0)
     rows = right_side.shape[0]

time: 71.4 us -> 73.4 us (1.028)
  blocking collectives: 40.8 us -> 42.4 us
    all_to_all x2, blocking collectives: 40.8 us -> 42.4 us  [all_sum(): value = jnp.sum(lax.all_to_all(spread, axis, 0, 0, tiled=True), axis=0)]
where the time goes in v12:
time: 73.4 us; the launch traced here: 73.1 us
  blocking collectives  42.4 us (58%)
  starting transfers between devices  20.6 us (28%)
  matrix products  2.99 us (4%)
  waiting for transfers between devices  2.83 us (4%)
  other arithmetic  2.7 us (4%)
  local copies, waits for them, and re-layouts  1.32 us (2%)
    all_to_all x2, blocking collectives, all_sum(): value = jnp.sum(lax.all_to_all(spread, axis, 0, 0, tiled=True), axis=0)  42.4 us
    ppermute x4, starting transfers between devices, shifted(): return lax.ppermute(array, axis, pairs)  20.6 us
    ppermute x4, waiting for transfers between devices, shifted(): return lax.ppermute(array, axis, pairs)  2.83 us
    dot_general x7, matrix products, on_device(): dot = lambda a, b: jnp.dot(a, b, precision=highest)  1.67 us
  transfers between devices with their start and end apart: 4, of which 1 were waited for; matrix products, arithmetic and copies ran while one was open for 0% of the time, Pallas kernels for 0%

profile of v12, /device:TPU:1, one launch (start us, length us, event | category | flops | bytes accessed | tf_op | source)
XLA Modules:
  0.0 73.1 jit_solution(6712258905977849667)
XLA Ops:
  0.0 0.0 copy-start
  0.0 0.0 copy-start.1
  0.0 1.0 %broadcast_multiply_fusion = f32[64,1024]{1,0:T(8,128)S(1)} fusion(f32[64,1024]{1,0:T(8,128)} %param.7, f32[1024]{0:T(1024)} %param.11), kind=kLoop, calls=%fused_computation.31 | loop fusion | flops 65536 | bytes 528384 | tf_op jit(solution)/shard_map/mul | solution.py:27
  1.1 0.0 copy-done.1
  1.1 0.0 copy-start.6
  1.1 0.1 reduce-precision_convert_fusion.1
  1.2 0.5 copy-done.6
  1.8 0.1 convert_reduce_fusion
  1.9 0.0 copy-start.2
  1.9 0.0 copy-start.4
  1.9 0.0 copy-start.5
  1.9 0.6 fusion.2
  2.5 0.2 copy-done.2
  2.6 0.1 convolution_bitcast_fusion.3
  2.8 0.0 copy-done
  2.8 0.2 fusion.3
  2.9 0.0 copy-done.4
  3.0 0.0 copy-done.5
  3.0 0.1 select_reduce_fusion
  3.1 0.1 copy.16
  3.2 0.1 select_maximum_fusion.4
  3.3 5.7 %collective-permute-start = (f32[64,8]{0,1:T(8,128)S(1)}, f32[64,8]{0,1:T(8,128)S(1)}, u32[]{:S(2)}, u32[]{:S(2)}) collective-permute-start(f32[64,8]{0,1:T(8,128)S(1)} %convolution_bitcast_fusion.3), channel_id=1, source_target_pairs={{0,2},{1,3},{2,4},{3,5},{4,6},{5,7},{6,8},{7,9},{8,10},{9,11},{10,... | collective-permute-start | bytes 6152 | tf_op jit(solution)/shard_map/ppermute | solution.py:14
  9.0 11.6 %collective-permute-start.2 = (f32[80,24]{0,1:T(8,128)S(1)}, f32[80,24]{0,1:T(8,128)S(1)}, u32[]{:S(2)}, u32[]{:S(2)}) collective-permute-start(f32[80,24]{0,1:T(8,128)S(1)} %select_maximum_fusion.4), channel_id=1, source_target_pairs={{1,0},{2,1},{3,2},{4,3},{5,4},{6,5},{7,6},{8,7},{9,8},{10,9},{11,1... | collective-permute-start | bytes 23048 | tf_op jit(solution)/shard_map/ppermute | solution.py:14
  20.6 1.9 %collective-permute-start.1 = (f32[80,24]{0,1:T(8,128)S(1)}, f32[80,24]{0,1:T(8,128)S(1)}, u32[]{:S(2)}, u32[]{:S(2)}) collective-permute-start(f32[80,24]{0,1:T(8,128)S(1)} %select_maximum_fusion.4), channel_id=1, source_target_pairs={{0,1},{1,2},{2,3},{3,4},{4,5},{5,6},{6,7},{7,8},{8,9},{9,10},{10,1... | collective-permute-start | bytes 23048 | tf_op jit(solution)/shard_map/ppermute | solution.py:14
  22.6 1.3 %collective-permute-start.3 = (f32[64,8]{0,1:T(8,128)S(1)}, f32[64,8]{0,1:T(8,128)S(1)}, u32[]{:S(2)}, u32[]{:S(2)}) collective-permute-start(f32[64,8]{0,1:T(8,128)S(1)} %convolution_bitcast_fusion.3), channel_id=1, source_target_pairs={{2,0},{3,1},{4,2},{5,3},{6,4},{7,5},{8,6},{9,7},{10,8},{11,9},{12,... | collective-permute-start | bytes 6152 | tf_op jit(solution)/shard_map/ppermute | solution.py:14
  23.9 0.0 collective-permute-done
  23.9 0.0 collective-permute-done.1
  23.9 0.0 collective-permute-done.2
  23.9 0.0 copy-start.3
  24.0 0.1 slice.78
  24.0 0.1 slice.79
  24.1 2.8 %collective-permute-done.3 = f32[64,8]{0,1:T(8,128)S(1)} collective-permute-done((f32[64,8]{0,1:T(8,128)S(1)}, f32[64,8]{0,1:T(8,128)S(1)}, u32[]{:S(2)}, u32[]{:S(2)}) %collective-permute-start.3) | collective-permute-done | bytes 2080 | tf_op jit(solution)/shard_map/ppermute | solution.py:14
  26.9 0.3 fusion.12
  27.2 0.3 fusion.11
  27.5 0.1 slice_bitcast_fusion
  27.6 0.1 slice_bitcast_fusion.1
  27.7 0.1 pad_maximum_fusion.1
  27.8 0.2 fusion.22
  28.0 0.1 fusion.54
  28.1 0.0 copy-done.3
  28.1 0.4 fusion
  28.5 0.4 fusion.1
  28.9 0.4 multiply_reduce_fusion
  29.3 0.1 stack.27
  29.4 0.1 reduce_sum.117
  29.5 16.9 %all_to_all.12 = f32[16,1,6]{2,1,0:T(1,128)S(1)} all-to-all(f32[16,1,6]{2,1,0:T(1,128)S(1)} %broadcast_in_dim.17), channel_id=1, replica_groups=mesh['curve'=64,'coef'=16] {'coef'}, dimensions={0} | all-to-all | bytes 768 | tf_op jit(solution)/shard_map/all_to_all | solution.py:21
  46.5 25.5 %all_to_all.13 = f32[64,1,6]{2,1,0:T(1,128)S(1)} all-to-all(f32[64,1,6]{2,1,0:T(1,128)S(1)} %broadcast_in_dim.18), channel_id=1, replica_groups=mesh['curve'=64,'coef'=16] {'curve'}, dimensions={0} | all-to-all | bytes 3072 | tf_op jit(solution)/shard_map/all_to_all | solution.py:21
  72.0 0.1 reduce_sum.119
  72.1 0.1 broadcast_in_dim.19
  72.3 0.8 %multiply_add_fusion = f32[64,1024]{1,0:T(8,128)} fusion(f32[64,1024]{1,0:T(8,128)S(1)} %fusion, f32[64,1024]{1,0:T(8,128)S(1)} %copy-done.1, f32[]{:T(128)S(1)} %bitcast.129, f32[]{:T(128)S(1)} %bitcast.128), kind=kLoop, calls=%fused_computation.23 | loop fusion | flops 196608 | bytes 786440 | tf_op jit(solution)/shard_map/add | solution.py:129
  (16 shorter events, 0.2 us)
Async XLA Ops:
  0.0 2.8 %copy-start = (f32[64,64]{1,0:T(8,128)S(1)}, f32[64,64]{1,0:T(8,128)}, u32[]{:S(2)}) copy-start(f32[64,64]{1,0:T(8,128)} %param.12) | copy-start | bytes 49156
  0.0 1.1 %copy-start.1 = (f32[64,1024]{1,0:T(8,128)S(1)}, f32[64,1024]{1,0:T(8,128)}, u32[]{:S(2)}) copy-start(f32[64,1024]{1,0:T(8,128)} %param.7) | copy-start | bytes 786436
  1.1 0.7 copy-start.6
  1.9 0.8 %copy-start.2 = (f32[64,64]{1,0:T(8,128)S(1)}, f32[64,64]{1,0:T(8,128)}, u32[]{:S(2)}) copy-start(f32[64,64]{1,0:T(8,128)} %param.13) | copy-start | bytes 49156
  1.9 1.1 %copy-start.4 = (f32[8,16]{1,0:T(8,128)S(1)}, f32[8,16]{1,0:T(8,128)}, u32[]{:S(2)}) copy-start(f32[8,16]{1,0:T(8,128)} %param.10) | copy-start | bytes 1540
  1.9 1.1 %copy-start.5 = (s32[8,16]{1,0:T(8,128)S(1)}, s32[8,16]{1,0:T(8,128)}, u32[]{:S(2)}) copy-start(s32[8,16]{1,0:T(8,128)} %param.9) | copy-start | bytes 1540
  3.3 20.6 %collective-permute-start = (f32[64,8]{0,1:T(8,128)S(1)}, f32[64,8]{0,1:T(8,128)S(1)}, u32[]{:S(2)}, u32[]{:S(2)}) collective-permute-start(f32[64,8]{0,1:T(8,128)S(1)} %convolution_bitcast_fusion.3), channel_id=1, source_target_pairs={{0,2},{1,3},{2,4},{3,5},{4,6},{5,7},{6,8},{7,9},{8,10},{9,11},{10,... | collective-permute-start | bytes 6152 | tf_op jit(solution)/shard_map/ppermute | solution.py:14
  9.0 14.9 %collective-permute-start.2 = (f32[80,24]{0,1:T(8,128)S(1)}, f32[80,24]{0,1:T(8,128)S(1)}, u32[]{:S(2)}, u32[]{:S(2)}) collective-permute-start(f32[80,24]{0,1:T(8,128)S(1)} %select_maximum_fusion.4), channel_id=1, source_target_pairs={{1,0},{2,1},{3,2},{4,3},{5,4},{6,5},{7,6},{8,7},{9,8},{10,9},{11,1... | collective-permute-start | bytes 23048 | tf_op jit(solution)/shard_map/ppermute | solution.py:14
  20.6 3.3 %collective-permute-start.1 = (f32[80,24]{0,1:T(8,128)S(1)}, f32[80,24]{0,1:T(8,128)S(1)}, u32[]{:S(2)}, u32[]{:S(2)}) collective-permute-start(f32[80,24]{0,1:T(8,128)S(1)} %select_maximum_fusion.4), channel_id=1, source_target_pairs={{0,1},{1,2},{2,3},{3,4},{4,5},{5,6},{6,7},{7,8},{8,9},{9,10},{10,1... | collective-permute-start | bytes 23048 | tf_op jit(solution)/shard_map/ppermute | solution.py:14
  22.6 4.4 %collective-permute-start.3 = (f32[64,8]{0,1:T(8,128)S(1)}, f32[64,8]{0,1:T(8,128)S(1)}, u32[]{:S(2)}, u32[]{:S(2)}) collective-permute-start(f32[64,8]{0,1:T(8,128)S(1)} %convolution_bitcast_fusion.3), channel_id=1, source_target_pairs={{2,0},{3,1},{4,2},{5,3},{6,4},{7,5},{8,6},{9,7},{10,8},{11,9},{12,... | collective-permute-start | bytes 6152 | tf_op jit(solution)/shard_map/ppermute | solution.py:14
  23.9 4.2 %copy-start.3 = (f32[1024]{0:T(1024)S(1)}, f32[1024]{0:T(1024)}, u32[]{:S(2)}) copy-start(f32[1024]{0:T(1024)} %param.11) | copy-start | bytes 12292

commit v13 on v6

--- a/solution.py
+++ b/solution.py
@@ -55,8 +55,9 @@
     counts = jnp.sum(slot_table, axis=1)
     highest = lax.Precision.HIGHEST
     dot = lambda a, b: jnp.dot(a, b, precision=highest)
-    moments = dot(right_side, slot_table.T)
-    own_part = dot(right_side * self_diag[None, :], slot_table.T) + dot(self_trans, moments)
+    onehot = lambda a, b: jnp.dot(a, b, precision=lax.Precision.HIGH)
+    moments = onehot(right_side, slot_table.T)
+    own_part = onehot(right_side * self_diag[None, :], slot_table.T) + dot(self_trans, moments)
     moments = dot(far_trans, moments)
     g = group_count
     filler = jnp.zeros((g, g), jnp.float32)
@@ -95,9 +96,9 @@
     near_counts = jnp.concatenate([counts_below, counts, counts_above])
     near_part = jnp.concatenate([part_below, own_part, part_above], axis=1)
     near_moments = near_part + near_counts[None, :] * local_near
-    first = local_part(right_side, self_diag, self_trans) + dot(local_near[:, g : 2 * g], slot_table)
+    first = local_part(right_side, self_diag, self_trans) + onehot(local_near[:, g : 2 * g], slot_table)
     local_next = dot(far_trans, dot(near_moments, select_mat.T))
-    second = local_part(first, self_diag, self_trans) + dot(local_next, slot_table)
+    second = local_part(first, self_diag, self_trans) + onehot(local_next, slot_table)
     krylov = (right_side, first, second)
     columns_sums = jnp.stack([jnp.sum(krylov[i] * krylov[j], axis=0) for i, j in GRAM_PAIRS])
     partials = jnp.sum(columns_sums, axis=1)

time: 72.8 us -> 72.7 us (level)
    dot_general x9 -> x5, matrix products: 3.04 us -> 0.95 us  [on_device(): dot = lambda a, b: jnp.dot(a, b, precision=highest)]
    dot_general x0 -> x4, matrix products: none -> 1.96 us  [on_device(): onehot = lambda a, b: jnp.dot(a, b, precision=lax.Precision.HIGH)]
where the time goes in v13:
time: 72.7 us; the launch traced here: 72.3 us
  blocking collectives  41.5 us (57%)
  starting transfers between devices  22.8 us (31%)
  matrix products  3.69 us (5%)
  other arithmetic  2.27 us (3%)
  local copies, waits for them, and re-layouts  1.06 us (1%)
  waiting for transfers between devices  0.8 us (1%)
    all_to_all x2, blocking collectives, all_sum(): value = jnp.sum(lax.all_to_all(spread, axis, 0, 0, tiled=True), axis=0)  41.5 us
    ppermute x4, starting transfers between devices, shifted(): return lax.ppermute(array, axis, pairs)  22.8 us
    dot_general x4, matrix products, on_device(): onehot = lambda a, b: jnp.dot(a, b, precision=lax.Precision.HIGH)  1.96 us
  transfers between devices with their start and end apart: 4, of which 1 were waited for; matrix products, arithmetic and copies ran while one was open for 0% of the time, Pallas kernels for 0%

profile of v13, /device:TPU:1, one launch (start us, length us, event | category | flops | bytes accessed | tf_op | source)
XLA Modules:
  0.0 72.3 jit_solution(763352625629191848)
XLA Ops:
  0.0 0.0 copy-start
  0.0 0.0 copy-start.1
  0.0 0.7 %broadcast_subtract_fusion = s32[1024]{0:T(1024)S(1)} fusion(s32[1024]{0:T(1024)} %param.8, s32[]{:T(128)S(6)} %mul.152), kind=kLoop, calls=%fused_computation.60 | loop fusion | flops 1024 | bytes 8196 | tf_op jit(solution)/shard_map/sub | solution.py:48
  0.7 0.1 convert_reduce_fusion
  0.9 0.0 copy-start.3
  0.9 1.1 %fusion.7 = f32[8,64]{1,0:T(8,128)S(1)} fusion(f32[64,1024]{1,0:T(8,128)} %param.7, s32[1024]{0:T(1024)S(1)} %broadcast_subtract_fusion), kind=kOutput, calls=%fused_computation.22 | convolution fusion | flops 3153920 | bytes 268288 | tf_op jit(solution)/shard_map/dot_general | solution.py:58
  2.0 0.0 copy-done.1
  2.0 0.0 copy-done.3
  2.0 0.0 copy-start.4
  2.0 0.0 copy-start.5
  2.0 0.0 copy-start.2
  2.1 0.2 fusion.3
  2.2 0.5 copy-done.4
  2.7 0.0 copy-done.5
  2.7 0.1 select_reduce_fusion
  2.9 0.1 copy.16
  2.9 0.0 copy-done.2
  2.9 0.1 convolution_bitcast_fusion.2
  3.1 0.0 copy-done
  3.1 0.2 fusion.2
  3.2 0.1 select_maximum_fusion.4
  3.4 5.7 %collective-permute-start = (f32[64,8]{0,1:T(8,128)S(1)}, f32[64,8]{0,1:T(8,128)S(1)}, u32[]{:S(2)}, u32[]{:S(2)}) collective-permute-start(f32[64,8]{0,1:T(8,128)S(1)} %convolution_bitcast_fusion.2), channel_id=1, source_target_pairs={{0,2},{1,3},{2,4},{3,5},{4,6},{5,7},{6,8},{7,9},{8,10},{9,11},{10,... | collective-permute-start | bytes 6152 | tf_op jit(solution)/shard_map/ppermute | solution.py:14
  9.1 1.3 %collective-permute-start.3 = (f32[64,8]{0,1:T(8,128)S(1)}, f32[64,8]{0,1:T(8,128)S(1)}, u32[]{:S(2)}, u32[]{:S(2)}) collective-permute-start(f32[64,8]{0,1:T(8,128)S(1)} %convolution_bitcast_fusion.2), channel_id=1, source_target_pairs={{2,0},{3,1},{4,2},{5,3},{6,4},{7,5},{8,6},{9,7},{10,8},{11,9},{12,... | collective-permute-start | bytes 6152 | tf_op jit(solution)/shard_map/ppermute | solution.py:14
  10.4 11.6 %collective-permute-start.2 = (f32[80,24]{0,1:T(8,128)S(1)}, f32[80,24]{0,1:T(8,128)S(1)}, u32[]{:S(2)}, u32[]{:S(2)}) collective-permute-start(f32[80,24]{0,1:T(8,128)S(1)} %select_maximum_fusion.4), channel_id=1, source_target_pairs={{1,0},{2,1},{3,2},{4,3},{5,4},{6,5},{7,6},{8,7},{9,8},{10,9},{11,1... | collective-permute-start | bytes 23048 | tf_op jit(solution)/shard_map/ppermute | solution.py:14
  22.0 4.2 %collective-permute-start.1 = (f32[80,24]{0,1:T(8,128)S(1)}, f32[80,24]{0,1:T(8,128)S(1)}, u32[]{:S(2)}, u32[]{:S(2)}) collective-permute-start(f32[80,24]{0,1:T(8,128)S(1)} %select_maximum_fusion.4), channel_id=1, source_target_pairs={{0,1},{1,2},{2,3},{3,4},{4,5},{5,6},{6,7},{7,8},{8,9},{9,10},{10,1... | collective-permute-start | bytes 23048 | tf_op jit(solution)/shard_map/ppermute | solution.py:14
  26.2 0.0 collective-permute-done
  26.2 0.8 %collective-permute-done.1 = f32[80,24]{0,1:T(8,128)S(1)} collective-permute-done((f32[80,24]{0,1:T(8,128)S(1)}, f32[80,24]{0,1:T(8,128)S(1)}, u32[]{:S(2)}, u32[]{:S(2)}) %collective-permute-start.1) | collective-permute-done | bytes 7712 | tf_op jit(solution)/shard_map/ppermute | solution.py:14
  27.0 0.0 collective-permute-done.2
  27.0 0.1 slice.71
  27.1 0.1 slice.70
  27.2 0.0 collective-permute-done.3
  27.2 0.3 fusion.8
  27.5 0.3 fusion.6
  27.7 0.1 slice_bitcast_fusion
  27.8 0.1 slice_bitcast_fusion.1
  27.9 0.1 pad_maximum_fusion
  28.0 0.2 fusion.20
  28.2 0.1 fusion.49
  28.3 0.4 fusion
  28.7 0.4 fusion.1
  29.1 0.4 multiply_reduce_fusion
  29.5 0.1 stack.27
  29.6 0.1 reduce_sum.107
  29.7 14.6 %all_to_all.12 = f32[16,1,6]{2,1,0:T(1,128)S(1)} all-to-all(f32[16,1,6]{2,1,0:T(1,128)S(1)} %broadcast_in_dim.17), channel_id=1, replica_groups=mesh['curve'=64,'coef'=16] {'coef'}, dimensions={0} | all-to-all | bytes 768 | tf_op jit(solution)/shard_map/all_to_all | solution.py:21
  44.3 26.9 %all_to_all.13 = f32[64,1,6]{2,1,0:T(1,128)S(1)} all-to-all(f32[64,1,6]{2,1,0:T(1,128)S(1)} %broadcast_in_dim.18), channel_id=1, replica_groups=mesh['curve'=64,'coef'=16] {'curve'}, dimensions={0} | all-to-all | bytes 3072 | tf_op jit(solution)/shard_map/all_to_all | solution.py:21
  71.3 0.1 reduce_sum.109
  71.3 0.1 broadcast_in_dim.19
  71.5 0.8 %multiply_add_fusion = f32[64,1024]{1,0:T(8,128)} fusion(f32[64,1024]{1,0:T(8,128)S(1)} %fusion, f32[64,1024]{1,0:T(8,128)S(1)} %copy-done.1, f32[]{:T(128)S(1)} %bitcast.128, f32[]{:T(128)S(1)} %bitcast.127), kind=kLoop, calls=%fused_computation.8 | loop fusion | flops 196608 | bytes 786440 | tf_op jit(solution)/shard_map/add | solution.py:121
  (15 shorter events, 0.2 us)
Async XLA Ops:
  0.0 3.1 %copy-start = (f32[64,64]{1,0:T(8,128)S(1)}, f32[64,64]{1,0:T(8,128)}, u32[]{:S(2)}) copy-start(f32[64,64]{1,0:T(8,128)} %param.12) | copy-start | bytes 49156
  0.0 2.0 %copy-start.1 = (f32[64,1024]{1,0:T(8,128)S(1)}, f32[64,1024]{1,0:T(8,128)}, u32[]{:S(2)}) copy-start(f32[64,1024]{1,0:T(8,128)} %param.7) | copy-start | bytes 786436
  0.9 1.1 %copy-start.3 = (f32[1024]{0:T(1024)S(1)}, f32[1024]{0:T(1024)}, u32[]{:S(2)}) copy-start(f32[1024]{0:T(1024)} %param.11) | copy-start | bytes 12292
  2.0 0.7 copy-start.4
  2.0 0.7 copy-start.5
  2.0 0.9 %copy-start.2 = (f32[64,64]{1,0:T(8,128)S(1)}, f32[64,64]{1,0:T(8,128)}, u32[]{:S(2)}) copy-start(f32[64,64]{1,0:T(8,128)} %param.13) | copy-start | bytes 49156
  3.4 22.8 %collective-permute-start = (f32[64,8]{0,1:T(8,128)S(1)}, f32[64,8]{0,1:T(8,128)S(1)}, u32[]{:S(2)}, u32[]{:S(2)}) collective-permute-start(f32[64,8]{0,1:T(8,128)S(1)} %convolution_bitcast_fusion.2), channel_id=1, source_target_pairs={{0,2},{1,3},{2,4},{3,5},{4,6},{5,7},{6,8},{7,9},{8,10},{9,11},{10,... | collective-permute-start | bytes 6152 | tf_op jit(solution)/shard_map/ppermute | solution.py:14
  9.1 18.1 %collective-permute-start.3 = (f32[64,8]{0,1:T(8,128)S(1)}, f32[64,8]{0,1:T(8,128)S(1)}, u32[]{:S(2)}, u32[]{:S(2)}) collective-permute-start(f32[64,8]{0,1:T(8,128)S(1)} %convolution_bitcast_fusion.2), channel_id=1, source_target_pairs={{2,0},{3,1},{4,2},{5,3},{6,4},{7,5},{8,6},{9,7},{10,8},{11,9},{12,... | collective-permute-start | bytes 6152 | tf_op jit(solution)/shard_map/ppermute | solution.py:14
  10.4 16.6 %collective-permute-start.2 = (f32[80,24]{0,1:T(8,128)S(1)}, f32[80,24]{0,1:T(8,128)S(1)}, u32[]{:S(2)}, u32[]{:S(2)}) collective-permute-start(f32[80,24]{0,1:T(8,128)S(1)} %select_maximum_fusion.4), channel_id=1, source_target_pairs={{1,0},{2,1},{3,2},{4,3},{5,4},{6,5},{7,6},{8,7},{9,8},{10,9},{11,1... | collective-permute-start | bytes 23048 | tf_op jit(solution)/shard_map/ppermute | solution.py:14
  22.0 5.0 %collective-permute-start.1 = (f32[80,24]{0,1:T(8,128)S(1)}, f32[80,24]{0,1:T(8,128)S(1)}, u32[]{:S(2)}, u32[]{:S(2)}) collective-permute-start(f32[80,24]{0,1:T(8,128)S(1)} %select_maximum_fusion.4), channel_id=1, source_target_pairs={{0,1},{1,2},{2,3},{3,4},{4,5},{5,6},{6,7},{7,8},{8,9},{9,10},{10,1... | collective-permute-start | bytes 23048 | tf_op jit(solution)/shard_map/ppermute | solution.py:14

commit v14 on v6

--- a/solution.py
+++ b/solution.py
@@ -45,10 +45,8 @@
 def on_device(right_side, group_ids, pair_sources, pair_weights, self_diag, self_trans, far_trans):
     group_count = pair_sources.shape[0]
     base_group = lax.axis_index(DEVICES) * group_count
-    slots = group_ids - base_group
-    slot_table = (slots[None, :] == jnp.arange(group_count, dtype=jnp.int32)[:, None]).astype(
-        jnp.float32
-    )
+    own_groups = base_group + jnp.arange(group_count, dtype=jnp.int32)
+    slot_table = (group_ids[None, :] == own_groups[:, None]).astype(jnp.float32)
     columns = base_group - group_count + jnp.arange(3 * group_count, dtype=jnp.int32)
     matches = (pair_sources[:, :, None] == columns[None, None, :]).astype(jnp.float32)
     select_mat = jnp.sum(pair_weights[:, :, None] * matches, axis=1)

time: 72.8 us -> 73 us (level)
    reduce_sum x1, other arithmetic: 0.12 us -> 0.92 us  [on_device(): counts = jnp.sum(slot_table, axis=1)]
    sub x1 -> x0, other arithmetic: 0.74 us -> none  [on_device(): slots = group_ids - base_group]
where the time goes in v14:
time: 73 us; the launch traced here: 72.7 us
  blocking collectives  41.5 us (57%)
  starting transfers between devices  22.8 us (31%)
  matrix products  3.93 us (5%)
  other arithmetic  2.34 us (3%)
  local copies, waits for them, and re-layouts  1.07 us (1%)
  waiting for transfers between devices  0.8 us (1%)
    all_to_all x2, blocking collectives, all_sum(): value = jnp.sum(lax.all_to_all(spread, axis, 0, 0, tiled=True), axis=0)  41.5 us
    ppermute x4, starting transfers between devices, shifted(): return lax.ppermute(array, axis, pairs)  22.8 us
    dot_general x9, matrix products, on_device(): dot = lambda a, b: jnp.dot(a, b, precision=highest)  3.16 us
  transfers between devices with their start and end apart: 4, of which 1 were waited for; matrix products, arithmetic and copies ran while one was open for 0% of the time, Pallas kernels for 0%

profile of v14, /device:TPU:1, one launch (start us, length us, event | category | flops | bytes accessed | tf_op | source)
XLA Modules:
  0.0 72.7 jit_solution(3340222826463801301)
XLA Ops:
  0.0 0.0 copy-start
  0.0 0.0 copy-start.1
  0.0 0.9 %fusion.12 = f32[8]{0:T(128)S(1)} fusion(s32[1024]{0:T(1024)} %param.8, s32[8]{0:T(128)S(1)} %iota_add_fusion.1), kind=kLoop, calls=%fused_computation.26 | loop fusion | flops 24568 | bytes 4160 | tf_op jit(solution)/shard_map/reduce_sum | solution.py:53
  0.9 0.0 copy-start.3
  0.9 0.0 copy-start.4
  1.0 1.2 %fusion.10 = f32[8,64]{1,0:T(8,128)S(1)} fusion(f32[64,1024]{1,0:T(8,128)} %param.7, s32[1024]{0:T(1024)} %param.8, s32[8]{0:T(128)S(1)} %iota_add_fusion.1), kind=kOutput, calls=%fused_computation.23 | convolution fusion | flops 6299648 | bytes 268320 | tf_op jit(solution)/shard_map/dot_general | solution.py:55
  2.2 0.0 copy-done.1
  2.2 0.1 copy-done.3
  2.2 0.0 copy-done.4
  2.2 0.0 copy-start.5
  2.2 0.0 copy-start.6
  2.3 0.0 copy-start.2
  2.3 0.2 fusion.3
  2.5 0.4 copy-done.5
  2.9 0.0 copy-done.6
  2.9 0.1 select_reduce_fusion
  3.1 0.1 copy.16
  3.1 0.0 copy-done.2
  3.1 0.1 convolution_bitcast_fusion.2
  3.3 0.0 copy-done
  3.3 0.2 fusion.2
  3.5 0.1 select_maximum_fusion.4
  3.6 5.7 %collective-permute-start = (f32[64,8]{0,1:T(8,128)S(1)}, f32[64,8]{0,1:T(8,128)S(1)}, u32[]{:S(2)}, u32[]{:S(2)}) collective-permute-start(f32[64,8]{0,1:T(8,128)S(1)} %convolution_bitcast_fusion.2), channel_id=1, source_target_pairs={{0,2},{1,3},{2,4},{3,5},{4,6},{5,7},{6,8},{7,9},{8,10},{9,11},{10,... | collective-permute-start | bytes 6152 | tf_op jit(solution)/shard_map/ppermute | solution.py:14
  9.3 1.3 %collective-permute-start.3 = (f32[64,8]{0,1:T(8,128)S(1)}, f32[64,8]{0,1:T(8,128)S(1)}, u32[]{:S(2)}, u32[]{:S(2)}) collective-permute-start(f32[64,8]{0,1:T(8,128)S(1)} %convolution_bitcast_fusion.2), channel_id=1, source_target_pairs={{2,0},{3,1},{4,2},{5,3},{6,4},{7,5},{8,6},{9,7},{10,8},{11,9},{12,... | collective-permute-start | bytes 6152 | tf_op jit(solution)/shard_map/ppermute | solution.py:14
  10.6 11.6 %collective-permute-start.2 = (f32[80,24]{0,1:T(8,128)S(1)}, f32[80,24]{0,1:T(8,128)S(1)}, u32[]{:S(2)}, u32[]{:S(2)}) collective-permute-start(f32[80,24]{0,1:T(8,128)S(1)} %select_maximum_fusion.4), channel_id=1, source_target_pairs={{1,0},{2,1},{3,2},{4,3},{5,4},{6,5},{7,6},{8,7},{9,8},{10,9},{11,1... | collective-permute-start | bytes 23048 | tf_op jit(solution)/shard_map/ppermute | solution.py:14
  22.2 4.2 %collective-permute-start.1 = (f32[80,24]{0,1:T(8,128)S(1)}, f32[80,24]{0,1:T(8,128)S(1)}, u32[]{:S(2)}, u32[]{:S(2)}) collective-permute-start(f32[80,24]{0,1:T(8,128)S(1)} %select_maximum_fusion.4), channel_id=1, source_target_pairs={{0,1},{1,2},{2,3},{3,4},{4,5},{5,6},{6,7},{7,8},{8,9},{9,10},{10,1... | collective-permute-start | bytes 23048 | tf_op jit(solution)/shard_map/ppermute | solution.py:14
  26.4 0.0 collective-permute-done
  26.4 0.8 %collective-permute-done.1 = f32[80,24]{0,1:T(8,128)S(1)} collective-permute-done((f32[80,24]{0,1:T(8,128)S(1)}, f32[80,24]{0,1:T(8,128)S(1)}, u32[]{:S(2)}, u32[]{:S(2)}) %collective-permute-start.1) | collective-permute-done | bytes 7712 | tf_op jit(solution)/shard_map/ppermute | solution.py:14
  27.2 0.0 collective-permute-done.2
  27.2 0.1 slice.71
  27.3 0.1 slice.70
  27.4 0.0 collective-permute-done.3
  27.4 0.3 fusion.13
  27.7 0.3 fusion.7
  28.0 0.1 slice_bitcast_fusion
  28.1 0.1 slice_bitcast_fusion.1
  28.2 0.1 pad_maximum_fusion
  28.2 0.2 fusion.29
  28.4 0.1 fusion.58
  28.6 0.4 fusion
  29.0 0.4 fusion.1
  29.4 0.5 multiply_reduce_fusion
  29.8 0.1 stack.27
  29.9 0.1 reduce_sum.107
  30.0 14.6 %all_to_all.12 = f32[16,1,6]{2,1,0:T(1,128)S(1)} all-to-all(f32[16,1,6]{2,1,0:T(1,128)S(1)} %broadcast_in_dim.17), channel_id=1, replica_groups=mesh['curve'=64,'coef'=16] {'coef'}, dimensions={0} | all-to-all | bytes 768 | tf_op jit(solution)/shard_map/all_to_all | solution.py:21
  44.7 26.9 %all_to_all.13 = f32[64,1,6]{2,1,0:T(1,128)S(1)} all-to-all(f32[64,1,6]{2,1,0:T(1,128)S(1)} %broadcast_in_dim.18), channel_id=1, replica_groups=mesh['curve'=64,'coef'=16] {'curve'}, dimensions={0} | all-to-all | bytes 3072 | tf_op jit(solution)/shard_map/all_to_all | solution.py:21
  71.6 0.1 reduce_sum.109
  71.7 0.1 broadcast_in_dim.19
  71.9 0.8 %multiply_add_fusion = f32[64,1024]{1,0:T(8,128)} fusion(f32[64,1024]{1,0:T(8,128)S(1)} %fusion, f32[64,1024]{1,0:T(8,128)S(1)} %copy-done.1, f32[]{:T(128)S(1)} %bitcast.128, f32[]{:T(128)S(1)} %bitcast.127), kind=kLoop, calls=%fused_computation.8 | loop fusion | flops 196608 | bytes 786440 | tf_op jit(solution)/shard_map/add | solution.py:118
  (16 shorter events, 0.2 us)
Async XLA Ops:
  0.0 3.3 %copy-start = (f32[64,64]{1,0:T(8,128)S(1)}, f32[64,64]{1,0:T(8,128)}, u32[]{:S(2)}) copy-start(f32[64,64]{1,0:T(8,128)} %param.12) | copy-start | bytes 49156
  0.0 2.2 %copy-start.1 = (f32[64,1024]{1,0:T(8,128)S(1)}, f32[64,1024]{1,0:T(8,128)}, u32[]{:S(2)}) copy-start(f32[64,1024]{1,0:T(8,128)} %param.7) | copy-start | bytes 786436
  0.9 1.3 %copy-start.3 = (s32[1024]{0:T(1024)S(1)}, s32[1024]{0:T(1024)}, u32[]{:S(2)}) copy-start(s32[1024]{0:T(1024)} %param.8) | copy-start | bytes 12292
  0.9 1.3 %copy-start.4 = (f32[1024]{0:T(1024)S(1)}, f32[1024]{0:T(1024)}, u32[]{:S(2)}) copy-start(f32[1024]{0:T(1024)} %param.11) | copy-start | bytes 12292
  2.2 0.7 copy-start.5
  2.2 0.7 copy-start.6
  2.3 0.9 %copy-start.2 = (f32[64,64]{1,0:T(8,128)S(1)}, f32[64,64]{1,0:T(8,128)}, u32[]{:S(2)}) copy-start(f32[64,64]{1,0:T(8,128)} %param.13) | copy-start | bytes 49156
  3.6 22.8 %collective-permute-start = (f32[64,8]{0,1:T(8,128)S(1)}, f32[64,8]{0,1:T(8,128)S(1)}, u32[]{:S(2)}, u32[]{:S(2)}) collective-permute-start(f32[64,8]{0,1:T(8,128)S(1)} %convolution_bitcast_fusion.2), channel_id=1, source_target_pairs={{0,2},{1,3},{2,4},{3,5},{4,6},{5,7},{6,8},{7,9},{8,10},{9,11},{10,... | collective-permute-start | bytes 6152 | tf_op jit(solution)/shard_map/ppermute | solution.py:14
  9.3 18.1 %collective-permute-start.3 = (f32[64,8]{0,1:T(8,128)S(1)}, f32[64,8]{0,1:T(8,128)S(1)}, u32[]{:S(2)}, u32[]{:S(2)}) collective-permute-start(f32[64,8]{0,1:T(8,128)S(1)} %convolution_bitcast_fusion.2), channel_id=1, source_target_pairs={{2,0},{3,1},{4,2},{5,3},{6,4},{7,5},{8,6},{9,7},{10,8},{11,9},{12,... | collective-permute-start | bytes 6152 | tf_op jit(solution)/shard_map/ppermute | solution.py:14
  10.6 16.6 %collective-permute-start.2 = (f32[80,24]{0,1:T(8,128)S(1)}, f32[80,24]{0,1:T(8,128)S(1)}, u32[]{:S(2)}, u32[]{:S(2)}) collective-permute-start(f32[80,24]{0,1:T(8,128)S(1)} %select_maximum_fusion.4), channel_id=1, source_target_pairs={{1,0},{2,1},{3,2},{4,3},{5,4},{6,5},{7,6},{8,7},{9,8},{10,9},{11,1... | collective-permute-start | bytes 23048 | tf_op jit(solution)/shard_map/ppermute | solution.py:14
  22.2 5.0 %collective-permute-start.1 = (f32[80,24]{0,1:T(8,128)S(1)}, f32[80,24]{0,1:T(8,128)S(1)}, u32[]{:S(2)}, u32[]{:S(2)}) collective-permute-start(f32[80,24]{0,1:T(8,128)S(1)} %select_maximum_fusion.4), channel_id=1, source_target_pairs={{0,1},{1,2},{2,3},{3,4},{4,5},{5,6},{6,7},{7,8},{8,9},{9,10},{10,1... | collective-permute-start | bytes 23048 | tf_op jit(solution)/shard_map/ppermute | solution.py:14

commit v15 on v6

--- a/solution.py
+++ b/solution.py
@@ -95,7 +95,8 @@
     near_counts = jnp.concatenate([counts_below, counts, counts_above])
     near_part = jnp.concatenate([part_below, own_part, part_above], axis=1)
     near_moments = near_part + near_counts[None, :] * local_near
-    first = local_part(right_side, self_diag, self_trans) + dot(local_near[:, g : 2 * g], slot_table)
+    own_local = lax.optimization_barrier(local_part(right_side, self_diag, self_trans))
+    first = own_local + dot(local_near[:, g : 2 * g], slot_table)
     local_next = dot(far_trans, dot(near_moments, select_mat.T))
     second = local_part(first, self_diag, self_trans) + dot(local_next, slot_table)
     krylov = (right_side, first, second)

time: 72.8 us -> 77.2 us (1.060)
  blocking collectives: 41.5 us -> 44.9 us
  starting transfers between devices: 22.8 us -> 23.8 us
    all_to_all x2, blocking collectives: 41.5 us -> 44.9 us  [all_sum(): value = jnp.sum(lax.all_to_all(spread, axis, 0, 0, tiled=True), axis=0)]
    ppermute x4, starting transfers between devices: 22.8 us -> 23.8 us  [shifted(): return lax.ppermute(array, axis, pairs)]
  transfers between devices with their start and end apart: 4 -> 4, of which waited for: 1 -> 1; matrix products, arithmetic and copies ran while one was open for 0% -> 1% of each run, Pallas kernels for 0% -> 0%
where the time goes in v15:
time: 77.2 us; the launch traced here: 76.8 us
  blocking collectives  44.9 us (58%)
  starting transfers between devices  23.8 us (31%)
  matrix products  3.81 us (5%)
  other arithmetic  2.27 us (3%)
  local copies, waits for them, and re-layouts  1.07 us (1%)
    all_to_all x2, blocking collectives, all_sum(): value = jnp.sum(lax.all_to_all(spread, axis, 0, 0, tiled=True), axis=0)  44.9 us
    ppermute x4, starting transfers between devices, shifted(): return lax.ppermute(array, axis, pairs)  23.8 us
    dot_general x9, matrix products, on_device(): dot = lambda a, b: jnp.dot(a, b, precision=highest)  3.08 us
  transfers between devices with their start and end apart: 4, of which 1 were waited for; matrix products, arithmetic and copies ran while one was open for 1% of the time, Pallas kernels for 0%

profile of v15, /device:TPU:1, one launch (start us, length us, event | category | flops | bytes accessed | tf_op | source)
XLA Modules:
  0.0 76.8 jit_solution(9859765722313841826)
XLA Ops:
  0.0 0.0 copy-start
  0.0 0.0 copy-start.1
  0.0 0.7 broadcast_subtract_fusion
  0.7 0.1 convert_reduce_fusion
  0.9 0.0 copy-start.3
  0.9 1.2 %fusion.5 = f32[8,64]{1,0:T(8,128)S(1)} fusion(f32[64,1024]{1,0:T(8,128)} %param.7, s32[1024]{0:T(1024)S(1)} %broadcast_subtract_fusion), kind=kOutput, calls=%fused_computation.21 | convolution fusion | flops 6299648 | bytes 268288 | tf_op jit(solution)/shard_map/dot_general | solution.py:57
  2.0 0.0 copy-done.1
  2.0 0.1 copy-done.3
  2.1 0.0 copy-start.4
  2.1 0.0 copy-start.5
  2.1 0.0 copy-start.2
  2.1 0.2 fusion.2
  2.3 0.5 copy-done.4
  2.8 0.0 copy-done.5
  2.8 0.1 select_reduce_fusion
  2.9 0.1 copy.16
  3.0 0.0 copy-done.2
  3.0 0.1 convolution_bitcast_fusion.2
  3.1 0.0 copy-done
  3.1 0.2 fusion.1
  3.3 0.1 select_maximum_fusion.4
  3.4 1.3 %collective-permute-start.3 = (f32[64,8]{0,1:T(8,128)S(1)}, f32[64,8]{0,1:T(8,128)S(1)}, u32[]{:S(2)}, u32[]{:S(2)}) collective-permute-start(f32[64,8]{0,1:T(8,128)S(1)} %convolution_bitcast_fusion.2), channel_id=1, source_target_pairs={{2,0},{3,1},{4,2},{5,3},{6,4},{7,5},{8,6},{9,7},{10,8},{11,9},{12,... | collective-permute-start | bytes 6152 | tf_op jit(solution)/shard_map/ppermute | solution.py:14
  4.7 6.4 %collective-permute-start = (f32[64,8]{0,1:T(8,128)S(1)}, f32[64,8]{0,1:T(8,128)S(1)}, u32[]{:S(2)}, u32[]{:S(2)}) collective-permute-start(f32[64,8]{0,1:T(8,128)S(1)} %convolution_bitcast_fusion.2), channel_id=1, source_target_pairs={{0,2},{1,3},{2,4},{3,5},{4,6},{5,7},{6,8},{7,9},{8,10},{9,11},{10,... | collective-permute-start | bytes 6152 | tf_op jit(solution)/shard_map/ppermute | solution.py:14
  11.1 14.2 %collective-permute-start.2 = (f32[80,24]{0,1:T(8,128)S(1)}, f32[80,24]{0,1:T(8,128)S(1)}, u32[]{:S(2)}, u32[]{:S(2)}) collective-permute-start(f32[80,24]{0,1:T(8,128)S(1)} %select_maximum_fusion.4), channel_id=1, source_target_pairs={{1,0},{2,1},{3,2},{4,3},{5,4},{6,5},{7,6},{8,7},{9,8},{10,9},{11,1... | collective-permute-start | bytes 23048 | tf_op jit(solution)/shard_map/ppermute | solution.py:14
  25.3 1.9 %collective-permute-start.1 = (f32[80,24]{0,1:T(8,128)S(1)}, f32[80,24]{0,1:T(8,128)S(1)}, u32[]{:S(2)}, u32[]{:S(2)}) collective-permute-start(f32[80,24]{0,1:T(8,128)S(1)} %select_maximum_fusion.4), channel_id=1, source_target_pairs={{0,1},{1,2},{2,3},{3,4},{4,5},{5,6},{6,7},{7,8},{8,9},{9,10},{10,1... | collective-permute-start | bytes 23048 | tf_op jit(solution)/shard_map/ppermute | solution.py:14
  27.3 0.4 convolution_add_fusion
  27.6 0.0 collective-permute-done
  27.7 0.8 collective-permute-done.1
  28.4 0.1 slice_bitcast_fusion.1
  28.5 0.0 collective-permute-done.2
  28.5 0.1 slice_bitcast_fusion
  28.6 0.1 pad_maximum_fusion
  28.6 0.1 slice.71
  28.7 0.1 slice.70
  28.8 0.0 collective-permute-done.3
  28.8 0.3 fusion.6
  29.1 0.2 fusion.18
  29.3 0.2 fusion.47
  29.4 0.3 convolution_add_fusion.2
  29.8 0.4 fusion
  30.2 0.4 multiply_reduce_fusion
  30.6 0.1 stack.27
  30.7 0.1 reduce_sum.107
  30.8 15.4 %all_to_all.12 = f32[16,1,6]{2,1,0:T(1,128)S(1)} all-to-all(f32[16,1,6]{2,1,0:T(1,128)S(1)} %broadcast_in_dim.17), channel_id=1, replica_groups=mesh['curve'=64,'coef'=16] {'coef'}, dimensions={0} | all-to-all | bytes 768 | tf_op jit(solution)/shard_map/all_to_all | solution.py:21
  46.2 29.5 %all_to_all.13 = f32[64,1,6]{2,1,0:T(1,128)S(1)} all-to-all(f32[64,1,6]{2,1,0:T(1,128)S(1)} %broadcast_in_dim.18), channel_id=1, replica_groups=mesh['curve'=64,'coef'=16] {'curve'}, dimensions={0} | all-to-all | bytes 3072 | tf_op jit(solution)/shard_map/all_to_all | solution.py:21
  75.8 0.1 reduce_sum.109
  75.8 0.1 broadcast_in_dim.19
  76.0 0.8 %multiply_add_fusion = f32[64,1024]{1,0:T(8,128)} fusion(f32[64,1024]{1,0:T(8,128)S(1)} %convolution_add_fusion.2, f32[64,1024]{1,0:T(8,128)S(1)} %copy-done.1, f32[]{:T(128)S(1)} %bitcast.128, f32[]{:T(128)S(1)} %bitcast.127), kind=kLoop, calls=%fused_computation.8 | loop fusion | flops 196608 | bytes 786440 | tf_op jit(solution)/shard_map/add | solution.py:121
  (15 shorter events, 0.2 us)
Async XLA Ops:
  0.0 3.1 %copy-start = (f32[64,64]{1,0:T(8,128)S(1)}, f32[64,64]{1,0:T(8,128)}, u32[]{:S(2)}) copy-start(f32[64,64]{1,0:T(8,128)} %param.12) | copy-start | bytes 49156
  0.0 2.0 %copy-start.1 = (f32[64,1024]{1,0:T(8,128)S(1)}, f32[64,1024]{1,0:T(8,128)}, u32[]{:S(2)}) copy-start(f32[64,1024]{1,0:T(8,128)} %param.7) | copy-start | bytes 786436
  0.9 1.2 %copy-start.3 = (f32[1024]{0:T(1024)S(1)}, f32[1024]{0:T(1024)}, u32[]{:S(2)}) copy-start(f32[1024]{0:T(1024)} %param.11) | copy-start | bytes 12292
  2.1 0.7 copy-start.4
  2.1 0.7 copy-start.5
  2.1 0.9 %copy-start.2 = (f32[64,64]{1,0:T(8,128)S(1)}, f32[64,64]{1,0:T(8,128)}, u32[]{:S(2)}) copy-start(f32[64,64]{1,0:T(8,128)} %param.13) | copy-start | bytes 49156
  3.4 25.4 %collective-permute-start.3 = (f32[64,8]{0,1:T(8,128)S(1)}, f32[64,8]{0,1:T(8,128)S(1)}, u32[]{:S(2)}, u32[]{:S(2)}) collective-permute-start(f32[64,8]{0,1:T(8,128)S(1)} %convolution_bitcast_fusion.2), channel_id=1, source_target_pairs={{2,0},{3,1},{4,2},{5,3},{6,4},{7,5},{8,6},{9,7},{10,8},{11,9},{12,... | collective-permute-start | bytes 6152 | tf_op jit(solution)/shard_map/ppermute | solution.py:14
  4.7 22.9 %collective-permute-start = (f32[64,8]{0,1:T(8,128)S(1)}, f32[64,8]{0,1:T(8,128)S(1)}, u32[]{:S(2)}, u32[]{:S(2)}) collective-permute-start(f32[64,8]{0,1:T(8,128)S(1)} %convolution_bitcast_fusion.2), channel_id=1, source_target_pairs={{0,2},{1,3},{2,4},{3,5},{4,6},{5,7},{6,8},{7,9},{8,10},{9,11},{10,... | collective-permute-start | bytes 6152 | tf_op jit(solution)/shard_map/ppermute | solution.py:14
  11.1 17.4 %collective-permute-start.2 = (f32[80,24]{0,1:T(8,128)S(1)}, f32[80,24]{0,1:T(8,128)S(1)}, u32[]{:S(2)}, u32[]{:S(2)}) collective-permute-start(f32[80,24]{0,1:T(8,128)S(1)} %select_maximum_fusion.4), channel_id=1, source_target_pairs={{1,0},{2,1},{3,2},{4,3},{5,4},{6,5},{7,6},{8,7},{9,8},{10,9},{11,1... | collective-permute-start | bytes 23048 | tf_op jit(solution)/shard_map/ppermute | solution.py:14
  25.3 3.1 %collective-permute-start.1 = (f32[80,24]{0,1:T(8,128)S(1)}, f32[80,24]{0,1:T(8,128)S(1)}, u32[]{:S(2)}, u32[]{:S(2)}) collective-permute-start(f32[80,24]{0,1:T(8,128)S(1)} %select_maximum_fusion.4), channel_id=1, source_target_pairs={{0,1},{1,2},{2,3},{3,4},{4,5},{5,6},{6,7},{7,8},{8,9},{9,10},{10,1... | collective-permute-start | bytes 23048 | tf_op jit(solution)/shard_map/ppermute | solution.py:14
